TPU v7x, 512 devices: a whole 4x8x8 slice. The times are simulated.
512 devices in a mesh: net: 64 (over z, y), tm: 8 (over x, core).
Axes of the slice: x: 4, y: 8, z: 8, core: 2. Of those that a mesh axis runs over, the one named last changes fastest.
Arguments:
- warm_mag: float32 [24, 16, 16384], P('tm', None, 'net'), may hold values from 0.94 to 1.06
- warm_angle: float32 [24, 16, 16384], P('tm', None, 'net'), may hold values from -0.6 to 0.6
- load_real: float32 [24, 16, 16384], P('tm', None, 'net'), may hold values from 0 to 1.2
- load_react: float32 [24, 16, 16384], P('tm', None, 'net'), may hold values from -0.3 to 0.5
- start_real: float32 [24, 16, 2048], P('tm', None, 'net'), may hold values from 0 to 2
- start_react: float32 [24, 16, 2048], P('tm', None, 'net'), may hold values from -3 to 3
- gen_bus: int32 [2048], P('net'), may hold values from 0 to 255
- gen_linear: float32 [2048], P('net'), may hold values from 0.2 to 2
- gen_quad: float32 [2048], P('net'), may hold values from 0.05 to 1
- gen_ramp: float32 [2048], P('net'), may hold values from 0.2 to 5
- gen_cap_real: float32 [2048], P('net'), may hold values from 0.5 to 3
- gen_cap_react: float32 [2048], P('net'), may hold values from 0.1 to 1
- branch_from: int32 [16384], P('net'), may hold values from 0 to 255
- branch_to: int32 [16384], P('net'), may hold values from 0 to 255
- branch_cond: float32 [16384], P('net'), may hold values from 0.2 to 2
- branch_susc: float32 [16384], P('net'), may hold values from -6 to -1.5
- branch_limit: float32 [16384], P('net'), may hold values from 0.5 to 4
- branch_steps: int32 [16384], P('net'), may hold values from 1 to 4
- cut_near: int32 [4096], P('net'), may hold values from 0 to 255
- cut_peer: int32 [4096, 1], P('net'), may hold values from 0 to 63; in each aligned block of 64 rows (0 to 63, 64 to 127, ...) at most 2 rows name the same one
- cut_bus: int32 [4096], P('net'), may hold values from 0 to 255
- cut_cond: float32 [4096], P('net'), may hold values from 0.2 to 2
- cut_susc: float32 [4096], P('net'), may hold values from -6 to -1.5
- cut_limit: float32 [4096], P('net'), may hold values from 0.5 to 4
- cut_steps: int32 [4096], P('net'), may hold values from 1 to 4
Outputs:
- bus_mag: float32 [24, 16, 16384], P('tm', None, 'net')
- bus_angle: float32 [24, 16, 16384], P('tm', None, 'net')
- bus_price: float32 [24, 16, 16384], P('tm', None, 'net')
- gen_real: float32 [24, 16, 2048], P('tm', None, 'net')
- gen_react: float32 [24, 16, 2048], P('tm', None, 'net')
Inputs may be any that keep to these rules, and one draw needn't show every extreme that they name: `cut_peer`: among the 64 cut branches of one partition no partition is named more than 2 times, a bound that some block reaches.
All inputs are finite; a program needn't handle non-finite values.
Results may differ from a plain program's by a relative error of at most 0.0003.
Values sent between devices are 32-bit elements; how exact they have to be, the bound alone decides.
No kernel may reach another device: no remote copies, remote signals or barrier semaphores. Data moves between devices by JAX's collectives and lax.ppermute only.
A program may use at most 64 MiB of HBM per device.

v0:
```python
import jax
import jax.numpy as jnp
from jax import lax
from jax.sharding import PartitionSpec as P

INNER = 4
ITERS = 2


STEP_SIZE = 0.0005
RADIUS = 0.05
BALANCE_WEIGHT = 2.0


def side_by_side(arrays, axis, split_dim, concat_dim, along):
    both = jnp.concatenate(arrays, axis=along)
    whole, at, finished = (
        lax.all_to_all(both, axis, split_axis=split_dim, concat_axis=concat_dim, tiled=True),
        0,
        [],
    )
    for a in arrays:
        finished.append(lax.slice_in_dim(whole, at, at + a.shape[along], axis=along))
        at += a.shape[along]
    return tuple(finished)


def extended(cells, sides, width):
    for axis, dim in sides:
        count = lax.axis_size(axis)
        ends = count - 1
        head = lax.slice_in_dim(cells, 0, width, axis=dim)
        tail = lax.slice_in_dim(cells, cells.shape[dim] - width, cells.shape[dim], axis=dim)
        cells = jnp.concatenate(
            [
                lax.ppermute(tail, axis, [(i, (i + 1) % count) for i in range(ends)]),
                cells,
                lax.ppermute(head, axis, [((i + 1) % count, i) for i in range(ends)]),
            ],
            axis=dim,
        )
    return cells


def branch_flows(copies, conduct, suscept):
    mag_from = copies[0]
    mag_to = copies[2]
    angle_diff = copies[1] - copies[3]
    cosine = jnp.cos(angle_diff)
    sine_part = jnp.sin(angle_diff)
    product = mag_from * mag_to
    real_from = conduct * mag_from * mag_from - product * (conduct * cosine + suscept * sine_part)
    react_from = -suscept * mag_from * mag_from - product * (conduct * sine_part - suscept * cosine)
    real_to = conduct * mag_to * mag_to - product * (conduct * cosine - suscept * sine_part)
    react_to = -suscept * mag_to * mag_to + product * (conduct * sine_part + suscept * cosine)
    return jnp.stack([real_from, react_from, real_to, react_to])


def branch_energy(copies, target, flow_target, conduct, suscept, ceiling):
    flow_all = branch_flows(copies, conduct, suscept)
    excess_from = jnp.maximum(
        flow_all[0] * flow_all[0] + flow_all[1] * flow_all[1] - ceiling * ceiling, 0.0
    )
    excess_to = jnp.maximum(
        flow_all[2] * flow_all[2] + flow_all[3] * flow_all[3] - ceiling * ceiling, 0.0
    )
    return (
        0.5 * jnp.sum((copies - target) * (copies - target))
        + 0.5 * jnp.sum((flow_all - flow_target) * (flow_all - flow_target))
        + 0.5 * jnp.sum(excess_from * excess_from + excess_to * excess_to)
    )


def branch_solve(copies, target, flow_target, conduct, suscept, ceiling, allowed):
    gradient_fn = jax.grad(branch_energy)
    for attempt in range(INNER):
        gradient = gradient_fn(copies, target, flow_target, conduct, suscept, ceiling)
        motion = jnp.clip(STEP_SIZE * gradient, -RADIUS, RADIUS)
        copies = jnp.where(attempt < allowed, copies - motion, copies)
    return copies


def incidence(bus_ids, local):
    return (bus_ids[:, None] == local[None, :]).astype(jnp.float32)


def pick(values, selector):
    return jnp.einsum("...b,bk->...k", values, selector, precision=lax.Precision.HIGHEST)


def place(values, selector):
    return jnp.einsum("...k,bk->...b", values, selector, precision=lax.Precision.HIGHEST)


def advance(carry, near_state, far_state, conduct, suscept, ceiling, allowed):
    bus_ends = jnp.stack([near_state[0], near_state[1], far_state[0], far_state[1]])
    price_ends = jnp.stack([near_state[2], near_state[3], far_state[2], far_state[3]])
    if carry is None:
        copies = bus_ends
        dual_volt = jnp.zeros_like(bus_ends)
        dual_flow = jnp.zeros_like(bus_ends)
        flow_prev = branch_flows(copies, conduct, suscept)
    else:
        copies, dual_volt, dual_flow, flow_prev = carry
    dual_volt = dual_volt + copies - bus_ends
    flow_target = flow_prev + dual_flow + 2.0 * price_ends
    dual_flow = -price_ends
    copies = branch_solve(
        copies, bus_ends - dual_volt, flow_target, conduct, suscept, ceiling, allowed
    )
    flow_prev = branch_flows(copies, conduct, suscept)
    return (copies, dual_volt, dual_flow, flow_prev)


def contributions(carry):
    copies, dual_volt, dual_flow, flow_prev = carry
    volt = copies + dual_volt
    flow = flow_prev + dual_flow
    return (
        jnp.stack([volt[0], volt[1], flow[0], flow[1]]),
        jnp.stack([volt[2], volt[3], flow[2], flow[3]]),
    )


def bus_update(totals, supply, degree, gen_count, warm_mag, warm_angle, load_real, load_react):
    mag = (totals[0] + warm_mag) / (degree + 1.0)
    angle = (totals[1] + warm_angle) / (degree + 1.0)
    weight = 1.0 + BALANCE_WEIGHT * (gen_count + degree)
    price_real = BALANCE_WEIGHT * (supply[0] - totals[2] - load_real) / weight
    price_react = BALANCE_WEIGHT * (supply[1] - totals[3] - load_react) / weight
    return jnp.stack([mag, angle, price_real, price_react])


def on_device(
    warm_mag,
    warm_angle,
    load_real,
    load_react,
    start_real,
    start_react,
    gen_bus,
    gen_linear,
    gen_quad,
    gen_ramp,
    gen_cap_real,
    gen_cap_react,
    branch_from,
    branch_to,
    branch_cond,
    branch_susc,
    branch_limit,
    branch_steps,
    cut_near,
    cut_peer,
    cut_bus,
    cut_cond,
    cut_susc,
    cut_limit,
    cut_steps,
):
    periods, scenarios, buses = warm_mag.shape
    cuts = cut_near.shape[0]
    partitions = lax.axis_size("net")
    capacity = max(2, cuts // partitions * 2)
    width = 4 * periods * scenarios
    bus_ids = jnp.arange(buses, dtype=jnp.int32)
    onehot_from = incidence(bus_ids, branch_from)
    onehot_to = incidence(bus_ids, branch_to)
    onehot_near = incidence(bus_ids, cut_near)
    onehot_gen = incidence(bus_ids, gen_bus)
    partner = cut_peer[:, 0]
    hits = (partner[:, None] == jnp.arange(partitions, dtype=jnp.int32)[None, :]).astype(jnp.int32)
    ranking = jnp.sum(jnp.cumsum(hits, axis=0) * hits, axis=1) - 1
    position = partner * capacity + ranking
    slot_match = jnp.arange(partitions * capacity, dtype=jnp.int32)[:, None] == position[None, :]
    slot_float = slot_match.astype(jnp.float32)
    degree_local = (
        jnp.sum(onehot_from, axis=1) + jnp.sum(onehot_to, axis=1) + jnp.sum(onehot_near, axis=1)
    )
    gen_count = jnp.sum(onehot_gen, axis=1)
    period_ids = lax.axis_index("tm") * periods + jnp.arange(periods, dtype=jnp.int32)
    horizon = periods * lax.axis_size("tm")
    neighbors = (
        (period_ids > 0).astype(jnp.float32) + (period_ids < horizon - 1).astype(jnp.float32)
    )[:, None, None]
    zeros_bus = jnp.zeros_like(warm_mag)
    state = jnp.stack([warm_mag, warm_angle, zeros_bus, zeros_bus])
    gen_real = start_real
    gen_react = start_react
    dual_real = jnp.zeros_like(start_real)
    dual_react = jnp.zeros_like(start_react)
    columns = jnp.stack(
        [
            (cut_bus + 1).astype(jnp.float32),
            cut_cond,
            cut_susc,
            cut_limit,
            cut_steps.astype(jnp.float32),
        ]
    )
    slot_params = jnp.einsum("kc,jc->jk", columns, slot_float, precision=lax.Precision.HIGHEST)
    slot_params = slot_params.at[:, 0].add(-1.0)
    setup_in = lax.all_to_all(
        slot_params.reshape(partitions, capacity, 5), "net", split_axis=0, concat_axis=0, tiled=True
    )
    setup_in = setup_in.reshape(partitions * capacity, 5)
    received = (bus_ids.astype(jnp.float32)[:, None] == setup_in[:, 0][None, :]).astype(jnp.float32)
    mirror_cond = setup_in[:, 1]
    mirror_susc = setup_in[:, 2]
    mirror_limit = setup_in[:, 3]
    mirror_steps = setup_in[:, 4]
    degree = degree_local + jnp.sum(received, axis=1)
    interior = None
    crossing = None
    mirror = None
    for rounds in range(ITERS):
        current = state
        found = jnp.einsum("vpsb,bj->jvps", current, received, precision=lax.Precision.HIGHEST)
        found = found.reshape(partitions, capacity, width)
        near_local = pick(current, onehot_near)
        near_slots = jnp.einsum(
            "vpsc,jc->jvps", near_local, slot_float, precision=lax.Precision.HIGHEST
        )
        near_in, replies = side_by_side(
            (near_slots.reshape(partitions, capacity, width), found), "net", 0, 0, 1
        )
        interior = advance(
            interior,
            pick(current, onehot_from),
            pick(current, onehot_to),
            branch_cond,
            branch_susc,
            branch_limit,
            branch_steps,
        )
        remote = jnp.einsum(
            "jv,jc->vc",
            replies.reshape(partitions * capacity, width),
            slot_float,
            precision=lax.Precision.HIGHEST,
        )
        remote = remote.reshape(4, periods, scenarios, cuts)
        crossing = advance(crossing, near_local, remote, cut_cond, cut_susc, cut_limit, cut_steps)
        inner_from, inner_to = contributions(interior)
        cut_from_side, cut_to_side = contributions(crossing)
        totals = (
            place(inner_from, onehot_from)
            + place(inner_to, onehot_to)
            + place(cut_from_side, onehot_near)
        )
        near_far = jnp.moveaxis(
            near_in.reshape(partitions * capacity, 4, periods, scenarios), 0, -1
        )
        far_local = pick(current, received)
        mirror = advance(
            mirror, near_far, far_local, mirror_cond, mirror_susc, mirror_limit, mirror_steps
        )
        mirror_from, mirror_to = contributions(mirror)
        totals = totals + place(mirror_to, received)
        gen_price = pick(current[2:4], onehot_gen)
        target_real = gen_real + dual_real - 2.0 * gen_price[0]
        target_react = gen_react + dual_react - 2.0 * gen_price[1]
        dual_real = gen_price[0]
        dual_react = gen_price[1]
        padded = extended(gen_real, (("tm", 0),), 1)
        neighbor_sum = padded[:-2] + padded[2:]
        gen_real = jnp.clip(
            (target_real - gen_linear + gen_ramp * neighbor_sum)
            / (2.0 * gen_quad + 1.0 + gen_ramp * neighbors),
            0.0,
            gen_cap_real,
        )
        gen_react = jnp.clip(target_react, -gen_cap_react, gen_cap_react)
        supply = place(jnp.stack([gen_real + dual_real, gen_react + dual_react]), onehot_gen)
        state = bus_update(
            totals, supply, degree, gen_count, warm_mag, warm_angle, load_real, load_react
        )
    return (state[0], state[1], state[2], gen_real, gen_react)


def solution(mesh):
    return jax.shard_map(
        on_device,
        mesh=mesh,
        in_specs=(
            P("tm", None, "net"),
            P("tm", None, "net"),
            P("tm", None, "net"),
            P("tm", None, "net"),
            P("tm", None, "net"),
            P("tm", None, "net"),
            P("net"),
            P("net"),
            P("net"),
            P("net"),
            P("net"),
            P("net"),
            P("net"),
            P("net"),
            P("net"),
            P("net"),
            P("net"),
            P("net"),
            P("net"),
            P("net", None),
            P("net"),
            P("net"),
            P("net"),
            P("net"),
            P("net"),
        ),
        out_specs=(
            P("tm", None, "net"),
            P("tm", None, "net"),
            P("tm", None, "net"),
            P("tm", None, "net"),
            P("tm", None, "net"),
        ),
        check_vma=False,
    )
```

profile of v0, /device:TPU:1, one launch (start us, length us, event | category | flops | bytes accessed | tf_op | source)
XLA Modules:
  0.0 154.5 jit_solution(15978414299163890898)
XLA Ops:
  1.4 4.5 %collective-permute-start = (f32[1,16,32]{2,1,0:T(8,128)S(1)}, f32[1,16,32]{2,1,0:T(8,128)S(1)}, u32[]{:S(2)}, u32[]{:S(2)}) collective-permute-start(f32[1,16,32]{2,1,0:T(8,128)S(1)} %get-tuple-element.489), channel_id=1, source_target_pairs={{0,1},{1,2},{2,3},{3,4},{4,5},{5,6},{6,7},{8,9},{9,10},{10,11},{11... | collective-permute-start | bytes 6152 | tf_op jit(solution)/shard_map/ppermute | solution.py:36
  5.9 5.6 %collective-permute-start.1 = (f32[1,16,32]{2,1,0:T(8,128)S(1)}, f32[1,16,32]{2,1,0:T(8,128)S(1)}, u32[]{:S(2)}, u32[]{:S(2)}) collective-permute-start(f32[1,16,32]{2,1,0:T(8,128)S(1)} %get-tuple-element.490), channel_id=1, source_target_pairs={{1,0},{2,1},{3,2},{4,3},{5,4},{6,5},{7,6},{9,8},{10,9},{11,10},{12... | collective-permute-start | bytes 6152 | tf_op jit(solution)/shard_map/ppermute | solution.py:38
  15.4 0.7 copy.54
  16.1 12.7 %all-to-all-start = ((f32[64,2,5]{2,1,0:T(2,128)}), f32[64,2,5]{2,1,0:T(2,128)S(1)}, u32[]{:S(2)}, u32[]{:S(2)}) async-start(f32[64,2,5]{2,1,0:T(2,128)} %bitcast.18), calls=%async_computation | async-start | bytes 131072 | tf_op jit(solution)/shard_map/all_to_all | solution.py:203
  31.4 0.8 copy-done
  34.2 0.7 convert_reduce_fusion
  40.4 0.9 fusion.374
  45.4 0.7 reshape.270
  46.9 3.9 %collective-permute-start.2 = (f32[1,16,32]{2,1,0:T(8,128)}, f32[1,16,32]{2,1,0:T(8,128)}, u32[]{:S(2)}, u32[]{:S(2)}) collective-permute-start(f32[1,16,32]{2,1,0:T(8,128)} %get-tuple-element.487), channel_id=1, source_target_pairs={{0,1},{1,2},{2,3},{3,4},{4,5},{5,6},{6,7},{8,9},{9,10},{10,11},{11... | collective-permute-start | bytes 6152 | tf_op jit(solution)/shard_map/ppermute | solution.py:36
  50.8 1.9 %collective-permute-start.3 = (f32[1,16,32]{2,1,0:T(8,128)}, f32[1,16,32]{2,1,0:T(8,128)}, u32[]{:S(2)}, u32[]{:S(2)}) collective-permute-start(f32[1,16,32]{2,1,0:T(8,128)} %get-tuple-element.488), channel_id=1, source_target_pairs={{1,0},{2,1},{3,2},{4,3},{5,4},{6,5},{7,6},{9,8},{10,9},{11,10},{12... | collective-permute-start | bytes 6152 | tf_op jit(solution)/shard_map/ppermute | solution.py:38
  54.8 0.7 reshape.273
  55.5 0.8 pad_maximum_fusion
  56.3 12.7 %all-to-all-start.1 = ((f32[64,4,192]{2,1,0:T(4,128)}), f32[64,4,192]{2,1,0:T(4,128)S(1)}, u32[]{:S(2)}, u32[]{:S(2)}) async-start(f32[64,4,192]{2,1,0:T(4,128)} %pad_maximum_fusion), calls=%async_computation.1 | async-start | bytes 524288 | tf_op jit(solution)/shard_map/all_to_all | solution.py:18
  71.9 11.1 %all-to-all-done.1 = f32[64,4,192]{2,1,0:T(4,128)S(1)} async-done(((f32[64,4,192]{2,1,0:T(4,128)}), f32[64,4,192]{2,1,0:T(4,128)S(1)}, u32[]{:S(2)}, u32[]{:S(2)}) %all-to-all-start.1) | async-done | bytes 196640 | tf_op jit(solution)/shard_map/all_to_all | solution.py:18
  88.6 0.7 fusion.654
  91.3 0.8 reshape.275
  94.2 0.7 fusion.670
  95.7 0.8 slice-done.1
  100.0 0.9 fusion.209
  102.4 0.9 fusion.768
  111.3 0.9 copy-done.35
  112.8 0.7 reshape.277
  114.1 1.0 reshape.276
  115.1 0.8 pad_maximum_fusion.1
  116.0 4.7 %all-to-all-start.2 = ((f32[64,4,192]{2,1,0:T(4,128)}), f32[64,4,192]{2,1,0:T(4,128)S(1)}, u32[]{:S(2)}, u32[]{:S(2)}) async-start(f32[64,4,192]{2,1,0:T(4,128)} %pad_maximum_fusion.1), calls=%async_computation.2 | async-start | bytes 524288 | tf_op jit(solution)/shard_map/all_to_all | solution.py:18
  120.9 1.4 add_bitcast_fusion.1
  123.3 11.7 %all-to-all-done.2 = f32[64,4,192]{2,1,0:T(4,128)S(1)} async-done(((f32[64,4,192]{2,1,0:T(4,128)}), f32[64,4,192]{2,1,0:T(4,128)S(1)}, u32[]{:S(2)}, u32[]{:S(2)}) %all-to-all-start.2) | async-done | bytes 196640 | tf_op jit(solution)/shard_map/all_to_all | solution.py:18
  138.0 0.8 copy-done.29
  142.0 0.8 reshape.279
  143.3 0.9 copy-done.6
  145.0 0.8 copy-done.28
  153.6 0.8 fusion.5
  (517 shorter events, 63.9 us)
Async XLA Ops:
  1.4 44.8 %collective-permute-start = (f32[1,16,32]{2,1,0:T(8,128)S(1)}, f32[1,16,32]{2,1,0:T(8,128)S(1)}, u32[]{:S(2)}, u32[]{:S(2)}) collective-permute-start(f32[1,16,32]{2,1,0:T(8,128)S(1)} %get-tuple-element.489), channel_id=1, source_target_pairs={{0,1},{1,2},{2,3},{3,4},{4,5},{5,6},{6,7},{8,9},{9,10},{10,11},{11... | collective-permute-start | bytes 6152 | tf_op jit(solution)/shard_map/ppermute | solution.py:36
  5.9 40.3 %collective-permute-start.1 = (f32[1,16,32]{2,1,0:T(8,128)S(1)}, f32[1,16,32]{2,1,0:T(8,128)S(1)}, u32[]{:S(2)}, u32[]{:S(2)}) collective-permute-start(f32[1,16,32]{2,1,0:T(8,128)S(1)} %get-tuple-element.490), channel_id=1, source_target_pairs={{1,0},{2,1},{3,2},{4,3},{5,4},{6,5},{7,6},{9,8},{10,9},{11,10},{12... | collective-permute-start | bytes 6152 | tf_op jit(solution)/shard_map/ppermute | solution.py:38
  13.8 18.8 %copy-start.61 = (s32[64]{0:T(128)}, s32[64]{0:T(128)S(1)}, u32[]{:S(2)}) copy-start(s32[64]{0:T(128)S(1)} %add_add_fusion.97) | copy-start | bytes 772
  16.1 36.9 %all-to-all-start = ((f32[64,2,5]{2,1,0:T(2,128)}), f32[64,2,5]{2,1,0:T(2,128)S(1)}, u32[]{:S(2)}, u32[]{:S(2)}) async-start(f32[64,2,5]{2,1,0:T(2,128)} %bitcast.18), calls=%async_computation | async-start | bytes 131072 | tf_op jit(solution)/shard_map/all_to_all | solution.py:203
  30.8 15.4 %copy-start.26 = (f32[2,3,16,32]{3,2,1,0:T(8,128)}, f32[2,3,16,32]{3,2,1,0:T(8,128)S(1)}, u32[]{:S(2)}) copy-start(f32[2,3,16,32]{3,2,1,0:T(8,128)S(1)} %fusion.355) | copy-start | bytes 36868
  37.0 2.0 %copy-start.95 = (pred[256]{0:T(512)(128)(4,1)}, pred[256]{0:T(512)(128)(4,1)S(1)}, u32[]{:S(2)}) copy-start(pred[256]{0:T(512)(128)(4,1)S(1)} %get-tuple-element.498) | copy-start | bytes 772
  37.0 2.6 %copy-start.93 = (pred[256]{0:T(512)(128)(4,1)}, pred[256]{0:T(512)(128)(4,1)S(1)}, u32[]{:S(2)}) copy-start(pred[256]{0:T(512)(128)(4,1)S(1)} %get-tuple-element.496) | copy-start | bytes 772
  37.0 3.3 %copy-start.70 = (pred[256]{0:T(512)(128)(4,1)}, pred[256]{0:T(512)(128)(4,1)S(1)}, u32[]{:S(2)}) copy-start(pred[256]{0:T(512)(128)(4,1)S(1)} %get-tuple-element.495) | copy-start | bytes 772
  44.1 2.1 %copy-start.48 = (f32[3,32]{1,0:T(4,128)}, f32[3,32]{1,0:T(4,128)S(1)}, u32[]{:S(2)}) copy-start(f32[3,32]{1,0:T(4,128)S(1)} %multiply_add_fusion.101) | copy-start | bytes 1156
  44.1 9.7 %copy-start.56 = (f32[256]{0:T(256)}, f32[256]{0:T(256)S(1)}, u32[]{:S(2)}) copy-start(f32[256]{0:T(256)S(1)} %iota_convert_fusion) | copy-start | bytes 3076
  44.8 1.4 copy-start.112
  46.3 6.7 %copy-start.32 = (f32[3,16,32]{2,1,0:T(8,128)}, f32[3,16,32]{2,1,0:T(8,128)S(1)}, u32[]{:S(2)}) copy-start(f32[3,16,32]{2,1,0:T(8,128)S(1)} %get-tuple-element.205) | copy-start | bytes 18436
  46.9 73.9 %collective-permute-start.2 = (f32[1,16,32]{2,1,0:T(8,128)}, f32[1,16,32]{2,1,0:T(8,128)}, u32[]{:S(2)}, u32[]{:S(2)}) collective-permute-start(f32[1,16,32]{2,1,0:T(8,128)} %get-tuple-element.487), channel_id=1, source_target_pairs={{0,1},{1,2},{2,3},{3,4},{4,5},{5,6},{6,7},{8,9},{9,10},{10,11},{11... | collective-permute-start | bytes 6152 | tf_op jit(solution)/shard_map/ppermute | solution.py:36
  50.8 70.0 %collective-permute-start.3 = (f32[1,16,32]{2,1,0:T(8,128)}, f32[1,16,32]{2,1,0:T(8,128)}, u32[]{:S(2)}, u32[]{:S(2)}) collective-permute-start(f32[1,16,32]{2,1,0:T(8,128)} %get-tuple-element.488), channel_id=1, source_target_pairs={{1,0},{2,1},{3,2},{4,3},{5,4},{6,5},{7,6},{9,8},{10,9},{11,10},{12... | collective-permute-start | bytes 6152 | tf_op jit(solution)/shard_map/ppermute | solution.py:38
  56.3 12.8 %copy-start.101 = (f32[256]{0:T(256)S(1)}, f32[256]{0:T(256)}, u32[]{:S(2)}) copy-start(f32[256]{0:T(256)} %get-tuple-element.528) | copy-start | bytes 3076
  56.3 12.8 %copy-start.117 = (f32[256]{0:T(256)S(1)}, f32[256]{0:T(256)}, u32[]{:S(2)}) copy-start(f32[256]{0:T(256)} %convert_reduce_fusion.2) | copy-start | bytes 3076
  56.3 26.6 %all-to-all-start.1 = ((f32[64,4,192]{2,1,0:T(4,128)}), f32[64,4,192]{2,1,0:T(4,128)S(1)}, u32[]{:S(2)}, u32[]{:S(2)}) async-start(f32[64,4,192]{2,1,0:T(4,128)} %pad_maximum_fusion), calls=%async_computation.1 | async-start | bytes 524288 | tf_op jit(solution)/shard_map/all_to_all | solution.py:18
  71.8 21.1 %copy-start.81 = (pred[128]{0:T(512)(128)(4,1)}, pred[128]{0:T(512)(128)(4,1)S(1)}, u32[]{:S(2)}) copy-start(pred[128]{0:T(512)(128)(4,1)S(1)} %get-tuple-element.20) | copy-start | bytes 388
  71.8 21.5 %copy-start.79 = (pred[128]{0:T(512)(128)(4,1)}, pred[128]{0:T(512)(128)(4,1)S(1)}, u32[]{:S(2)}) copy-start(pred[128]{0:T(512)(128)(4,1)S(1)} %get-tuple-element.19) | copy-start | bytes 388
  71.8 21.9 %copy-start.77 = (pred[128]{0:T(512)(128)(4,1)}, pred[128]{0:T(512)(128)(4,1)S(1)}, u32[]{:S(2)}) copy-start(pred[128]{0:T(512)(128)(4,1)S(1)} %get-tuple-element.18) | copy-start | bytes 388
  71.9 22.2 %copy-start.75 = (pred[128]{0:T(512)(128)(4,1)}, pred[128]{0:T(512)(128)(4,1)S(1)}, u32[]{:S(2)}) copy-start(pred[128]{0:T(512)(128)(4,1)S(1)} %get-tuple-element.17) | copy-start | bytes 388
  115.9 4.9 %copy-start.27 = (f32[2,3,16,32]{3,2,1,0:T(8,128)S(1)}, f32[2,3,16,32]{3,2,1,0:T(8,128)}, u32[]{:S(2)}) copy-start(f32[2,3,16,32]{3,2,1,0:T(8,128)} %copy-done.26) | copy-start | bytes 36868
  115.9 4.9 %copy-start.30 = (f32[2,3,16,32]{3,2,1,0:T(8,128)S(1)}, f32[2,3,16,32]{3,2,1,0:T(8,128)}, u32[]{:S(2)}) copy-start(f32[2,3,16,32]{3,2,1,0:T(8,128)} %fusion.209) | copy-start | bytes 36868
  115.9 4.9 %copy-start.33 = (f32[3,16,32]{2,1,0:T(8,128)S(1)}, f32[3,16,32]{2,1,0:T(8,128)}, u32[]{:S(2)}) copy-start(f32[3,16,32]{2,1,0:T(8,128)} %copy-done.32) | copy-start | bytes 18436
  116.0 4.9 %copy-start.37 = (f32[3,16,32]{2,1,0:T(8,128)S(1)}, f32[3,16,32]{2,1,0:T(8,128)}, u32[]{:S(2)}) copy-start(f32[3,16,32]{2,1,0:T(8,128)} %param.32) | copy-start | bytes 18436
  116.0 4.9 %copy-start.49 = (f32[3,32]{1,0:T(4,128)S(1)}, f32[3,32]{1,0:T(4,128)}, u32[]{:S(2)}) copy-start(f32[3,32]{1,0:T(4,128)} %copy-done.48) | copy-start | bytes 1156
  116.0 4.9 %copy-start.84 = (f32[32]{0:T(128)S(1)}, f32[32]{0:T(128)}, u32[]{:S(2)}) copy-start(f32[32]{0:T(128)} %param.36) | copy-start | bytes 388
  116.0 4.9 %copy-start.104 = (f32[32]{0:T(128)S(1)}, f32[32]{0:T(128)}, u32[]{:S(2)}) copy-start(f32[32]{0:T(128)} %param.34) | copy-start | bytes 388
  116.0 4.9 %copy-start.106 = (f32[32]{0:T(128)S(1)}, f32[32]{0:T(128)}, u32[]{:S(2)}) copy-start(f32[32]{0:T(128)} %param.37) | copy-start | bytes 388
  116.0 4.9 %copy-start.108 = (f32[32]{0:T(128)S(1)}, f32[32]{0:T(128)}, u32[]{:S(2)}) copy-start(f32[32]{0:T(128)} %param.38) | copy-start | bytes 388
  116.0 4.9 %copy-start.113 = (f32[32]{0:T(128)S(1)}, f32[32]{0:T(128)}, u32[]{:S(2)}) copy-start(f32[32]{0:T(128)} %copy-done.112) | copy-start | bytes 388
  116.0 18.9 %all-to-all-start.2 = ((f32[64,4,192]{2,1,0:T(4,128)}), f32[64,4,192]{2,1,0:T(4,128)S(1)}, u32[]{:S(2)}, u32[]{:S(2)}) async-start(f32[64,4,192]{2,1,0:T(4,128)} %pad_maximum_fusion.1), calls=%async_computation.2 | async-start | bytes 524288 | tf_op jit(solution)/shard_map/all_to_all | solution.py:18
  (98 other events, 71.6 us)
where the time goes:
time: 156 us; the launch traced here: 154 us
  local copies, waits for them, and re-layouts  47 us (30%)
  starting transfers between devices  46 us (29%)
  other arithmetic  26.5 us (17%)
  waiting for transfers between devices  22.8 us (15%)
  matrix products  9.39 us (6%)
  between operations  2.83 us (2%)
    unnamed x242, local copies, waits for them, and re-layouts  32.4 us
    all_to_all x2, waiting for transfers between devices, side_by_side(): lax.all_to_all(both, axis, split_axis=split_dim, concat_axis=concat_dim,...  22.8 us
    all_to_all x2, starting transfers between devices, side_by_side(): lax.all_to_all(both, axis, split_axis=split_dim, concat_axis=concat_dim,...  17.5 us
    all_to_all x1, starting transfers between devices, on_device(): lax.all_to_all(slot_params.reshape(partitions, capacity, 5), 'net', split...  12.7 us
    ppermute x2, starting transfers between devices, extended(): lax.ppermute(tail, axis, [(i, (i + 1) % count) for i in range(ends)])  8.41 us
    ppermute x2, starting transfers between devices, extended(): lax.ppermute(head, axis, [((i + 1) % count, i) for i in range(ends)])  7.49 us
    mul x24, other arithmetic, branch_energy(): flow_all[3] * flow_all[3]  5.98 us
    dot_general x10, matrix products, pick(): jnp.einsum('...b,bk->...k', values, selector, precision=lax.Precision.HIG...  3.38 us
  transfers between devices with their start and end apart: 7, of which 2 were waited for; matrix products, arithmetic and copies ran while one was open for 27% of the time, Pallas kernels for 0%

commit v1 on v0

v1 whole, which is shorter than its diff:
```python
import jax
import jax.numpy as jnp
from jax import lax
from jax.experimental import pallas as pl
from jax.experimental.pallas import tpu as pltpu
from jax.sharding import PartitionSpec as P

INNER = 4
STEP_SIZE = 0.0005
RADIUS = 0.05
BALANCE_WEIGHT = 2.0
HI = lax.Precision.HIGHEST
F32 = jnp.float32


def mm(a, b):
    return lax.dot_general(a, b, (((1,), (0,)), ((), ())), precision=HI, preferred_element_type=F32)


def mm_t(a, b):
    return lax.dot_general(a, b, (((1,), (1,)), ((), ())), precision=HI, preferred_element_type=F32)


def onehot(ids_row, count):
    n = ids_row.shape[1]
    return (lax.broadcasted_iota(jnp.int32, (count, n), 0) == ids_row).astype(F32)


def col_sum(inc):
    return mm_t(jnp.ones((8, inc.shape[1]), F32), inc)[0:1]


def rows(*parts):
    return jnp.concatenate(parts, axis=0)


def flows(x, g, b):
    mf, af, mt, at = x
    d = af - at
    c = jnp.cos(d)
    s = jnp.sin(d)
    p = mf * mt
    return (
        g * mf * mf - p * (g * c + b * s),
        -b * mf * mf - p * (g * s - b * c),
        g * mt * mt - p * (g * c - b * s),
        -b * mt * mt + p * (g * s + b * c),
    )


def energy_grad(x, t, ft, g, b, l2):
    mf, af, mt, at = x
    d = af - at
    c = jnp.cos(d)
    s = jnp.sin(d)
    p = mf * mt
    ka = g * c + b * s
    kb = g * s - b * c
    kc = g * c - b * s
    kd = g * s + b * c
    f0 = g * mf * mf - p * ka
    f1 = -b * mf * mf - p * kb
    f2 = g * mt * mt - p * kc
    f3 = -b * mt * mt + p * kd
    ef = jnp.maximum(f0 * f0 + f1 * f1 - l2, 0.0)
    et = jnp.maximum(f2 * f2 + f3 * f3 - l2, 0.0)
    w0 = (f0 - ft[0]) + 2.0 * ef * f0
    w1 = (f1 - ft[1]) + 2.0 * ef * f1
    w2 = (f2 - ft[2]) + 2.0 * et * f2
    w3 = (f3 - ft[3]) + 2.0 * et * f3
    g_mf = (mf - t[0]) + w0 * (2.0 * g * mf - mt * ka) - w1 * (2.0 * b * mf + mt * kb) - w2 * mt * kc + w3 * mt * kd
    g_mt = (mt - t[2]) - w0 * mf * ka - w1 * mf * kb + w2 * (2.0 * g * mt - mf * kc) - w3 * (2.0 * b * mt - mf * kd)
    g_d = p * (w0 * kb - w1 * ka + w2 * kd + w3 * kc)
    return (g_mf, (af - t[1]) + g_d, g_mt, (at - t[3]) - g_d)


def solve(x, t, ft, g, b, l2, steps):
    for attempt in range(INNER):
        grad = energy_grad(x, t, ft, g, b, l2)
        x = tuple(
            jnp.where(attempt < steps, xi - jnp.clip(STEP_SIZE * gi, -RADIUS, RADIUS), xi)
            for xi, gi in zip(x, grad)
        )
    return x


def advance(carry, near, far, prm):
    g, b, lim, steps = prm
    ends = (near[0], near[1], far[0], far[1])
    prices = (near[2], near[3], far[2], far[3])
    if carry is None:
        copies = ends
        flow_prev = flows(copies, g, b)
        volt = tuple(jnp.zeros_like(e) for e in ends)
        target = ends
        flow_target = flow_prev
        dual_flow = volt
    else:
        copies, flow_prev = carry
        volt = tuple(c - e for c, e in zip(copies, ends))
        target = tuple(e - v for e, v in zip(ends, volt))
        flow_target = tuple(f + 2.0 * q for f, q in zip(flow_prev, prices))
        dual_flow = tuple(-q for q in prices)
    copies = solve(copies, target, flow_target, g, b, lim * lim, steps)
    flow_prev = flows(copies, g, b)
    side_from = rows(
        copies[0] + volt[0], copies[1] + volt[1], flow_prev[0] + dual_flow[0], flow_prev[1] + dual_flow[1]
    )
    side_to = rows(
        copies[2] + volt[2], copies[3] + volt[3], flow_prev[2] + dual_flow[2], flow_prev[3] + dual_flow[3]
    )
    return (copies, flow_prev), side_from, side_to


def split4(a, n):
    return tuple(a[i * n:(i + 1) * n] for i in range(4))


def vmem_call(kernel, outs, *args):
    return pl.pallas_call(
        kernel,
        out_shape=outs,
        in_specs=[pl.BlockSpec(memory_space=pltpu.VMEM)] * len(args),
        out_specs=tuple(pl.BlockSpec(memory_space=pltpu.VMEM) for _ in outs),
        compiler_params=pltpu.CompilerParams(vmem_limit_bytes=48 * 1024 * 1024),
    )(*args)


def slot_table(peer_col, cap, slots):
    cuts = peer_col.shape[0]
    parts = slots // cap
    mine = (peer_col == lax.broadcasted_iota(jnp.int32, (cuts, parts), 1)).astype(F32)
    same = mm_t(mine, mine)
    earlier = lax.broadcasted_iota(jnp.int32, (cuts, cuts), 1) < lax.broadcasted_iota(jnp.int32, (cuts, cuts), 0)
    rank = jnp.sum(jnp.where(earlier, same, 0.0), axis=1, keepdims=True)
    position = peer_col.astype(F32) * cap + rank
    return (position == lax.broadcasted_iota(jnp.int32, (cuts, slots), 1).astype(F32)).astype(F32)


def on_device(
    warm_mag, warm_angle, load_real, load_react, start_real, start_react,
    gen_bus, gen_linear, gen_quad, gen_ramp, gen_cap_real, gen_cap_react,
    branch_from, branch_to, branch_cond, branch_susc, branch_limit, branch_steps,
    cut_near, cut_peer, cut_bus, cut_cond, cut_susc, cut_limit, cut_steps,
):
    periods, scen, buses = warm_mag.shape
    nrow = periods * scen
    cuts = cut_near.shape[0]
    parts = lax.axis_size("net")
    cap = max(2, cuts // parts * 2)
    slots = parts * cap
    gens = gen_bus.shape[0]
    ntm = lax.axis_size("tm")
    horizon = periods * ntm

    def row(v):
        return v.reshape(1, -1)

    wm = warm_mag.reshape(nrow, buses)
    wa = warm_angle.reshape(nrow, buses)
    lr = load_real.reshape(nrow, buses)
    lq = load_react.reshape(nrow, buses)
    sr = start_real.reshape(nrow, gens)
    sq = start_react.reshape(nrow, gens)
    halo = 2 * scen
    lo = lax.ppermute(sr[nrow - halo:], "tm", [(i, i + 1) for i in range(ntm - 1)])
    hi = lax.ppermute(sr[:halo], "tm", [(i + 1, i) for i in range(ntm - 1)])
    window = nrow + 2 * scen
    period_ext = (
        lax.axis_index("tm") * periods - 1 + jnp.arange(window, dtype=jnp.int32) // scen
    ).reshape(window, 1)
    gen_rows = (row(gen_bus), row(gen_linear), row(gen_quad), row(gen_ramp), row(gen_cap_real), row(gen_cap_react))
    br_rows = (row(branch_from), row(branch_to), row(branch_cond), row(branch_susc), row(branch_limit),
               row(branch_steps.astype(F32)))
    cut_rows = (row(cut_near), row(cut_cond), row(cut_susc), row(cut_limit), row(cut_steps.astype(F32)))
    cut_bus_row = row(cut_bus.astype(F32))
    nvals0 = 128

    def prep_kernel(peer_ref, near_ref, bus_ref, cond_ref, susc_ref, lim_ref, steps_ref, wm_ref, wa_ref,
                    slot_out, pay_out):
        slot_t = slot_table(peer_ref[...], cap, slots)
        slot_out[...] = slot_t
        inc_near = onehot(near_ref[...], buses)
        by_slot = mm(inc_near, slot_t)
        prm = rows(bus_ref[...] + 1.0, cond_ref[...], susc_ref[...], lim_ref[...], steps_ref[...],
                   jnp.zeros((3, cuts), F32))
        vals = rows(
            mm(prm, slot_t),
            mm(rows(wm_ref[...], wa_ref[...]), by_slot),
            jnp.zeros((nvals0 - 8 - 2 * nrow, slots), F32),
        )
        pay_out[...] = vals.T

    slot_t, pay_setup = vmem_call(
        prep_kernel,
        (jax.ShapeDtypeStruct((cuts, slots), F32), jax.ShapeDtypeStruct((slots, nvals0), F32)),
        cut_peer, cut_rows[0], cut_bus_row, cut_rows[1], cut_rows[2], cut_rows[3], cut_rows[4], wm, wa,
    )
    recv_setup = lax.all_to_all(pay_setup, "net", 0, 0, tiled=True)

    def mid_kernel(recv_ref, wm_ref, wa_ref, mirror_out, pay_out):
        mirror = recv_ref[...].T
        mirror_out[...] = mirror
        inc_recv = onehot(mirror[0:1].astype(jnp.int32) - 1, buses)
        vals = rows(mm(rows(wm_ref[...], wa_ref[...]), inc_recv), jnp.zeros((nvals0 - 2 * nrow, slots), F32))
        pay_out[...] = vals.T

    mirror_t, pay_0 = vmem_call(
        mid_kernel,
        (jax.ShapeDtypeStruct((nvals0, slots), F32), jax.ShapeDtypeStruct((slots, nvals0), F32)),
        recv_setup, wm, wa,
    )
    recv_0 = lax.all_to_all(pay_0, "net", 0, 0, tiled=True)

    def iteration(first, refs):
        (st_ref, wm_ref, wa_ref, lr_ref, lq_ref, recv_ref, mirror_ref, slot_ref,
         bf_ref, bt_ref, bc_ref, bs_ref, bl_ref, bn_ref,
         cn_ref, cc_ref, cs_ref, cl_ref, cstep_ref,
         gb_ref, gl_ref, gq_ref, gr_ref, gcr_ref, gcq_ref, pe_ref) = refs[:26]
        rest = refs[26:]
        wmv, wav = wm_ref[...], wa_ref[...]
        slot_t = slot_ref[...]
        mirror = mirror_ref[...]
        inc_from = onehot(bf_ref[...], buses)
        inc_to = onehot(bt_ref[...], buses)
        inc_near = onehot(cn_ref[...], buses)
        inc_recv = onehot(mirror[0:1].astype(jnp.int32) - 1, buses)
        inc_gen = onehot(gb_ref[...], buses)
        degree = col_sum(inc_from) + col_sum(inc_to) + col_sum(inc_near) + col_sum(inc_recv)
        gen_count = col_sum(inc_gen)
        zero_b = jnp.zeros((nrow, buses), F32)
        if first:
            state = (wmv, wav, zero_b, zero_b)
            (sr_lo_ref, sr_ref, sr_hi_ref, sq_ref) = rest[:4]
            outs = rest[4:]
            far_slot = recv_ref[...].T
            zc = jnp.zeros((nrow, cuts), F32)
            zm = jnp.zeros((nrow, slots), F32)
            far_c = mm_t(rows(far_slot[0:nrow], far_slot[nrow:2 * nrow]), slot_t)
            far_cross = (far_c[0:nrow], far_c[nrow:], zc, zc)
            near_mirror = (mirror[8:8 + nrow], mirror[8 + nrow:8 + 2 * nrow], zm, zm)
            carry_in = (None, None, None)
        else:
            state = tuple(st_ref[i] for i in range(4))
            (ci_ref, cc_in_ref, cm_ref, g0_ref, gq0_ref) = rest[:5]
            outs = rest[5:]
            both = recv_ref[...].T
            near_mirror = split4(both[0:4 * nrow], nrow)
            far_c = mm_t(both[4 * nrow:], slot_t)
            far_cross = split4(far_c, nrow)
            carry_in = tuple(
                (tuple(r[i] for i in range(4)), tuple(r[4 + i] for i in range(4))) for r in (ci_ref, cc_in_ref, cm_ref)
            )
        stack = rows(*state)
        pick_from = split4(mm(stack, inc_from), nrow)
        pick_to = split4(mm(stack, inc_to), nrow)
        pick_near = split4(mm(stack, inc_near), nrow)
        pick_recv = split4(mm(stack, inc_recv), nrow)
        prm_in = (bc_ref[...], bs_ref[...], bl_ref[...], bn_ref[...])
        prm_cut = (cc_ref[...], cs_ref[...], cl_ref[...], cstep_ref[...])
        prm_mir = (mirror[1:2], mirror[2:3], mirror[3:4], mirror[4:5])
        carry_i, fi, ti = advance(carry_in[0], pick_from, pick_to, prm_in)
        carry_c, fc, _ = advance(carry_in[1], pick_near, far_cross, prm_cut)
        carry_m, _, tmr = advance(carry_in[2], near_mirror, pick_recv, prm_mir)
        totals = mm_t(fi, inc_from) + mm_t(ti, inc_to) + mm_t(fc, inc_near) + mm_t(tmr, inc_recv)
        totals = split4(totals, nrow)

        lin, quad, ramp, capr, capq = gl_ref[...], gq_ref[...], gr_ref[...], gcr_ref[...], gcq_ref[...]
        per = pe_ref[...]
        nb = (per > 0).astype(F32) + (per < horizon - 1).astype(F32)
        denom = 2.0 * quad + 1.0 + ramp * nb
        if first:
            ext = rows(sr_lo_ref[...], sr_ref[...], sr_hi_ref[...])
            g0 = jnp.clip((ext[scen:scen + window] - lin + ramp * (ext[0:window] + ext[2 * scen:2 * scen + window]))
                          / denom, 0.0, capr)
            g0 = jnp.where((per >= 0) & (per < horizon), g0, 0.0)
            gen_real = g0[scen:scen + nrow]
            gen_react = jnp.clip(sq_ref[...], -capq, capq)
            supply = mm_t(rows(gen_real, gen_react), inc_gen)
        else:
            g0 = g0_ref[...]
            gp = mm(rows(state[2], state[3]), inc_gen)
            gp_r, gp_q = gp[0:nrow], gp[nrow:]
            gen_real = jnp.clip(
                (g0[scen:scen + nrow] - 2.0 * gp_r - lin + ramp * (g0[0:nrow] + g0[2 * scen:2 * scen + nrow]))
                / denom[scen:scen + nrow],
                0.0,
                capr,
            )
            gen_react = jnp.clip(gq0_ref[...] - 2.0 * gp_q, -capq, capq)
            supply = mm_t(rows(gen_real + gp_r, gen_react + gp_q), inc_gen)
        supply_r, supply_q = supply[0:nrow], supply[nrow:]
        mag = (totals[0] + wmv) / (degree + 1.0)
        ang = (totals[1] + wav) / (degree + 1.0)
        weight = 1.0 + BALANCE_WEIGHT * (gen_count + degree)
        pr = BALANCE_WEIGHT * (supply_r - totals[2] - lr_ref[...]) / weight
        pq = BALANCE_WEIGHT * (supply_q - totals[3] - lq_ref[...]) / weight
        if first:
            (st_out, ci_out, cc_out, cm_out, g0_out, gq0_out, pay_out) = outs
            st_out[0] = mag
            st_out[1] = ang
            st_out[2] = pr
            st_out[3] = pq
            for ref, carry in ((ci_out, carry_i), (cc_out, carry_c), (cm_out, carry_m)):
                for i in range(4):
                    ref[i] = carry[0][i]
                    ref[4 + i] = carry[1][i]
            g0_out[...] = g0
            gq0_out[...] = gen_react
            new_stack = rows(mag, ang, pr, pq)
            near_slot = mm(inc_near, slot_t)
            pay_out[...] = rows(mm(new_stack, near_slot), mm(new_stack, inc_recv)).T
        else:
            (mag_out, ang_out, pr_out, gr_out, gq_out) = outs
            mag_out[...] = mag
            ang_out[...] = ang
            pr_out[...] = pr
            gr_out[...] = gen_real
            gq_out[...] = gen_react

    common = (wm, wa, lr, lq)
    tail = (slot_t, *br_rows, *cut_rows, *gen_rows, period_ext)
    sds = jax.ShapeDtypeStruct
    st1, ci1, cc1, cm1, g0, gq0, pay_1 = vmem_call(
        lambda *refs: iteration(True, refs),
        (
            sds((4, nrow, buses), F32),
            sds((8, nrow, buses), F32),
            sds((8, nrow, cuts), F32),
            sds((8, nrow, slots), F32),
            sds((window, gens), F32),
            sds((nrow, gens), F32),
            sds((slots, 8 * nrow), F32),
        ),
        wm, *common, recv_0, mirror_t, *tail, lo, sr, hi, sq,
    )
    recv_1 = lax.all_to_all(pay_1, "net", 0, 0, tiled=True)
    mag, ang, pr, gr, gq = vmem_call(
        lambda *refs: iteration(False, refs),
        (
            sds((nrow, buses), F32),
            sds((nrow, buses), F32),
            sds((nrow, buses), F32),
            sds((nrow, gens), F32),
            sds((nrow, gens), F32),
        ),
        st1, *common, recv_1, mirror_t, *tail, ci1, cc1, cm1, g0, gq0,
    )
    shape_b = (periods, scen, buses)
    shape_g = (periods, scen, gens)
    return (mag.reshape(shape_b), ang.reshape(shape_b), pr.reshape(shape_b), gr.reshape(shape_g),
            gq.reshape(shape_g))


def solution(mesh):
    bus = P("tm", None, "net")
    one = P("net")
    return jax.shard_map(
        on_device,
        mesh=mesh,
        in_specs=(bus,) * 6 + (one,) * 12 + (one, P("net", None)) + (one,) * 5,
        out_specs=(bus,) * 5,
        check_vma=False,
    )
```

time: 156 us -> 89.2 us (0.57)
  blocking collectives: 0 us -> 52.4 us
  local copies, waits for them, and re-layouts: 47 us -> 4.69 us
  starting transfers between devices: 46 us -> 11.9 us
  other arithmetic: 26.5 us -> 0.68 us
  waiting for transfers between devices: 22.8 us -> 3.15 us
  Pallas kernels: 0 us -> 14.9 us
  matrix products: 9.39 us -> 0 us
  between operations: 2.83 us -> 0.88 us
    all_to_all x0 -> x2, blocking collectives: none -> 52.4 us  [the longest x1 28.1 us: on_device(): recv_setup = lax.all_to_all(pay_setup, 'net', 0, 0, tiled=True)]
    unnamed x242 -> x53, local copies, waits for them, and re-layouts: 32.4 us -> 4.44 us
    all_to_all x3 -> x1, starting transfers between devices: 30.1 us -> 4.7 us  [on_device(): recv_0 = lax.all_to_all(pay_0, 'net', 0, 0, tiled=True)]
    all_to_all x3 -> x1, waiting for transfers between devices: 22.8 us -> 0.42 us  [on_device(): recv_0 = lax.all_to_all(pay_0, 'net', 0, 0, tiled=True)]
    pallas_call x0 -> x4, Pallas kernels: none -> 14.9 us  [vmem_call(): pl.pallas_call(kernel, out_shape=outs, in_specs=[pl.BlockSpec(memory_spac...]
    mul x75 -> x0, other arithmetic: 11.2 us -> none  [the longest x24 5.98 us: branch_energy(): flow_all[3] * flow_all[3]]
    ppermute x4 -> x2, starting transfers between devices: 15.9 us -> 7.16 us  [the longest x1 5.24 us: on_device(): lax.ppermute(sr[nrow - halo:], 'tm', [(i, i + 1) for i in range(ntm - 1)])]
    dot_general x26 -> x0, matrix products: 8.54 us -> none  [the longest x10 3.38 us: pick(): jnp.einsum('...b,bk->...k', values, selector, precision=lax.Precision.HIG...]
  transfers between devices with their start and end apart: 7 -> 3, of which waited for: 2 -> 2; matrix products, arithmetic and copies ran while one was open for 27% -> 0% of each run, Pallas kernels for 0% -> 0%
where the time goes in v1:
time: 89.2 us; the launch traced here: 88.6 us
  blocking collectives  52.4 us (59%)
  Pallas kernels  14.9 us (17%)
  starting transfers between devices  11.9 us (13%)
  local copies, waits for them, and re-layouts  4.69 us (5%)
  waiting for transfers between devices  3.15 us (4%)
    all_to_all x1, blocking collectives, on_device(): recv_setup = lax.all_to_all(pay_setup, 'net', 0, 0, tiled=True)  28.1 us
    all_to_all x1, blocking collectives, on_device(): recv_1 = lax.all_to_all(pay_1, 'net', 0, 0, tiled=True)  24.3 us
    pallas_call x4, Pallas kernels, vmem_call(): pl.pallas_call(kernel, out_shape=outs, in_specs=[pl.BlockSpec(memory_spac...  14.9 us
    ppermute x1, starting transfers between devices, on_device(): lax.ppermute(sr[nrow - halo:], 'tm', [(i, i + 1) for i in range(ntm - 1)])  5.24 us
    all_to_all x1, starting transfers between devices, on_device(): recv_0 = lax.all_to_all(pay_0, 'net', 0, 0, tiled=True)  4.7 us
    unnamed x53, local copies, waits for them, and re-layouts  4.44 us
    ppermute x1, waiting for transfers between devices, on_device(): hi = lax.ppermute(sr[:halo], 'tm', [(i + 1, i) for i in range(ntm - 1)])  2.73 us
    ppermute x1, starting transfers between devices, on_device(): hi = lax.ppermute(sr[:halo], 'tm', [(i + 1, i) for i in range(ntm - 1)])  1.92 us
  transfers between devices with their start and end apart: 3, of which 2 were waited for; matrix products, arithmetic and copies ran while one was open for 0% of the time, Pallas kernels for 0%

profile of v1, /device:TPU:1, one launch (start us, length us, event | category | flops | bytes accessed | tf_op | source)
XLA Modules:
  0.0 88.6 jit_solution(6348285948487634889)
XLA Ops:
  0.6 0.7 convert_bitcast_fusion.steps_ref.refs_18_
  1.3 0.6 copy-done.24
  2.0 0.1 copy.30.peer_ref
  2.1 0.6 copy-done.11
  2.7 0.0 copy-done.8
  2.7 0.0 copy-done.9
  2.7 0.0 copy-done.10
  2.8 0.8 copy-done
  3.6 0.8 copy-done.2
  4.4 1.1 %shard_map.272 = (f32[64,128]{1,0:T(8,128)S(1)}, f32[128,128]{1,0:T(8,128)S(1)}) custom-call(s32[64,1]{1,0:T(8,128)S(1)} %copy.30.peer_ref, s32[1,64]{1,0:T(1,128)S(1)} %bitcast.57, f32[1,64]{1,0:T(1,128)S(1)} %convert_bitcast_fusion.1.bus_ref, f32[1,64]{1,0:T(1,128)S(1)} %bitcast.60, f32[1,64]{1,0:T(1,128)S(1)} %bitcast.63, f32[1,64]{1,0:T(1,128)S(1)} %bitcast.66, ...), custom_call_target="tpu_custom_call" | custom-call | tf_op jit(solution)/shard_map/pallas_call | solution.py:120
  5.5 28.1 %all_to_all.33 = f32[64,2,128]{2,1,0:T(2,128)S(1)} all-to-all(f32[64,2,128]{2,1,0:T(2,128)S(1)} %bitcast.53), channel_id=1, replica_groups=mesh['net'=64,'tm'=8] {'net'}, dimensions={0} | all-to-all | bytes 131072 | tf_op jit(solution)/shard_map/all_to_all | solution.py:199
  33.6 1.0 %shard_map.273 = (f32[128,128]{1,0:T(8,128)S(1)}, f32[128,128]{1,0:T(8,128)}) custom-call(f32[128,128]{1,0:T(8,128)S(1)} %bitcast.47, f32[48,256]{1,0:T(8,128)S(1)} %bitcast.38, f32[48,256]{1,0:T(8,128)S(1)} %bitcast.43), custom_call_target="tpu_custom_call" | custom-call | tf_op jit(solution)/shard_map/pallas_call | solution.py:120
  34.6 4.7 %all-to-all-start.1 = ((f32[64,2,128]{2,1,0:T(2,128)}), f32[64,2,128]{2,1,0:T(2,128)S(1)}, u32[]{:S(2)}, u32[]{:S(2)}) async-start(f32[64,2,128]{2,1,0:T(2,128)} %bitcast.12), calls=%async_computation.1 | async-start | bytes 131072 | tf_op jit(solution)/shard_map/all_to_all | solution.py:213
  39.4 5.2 %collective-permute-start = (f32[32,32]{1,0:T(8,128)S(1)}, f32[32,32]{1,0:T(8,128)S(1)}, u32[]{:S(2)}, u32[]{:S(2)}) collective-permute-start(f32[32,32]{1,0:T(8,128)S(1)} %bitcast.92), channel_id=1, source_target_pairs={{0,1},{1,2},{2,3},{3,4},{4,5},{5,6},{6,7},{8,9},{9,10},{10,11},{11... | collective-permute-start | bytes 12296 | tf_op jit(solution)/shard_map/ppermute | solution.py:166
  44.6 1.9 %collective-permute-start.1 = (f32[32,32]{1,0:T(8,128)S(1)}, f32[32,32]{1,0:T(8,128)S(1)}, u32[]{:S(2)}, u32[]{:S(2)}) collective-permute-start(f32[32,32]{1,0:T(8,128)S(1)} %bitcast.91), channel_id=1, source_target_pairs={{1,0},{2,1},{3,2},{4,3},{5,4},{6,5},{7,6},{9,8},{10,9},{11,10},{12... | collective-permute-start | bytes 12296 | tf_op jit(solution)/shard_map/ppermute | solution.py:167
  46.6 0.7 copy-done.23
  47.3 2.7 %collective-permute-done.1.refs_28_ = f32[32,32]{1,0:T(8,128)S(1)} collective-permute-done((f32[32,32]{1,0:T(8,128)S(1)}, f32[32,32]{1,0:T(8,128)S(1)}, u32[]{:S(2)}, u32[]{:S(2)}) %collective-permute-start.1) | collective-permute-done | bytes 4128 | tf_op jit(solution)/shard_map/ppermute | solution.py:167
  50.0 0.4 all-to-all-done.1
  50.5 0.6 copy-done.13
  51.1 0.0 copy-done.14
  51.1 0.0 copy-done.15
  51.1 0.0 copy-done.16
  51.1 0.0 copy-done.19
  51.1 0.0 copy-done.20
  51.2 0.0 copy-done.21
  51.2 0.0 copy-done.22
  51.2 0.0 copy-done.12
  51.2 6.4 %shard_map.274 = (f32[4,48,256]{2,1,0:T(8,128)S(1)}, f32[8,48,256]{2,1,0:T(8,128)S(1)}, f32[8,48,64]{2,1,0:T(8,128)S(1)}, f32[8,48,128]{2,1,0:T(8,128)S(1)}, f32...) custom-call(f32[48,256]{1,0:T(8,128)S(1)} %bitcast.39, f32[48,256]{1,0:T(8,128)S(1)} %bitcast.40, ...), custom_call_target="tpu_custom_call" | custom-call | tf_op jit(solution)/shard_map/pallas_call | solution.py:120
  57.7 0.1 all_to_all.27
  57.8 24.3 %all_to_all.34 = f32[64,2,384]{2,1,0:T(2,128)S(1)} all-to-all(f32[64,2,384]{2,1,0:T(2,128)S(1)} %all_to_all.27), channel_id=1, replica_groups=mesh['net'=64,'tm'=8] {'net'}, dimensions={0} | all-to-all | bytes 393216 | tf_op jit(solution)/shard_map/all_to_all | solution.py:337
  82.1 0.1 all_to_all.29.refs_5_
  82.2 6.4 %shard_map.275 = (f32[48,256]{1,0:T(8,128)}, f32[48,256]{1,0:T(8,128)}, f32[48,256]{1,0:T(8,128)}, f32[48,32]{1,0:T(8,128)}, f32[48,32]{1,0:T(8,128)}) custom-call(f32[4,48,256]{2,1,0:T(8,128)S(1)} %get-tuple-element.25.refs_0_, f32[48,256]{1,0:T(8,128)S(1)} %bitcast.41, f32[48,256]{1,0:T(8,128)S(1)} %bitcast.45, f32[48,256]{1,0:T(8,128)S(1)} %bitcast.49, ...), custom_call_target="tpu_custom_call" | custom-call | tf_op jit(solution)/shard_map/pallas_call | solution.py:120
  (40 shorter events, 0.1 us)
Async XLA Ops:
  0.6 0.7 copy-start.25
  1.3 0.7 copy-start.24
  2.1 0.7 copy-start.11
  2.1 0.7 copy-start.8
  2.1 0.7 copy-start.9
  2.1 0.7 copy-start.10
  2.8 0.8 copy-start
  3.6 0.8 copy-start.2
  5.4 28.2 %copy-start.1 = (f32[3,16,256]{2,1,0:T(8,128)S(1)}, f32[3,16,256]{2,1,0:T(8,128)}, u32[]{:S(2)}) copy-start(f32[3,16,256]{2,1,0:T(8,128)} %param.25) | copy-start | bytes 147460
  5.4 28.2 %copy-start.3 = (f32[3,16,256]{2,1,0:T(8,128)S(1)}, f32[3,16,256]{2,1,0:T(8,128)}, u32[]{:S(2)}) copy-start(f32[3,16,256]{2,1,0:T(8,128)} %param.26) | copy-start | bytes 147460
  34.6 4.7 %copy-start.6 = (f32[3,16,32]{2,1,0:T(8,128)S(1)}, f32[3,16,32]{2,1,0:T(8,128)}, u32[]{:S(2)}) copy-start(f32[3,16,32]{2,1,0:T(8,128)} %param.29) | copy-start | bytes 18436
  34.6 15.8 %all-to-all-start.1 = ((f32[64,2,128]{2,1,0:T(2,128)}), f32[64,2,128]{2,1,0:T(2,128)S(1)}, u32[]{:S(2)}, u32[]{:S(2)}) async-start(f32[64,2,128]{2,1,0:T(2,128)} %bitcast.12), calls=%async_computation.1 | async-start | bytes 131072 | tf_op jit(solution)/shard_map/all_to_all | solution.py:213
  39.3 11.2 %copy-start.5 = (f32[3,16,256]{2,1,0:T(8,128)S(1)}, f32[3,16,256]{2,1,0:T(8,128)}, u32[]{:S(2)}) copy-start(f32[3,16,256]{2,1,0:T(8,128)} %param.28) | copy-start | bytes 147460
  39.4 11.1 %copy-start.4 = (f32[3,16,256]{2,1,0:T(8,128)S(1)}, f32[3,16,256]{2,1,0:T(8,128)}, u32[]{:S(2)}) copy-start(f32[3,16,256]{2,1,0:T(8,128)} %param.27) | copy-start | bytes 147460
  39.4 7.9 %collective-permute-start = (f32[32,32]{1,0:T(8,128)S(1)}, f32[32,32]{1,0:T(8,128)S(1)}, u32[]{:S(2)}, u32[]{:S(2)}) collective-permute-start(f32[32,32]{1,0:T(8,128)S(1)} %bitcast.92), channel_id=1, source_target_pairs={{0,1},{1,2},{2,3},{3,4},{4,5},{5,6},{6,7},{8,9},{9,10},{10,11},{11... | collective-permute-start | bytes 12296 | tf_op jit(solution)/shard_map/ppermute | solution.py:166
  44.6 5.4 %collective-permute-start.1 = (f32[32,32]{1,0:T(8,128)S(1)}, f32[32,32]{1,0:T(8,128)S(1)}, u32[]{:S(2)}, u32[]{:S(2)}) collective-permute-start(f32[32,32]{1,0:T(8,128)S(1)} %bitcast.91), channel_id=1, source_target_pairs={{1,0},{2,1},{3,2},{4,3},{5,4},{6,5},{7,6},{9,8},{10,9},{11,10},{12... | collective-permute-start | bytes 12296 | tf_op jit(solution)/shard_map/ppermute | solution.py:167
  46.6 0.7 copy-start.23
  47.2 3.3 %copy-start.7 = (f32[3,16,32]{2,1,0:T(8,128)S(1)}, f32[3,16,32]{2,1,0:T(8,128)}, u32[]{:S(2)}) copy-start(f32[3,16,32]{2,1,0:T(8,128)} %param.30) | copy-start | bytes 18436
  50.4 0.7 copy-start.13
  50.4 0.7 copy-start.14
  50.4 0.7 copy-start.15
  50.4 0.7 copy-start.16
  50.4 0.7 copy-start.18
  50.4 0.7 copy-start.19
  50.4 0.7 copy-start.20
  50.5 0.7 copy-start.21
  50.5 0.7 copy-start.22
  50.5 0.8 copy-start.12
  50.5 0.7 copy-start.17

commit v2 on v1

--- a/solution.py
+++ b/solution.py
@@ -212,59 +212,33 @@
     )
     recv_0 = lax.all_to_all(pay_0, "net", 0, 0, tiled=True)
 
-    def iteration(first, refs):
-        (st_ref, wm_ref, wa_ref, lr_ref, lq_ref, recv_ref, mirror_ref, slot_ref,
-         bf_ref, bt_ref, bc_ref, bs_ref, bl_ref, bn_ref,
-         cn_ref, cc_ref, cs_ref, cl_ref, cstep_ref,
-         gb_ref, gl_ref, gq_ref, gr_ref, gcr_ref, gcq_ref, pe_ref) = refs[:26]
-        rest = refs[26:]
-        wmv, wav = wm_ref[...], wa_ref[...]
-        slot_t = slot_ref[...]
-        mirror = mirror_ref[...]
+    def local_part(first, refs):
+        if first:
+            (wm_ref, wa_ref, bf_ref, bt_ref, bc_ref, bs_ref, bl_ref, bn_ref,
+             gb_ref, gl_ref, gq_ref, gr_ref, gcr_ref, gcq_ref, pe_ref,
+             sr_lo_ref, sr_ref, sr_hi_ref, sq_ref,
+             tot_out, sup_out, ci_out, g0_out, gq0_out) = refs
+            zero_b = jnp.zeros((nrow, buses), F32)
+            state = (wm_ref[...], wa_ref[...], zero_b, zero_b)
+            carry_in = None
+        else:
+            (st_ref, bf_ref, bt_ref, bc_ref, bs_ref, bl_ref, bn_ref,
+             gb_ref, gl_ref, gq_ref, gr_ref, gcr_ref, gcq_ref, pe_ref,
+             ci_ref, g0_ref, gq0_ref,
+             tot_out, sup_out, gr_out, gq_out) = refs
+            state = tuple(st_ref[i] for i in range(4))
+            carry_in = (tuple(ci_ref[i] for i in range(4)), tuple(ci_ref[4 + i] for i in range(4)))
         inc_from = onehot(bf_ref[...], buses)
         inc_to = onehot(bt_ref[...], buses)
-        inc_near = onehot(cn_ref[...], buses)
-        inc_recv = onehot(mirror[0:1].astype(jnp.int32) - 1, buses)
         inc_gen = onehot(gb_ref[...], buses)
-        degree = col_sum(inc_from) + col_sum(inc_to) + col_sum(inc_near) + col_sum(inc_recv)
-        gen_count = col_sum(inc_gen)
-        zero_b = jnp.zeros((nrow, buses), F32)
-        if first:
-            state = (wmv, wav, zero_b, zero_b)
-            (sr_lo_ref, sr_ref, sr_hi_ref, sq_ref) = rest[:4]
-            outs = rest[4:]
-            far_slot = recv_ref[...].T
-            zc = jnp.zeros((nrow, cuts), F32)
-            zm = jnp.zeros((nrow, slots), F32)
-            far_c = mm_t(rows(far_slot[0:nrow], far_slot[nrow:2 * nrow]), slot_t)
-            far_cross = (far_c[0:nrow], far_c[nrow:], zc, zc)
-            near_mirror = (mirror[8:8 + nrow], mirror[8 + nrow:8 + 2 * nrow], zm, zm)
-            carry_in = (None, None, None)
-        else:
-            state = tuple(st_ref[i] for i in range(4))
-            (ci_ref, cc_in_ref, cm_ref, g0_ref, gq0_ref) = rest[:5]
-            outs = rest[5:]
-            both = recv_ref[...].T
-            near_mirror = split4(both[0:4 * nrow], nrow)
-            far_c = mm_t(both[4 * nrow:], slot_t)
-            far_cross = split4(far_c, nrow)
-            carry_in = tuple(
-                (tuple(r[i] for i in range(4)), tuple(r[4 + i] for i in range(4))) for r in (ci_ref, cc_in_ref, cm_ref)
-            )
         stack = rows(*state)
         pick_from = split4(mm(stack, inc_from), nrow)
         pick_to = split4(mm(stack, inc_to), nrow)
-        pick_near = split4(mm(stack, inc_near), nrow)
-        pick_recv = split4(mm(stack, inc_recv), nrow)
         prm_in = (bc_ref[...], bs_ref[...], bl_ref[...], bn_ref[...])
-        prm_cut = (cc_ref[...], cs_ref[...], cl_ref[...], cstep_ref[...])
-        prm_mir = (mirror[1:2], mirror[2:3], mirror[3:4], mirror[4:5])
-        carry_i, fi, ti = advance(carry_in[0], pick_from, pick_to, prm_in)
-        carry_c, fc, _ = advance(carry_in[1], pick_near, far_cross, prm_cut)
-        carry_m, _, tmr = advance(carry_in[2], near_mirror, pick_recv, prm_mir)
-        totals = mm_t(fi, inc_from) + mm_t(ti, inc_to) + mm_t(fc, inc_near) + mm_t(tmr, inc_recv)
-        totals = split4(totals, nrow)
-
+        carry_i, fi, ti = advance(carry_in, pick_from, pick_to, prm_in)
+        totals = mm_t(fi, inc_from) + mm_t(ti, inc_to)
+        for i in range(4):
+            tot_out[i] = totals[i * nrow:(i + 1) * nrow]
         lin, quad, ramp, capr, capq = gl_ref[...], gq_ref[...], gr_ref[...], gcr_ref[...], gcq_ref[...]
         per = pe_ref[...]
         nb = (per > 0).astype(F32) + (per < horizon - 1).astype(F32)
@@ -277,6 +251,11 @@
             gen_real = g0[scen:scen + nrow]
             gen_react = jnp.clip(sq_ref[...], -capq, capq)
             supply = mm_t(rows(gen_real, gen_react), inc_gen)
+            for i in range(4):
+                ci_out[i] = carry_i[0][i]
+                ci_out[4 + i] = carry_i[1][i]
+            g0_out[...] = g0
+            gq0_out[...] = gen_react
         else:
             g0 = g0_ref[...]
             gp = mm(rows(state[2], state[3]), inc_gen)
@@ -289,62 +268,119 @@
             )
             gen_react = jnp.clip(gq0_ref[...] - 2.0 * gp_q, -capq, capq)
             supply = mm_t(rows(gen_real + gp_r, gen_react + gp_q), inc_gen)
-        supply_r, supply_q = supply[0:nrow], supply[nrow:]
+            gr_out[...] = gen_real
+            gq_out[...] = gen_react
+        sup_out[0] = supply[0:nrow]
+        sup_out[1] = supply[nrow:]
+
+    def mirror0_kernel(mirror_ref, wm_ref, wa_ref, tot_out, cm_out):
+        mirror = mirror_ref[...]
+        inc_recv = onehot(mirror[0:1].astype(jnp.int32) - 1, buses)
+        zm = jnp.zeros((nrow, slots), F32)
+        zero_b = jnp.zeros((nrow, buses), F32)
+        stack = rows(wm_ref[...], wa_ref[...], zero_b, zero_b)
+        pick_recv = split4(mm(stack, inc_recv), nrow)
+        near_mirror = (mirror[8:8 + nrow], mirror[8 + nrow:8 + 2 * nrow], zm, zm)
+        prm_mir = (mirror[1:2], mirror[2:3], mirror[3:4], mirror[4:5])
+        carry_m, _, tmr = advance(None, near_mirror, pick_recv, prm_mir)
+        totals = mm_t(tmr, inc_recv)
+        for i in range(4):
+            tot_out[i] = totals[i * nrow:(i + 1) * nrow]
+            cm_out[i] = carry_m[0][i]
+            cm_out[4 + i] = carry_m[1][i]
+
+    def cut_part(first, refs):
+        (st_ref, wm_ref, wa_ref, lr_ref, lq_ref, recv_ref, mirror_ref, slot_ref,
+         bf_ref, bt_ref, cn_ref, cc_ref, cs_ref, cl_ref, cstep_ref, gb_ref,
+         tin_ref, sup_ref, tm_ref) = refs[:19]
+        rest = refs[19:]
+        wmv, wav = wm_ref[...], wa_ref[...]
+        slot_t = slot_ref[...]
+        mirror = mirror_ref[...]
+        inc_near = onehot(cn_ref[...], buses)
+        inc_recv = onehot(mirror[0:1].astype(jnp.int32) - 1, buses)
+        degree = (col_sum(onehot(bf_ref[...], buses)) + col_sum(onehot(bt_ref[...], buses)) + col_sum(inc_near)
+                  + col_sum(inc_recv))
+        gen_count = col_sum(onehot(gb_ref[...], buses))
+        prm_cut = (cc_ref[...], cs_ref[...], cl_ref[...], cstep_ref[...])
+        if first:
+            (cc_out, st_out, pay_out) = rest
+            zero_b = jnp.zeros((nrow, buses), F32)
+            state = (wmv, wav, zero_b, zero_b)
+            far_slot = recv_ref[...].T
+            zc = jnp.zeros((nrow, cuts), F32)
+            far_c = mm_t(rows(far_slot[0:nrow], far_slot[nrow:2 * nrow]), slot_t)
+            far_cross = (far_c[0:nrow], far_c[nrow:], zc, zc)
+            stack = rows(*state)
+            pick_near = split4(mm(stack, inc_near), nrow)
+            carry_c, fc, _ = advance(None, pick_near, far_cross, prm_cut)
+            totals = tin_ref[...] + tm_ref[...] + mm_t(fc, inc_near).reshape(4, nrow, buses)
+        else:
+            (cc_in_ref, cm_ref, mag_out, ang_out, pr_out) = rest
+            state = tuple(st_ref[i] for i in range(4))
+            both = recv_ref[...].T
+            near_mirror = split4(both[0:4 * nrow], nrow)
+            far_cross = split4(mm_t(both[4 * nrow:], slot_t), nrow)
+            stack = rows(*state)
+            pick_near = split4(mm(stack, inc_near), nrow)
+            pick_recv = split4(mm(stack, inc_recv), nrow)
+            carry_c_in = (tuple(cc_in_ref[i] for i in range(4)), tuple(cc_in_ref[4 + i] for i in range(4)))
+            carry_m_in = (tuple(cm_ref[i] for i in range(4)), tuple(cm_ref[4 + i] for i in range(4)))
+            _, fc, _ = advance(carry_c_in, pick_near, far_cross, prm_cut)
+            prm_mir = (mirror[1:2], mirror[2:3], mirror[3:4], mirror[4:5])
+            _, _, tmr = advance(carry_m_in, near_mirror, pick_recv, prm_mir)
+            totals = tin_ref[...] + (mm_t(fc, inc_near) + mm_t(tmr, inc_recv)).reshape(4, nrow, buses)
         mag = (totals[0] + wmv) / (degree + 1.0)
         ang = (totals[1] + wav) / (degree + 1.0)
         weight = 1.0 + BALANCE_WEIGHT * (gen_count + degree)
-        pr = BALANCE_WEIGHT * (supply_r - totals[2] - lr_ref[...]) / weight
-        pq = BALANCE_WEIGHT * (supply_q - totals[3] - lq_ref[...]) / weight
+        pr = BALANCE_WEIGHT * (sup_ref[0] - totals[2] - lr_ref[...]) / weight
+        pq = BALANCE_WEIGHT * (sup_ref[1] - totals[3] - lq_ref[...]) / weight
         if first:
-            (st_out, ci_out, cc_out, cm_out, g0_out, gq0_out, pay_out) = outs
+            for i in range(4):
+                cc_out[i] = carry_c[0][i]
+                cc_out[4 + i] = carry_c[1][i]
             st_out[0] = mag
             st_out[1] = ang
             st_out[2] = pr
             st_out[3] = pq
-            for ref, carry in ((ci_out, carry_i), (cc_out, carry_c), (cm_out, carry_m)):
-                for i in range(4):
-                    ref[i] = carry[0][i]
-                    ref[4 + i] = carry[1][i]
-            g0_out[...] = g0
-            gq0_out[...] = gen_react
             new_stack = rows(mag, ang, pr, pq)
             near_slot = mm(inc_near, slot_t)
             pay_out[...] = rows(mm(new_stack, near_slot), mm(new_stack, inc_recv)).T
         else:
-            (mag_out, ang_out, pr_out, gr_out, gq_out) = outs
             mag_out[...] = mag
             ang_out[...] = ang
             pr_out[...] = pr
-            gr_out[...] = gen_real
-            gq_out[...] = gen_react
-
-    common = (wm, wa, lr, lq)
-    tail = (slot_t, *br_rows, *cut_rows, *gen_rows, period_ext)
+
     sds = jax.ShapeDtypeStruct
-    st1, ci1, cc1, cm1, g0, gq0, pay_1 = vmem_call(
-        lambda *refs: iteration(True, refs),
-        (
-            sds((4, nrow, buses), F32),
-            sds((8, nrow, buses), F32),
-            sds((8, nrow, cuts), F32),
-            sds((8, nrow, slots), F32),
-            sds((window, gens), F32),
-            sds((nrow, gens), F32),
-            sds((slots, 8 * nrow), F32),
-        ),
-        wm, *common, recv_0, mirror_t, *tail, lo, sr, hi, sq,
+    tot_shape = sds((4, nrow, buses), F32)
+    br_all = br_rows
+    gen_all = (*gen_rows, period_ext)
+    tin0, sup0, ci1, g0, gq0 = vmem_call(
+        lambda *refs: local_part(True, refs),
+        (tot_shape, sds((2, nrow, buses), F32), sds((8, nrow, buses), F32), sds((window, gens), F32),
+         sds((nrow, gens), F32)),
+        wm, wa, *br_all, *gen_all, lo, sr, hi, sq,
+    )
+    tm0, cm1 = vmem_call(
+        mirror0_kernel, (tot_shape, sds((8, nrow, slots), F32)), mirror_t, wm, wa,
+    )
+    cut_in = (*cut_rows, gen_rows[0])
+    cc1, st1, pay_1 = vmem_call(
+        lambda *refs: cut_part(True, refs),
+        (sds((8, nrow, cuts), F32), tot_shape, sds((slots, 8 * nrow), F32)),
+        wm, wm, wa, lr, lq, recv_0, mirror_t, slot_t, br_rows[0], br_rows[1], *cut_in, tin0, sup0, tm0,
     )
     recv_1 = lax.all_to_all(pay_1, "net", 0, 0, tiled=True)
-    mag, ang, pr, gr, gq = vmem_call(
-        lambda *refs: iteration(False, refs),
-        (
-            sds((nrow, buses), F32),
-            sds((nrow, buses), F32),
-            sds((nrow, buses), F32),
-            sds((nrow, gens), F32),
-            sds((nrow, gens), F32),
-        ),
-        st1, *common, recv_1, mirror_t, *tail, ci1, cc1, cm1, g0, gq0,
+    tin1, sup1, gr, gq = vmem_call(
+        lambda *refs: local_part(False, refs),
+        (tot_shape, sds((2, nrow, buses), F32), sds((nrow, gens), F32), sds((nrow, gens), F32)),
+        st1, *br_all, *gen_all, ci1, g0, gq0,
+    )
+    mag, ang, pr = vmem_call(
+        lambda *refs: cut_part(False, refs),
+        (sds((nrow, buses), F32), sds((nrow, buses), F32), sds((nrow, buses), F32)),
+        st1, wm, wa, lr, lq, recv_1, mirror_t, slot_t, br_rows[0], br_rows[1], *cut_in, tin1, sup1, tin1,
+        cc1, cm1,
     )
     shape_b = (periods, scen, buses)
     shape_g = (periods, scen, gens)

time: 89.2 us -> 88.4 us (level)
  blocking collectives: 52.4 us -> 28.1 us
  starting transfers between devices: 11.9 us -> 24 us
  waiting for transfers between devices: 3.15 us -> 12.1 us
  Pallas kernels: 14.9 us -> 16.7 us
    all_to_all x1 -> x0, blocking collectives: 24.3 us -> none  [on_device(): recv_1 = lax.all_to_all(pay_1, 'net', 0, 0, tiled=True)]
    all_to_all x0 -> x1, starting transfers between devices: none -> 12.3 us  [on_device(): recv_1 = lax.all_to_all(pay_1, 'net', 0, 0, tiled=True)]
    all_to_all x0 -> x1, waiting for transfers between devices: none -> 9.36 us  [on_device(): recv_1 = lax.all_to_all(pay_1, 'net', 0, 0, tiled=True)]
    pallas_call x4 -> x7, Pallas kernels: 14.9 us -> 16.7 us  [vmem_call(): pl.pallas_call(kernel, out_shape=outs, in_specs=[pl.BlockSpec(memory_spac...]
  transfers between devices with their start and end apart: 3 -> 4, of which waited for: 2 -> 2; matrix products, arithmetic and copies ran while one was open for 0% -> 0% of each run, Pallas kernels for 0% -> 9%
where the time goes in v2:
time: 88.4 us; the launch traced here: 87.9 us
  blocking collectives  28.1 us (32%)
  starting transfers between devices  24 us (27%)
  Pallas kernels  16.7 us (19%)
  waiting for transfers between devices  12.1 us (14%)
  local copies, waits for them, and re-layouts  5.25 us (6%)
  between operations  0.94 us (1%)
    all_to_all x1, blocking collectives, on_device(): recv_setup = lax.all_to_all(pay_setup, 'net', 0, 0, tiled=True)  28.1 us
    pallas_call x7, Pallas kernels, vmem_call(): pl.pallas_call(kernel, out_shape=outs, in_specs=[pl.BlockSpec(memory_spac...  16.7 us
    all_to_all x1, starting transfers between devices, on_device(): recv_1 = lax.all_to_all(pay_1, 'net', 0, 0, tiled=True)  12.3 us
    all_to_all x1, waiting for transfers between devices, on_device(): recv_1 = lax.all_to_all(pay_1, 'net', 0, 0, tiled=True)  9.36 us
    ppermute x1, starting transfers between devices, on_device(): lax.ppermute(sr[nrow - halo:], 'tm', [(i, i + 1) for i in range(ntm - 1)])  5.11 us
    all_to_all x1, starting transfers between devices, on_device(): recv_0 = lax.all_to_all(pay_0, 'net', 0, 0, tiled=True)  4.68 us
    unnamed x53, local copies, waits for them, and re-layouts  4.32 us
    ppermute x1, waiting for transfers between devices, on_device(): hi = lax.ppermute(sr[:halo], 'tm', [(i + 1, i) for i in range(ntm - 1)])  2.73 us
  transfers between devices with their start and end apart: 4, of which 2 were waited for; matrix products, arithmetic and copies ran while one was open for 0% of the time, Pallas kernels for 9%

profile of v2, /device:TPU:1, one launch (start us, length us, event | category | flops | bytes accessed | tf_op | source)
XLA Modules:
  0.0 87.9 jit_solution(15514826548103728263)
XLA Ops:
  0.6 0.7 convert_bitcast_fusion.steps_ref.refs_14_
  1.3 0.6 copy-done.24
  2.0 0.1 copy.30.peer_ref
  2.1 0.0 copy-start.13
  2.1 0.6 copy-done.14
  2.7 0.0 copy-done.11
  2.7 0.0 copy-done.12
  2.7 0.0 copy-done.13
  2.8 0.8 copy-done
  3.6 0.8 copy-done.2
  4.4 1.1 %shard_map.272 = (f32[64,128]{1,0:T(8,128)S(1)}, f32[128,128]{1,0:T(8,128)S(1)}) custom-call(s32[64,1]{1,0:T(8,128)S(1)} %copy.30.peer_ref, s32[1,64]{1,0:T(1,128)S(1)} %bitcast.73, f32[1,64]{1,0:T(1,128)S(1)} %convert_bitcast_fusion.1.bus_ref, f32[1,64]{1,0:T(1,128)S(1)} %bitcast.76, f32[1,64]{1,0:T(1,128)S(1)} %bitcast.79, f32[1,64]{1,0:T(1,128)S(1)} %bitcast.82, ...), custom_call_target="tpu_custom_call" | custom-call | tf_op jit(solution)/shard_map/pallas_call | solution.py:120
  5.5 28.1 %all_to_all.33 = f32[64,2,128]{2,1,0:T(2,128)S(1)} all-to-all(f32[64,2,128]{2,1,0:T(2,128)S(1)} %bitcast.57), channel_id=1, replica_groups=mesh['net'=64,'tm'=8] {'net'}, dimensions={0} | all-to-all | bytes 131072 | tf_op jit(solution)/shard_map/all_to_all | solution.py:199
  33.6 1.0 %shard_map.273 = (f32[128,128]{1,0:T(8,128)S(1)}, f32[128,128]{1,0:T(8,128)}) custom-call(f32[128,128]{1,0:T(8,128)S(1)} %bitcast.50, f32[48,256]{1,0:T(8,128)S(1)} %bitcast.38, f32[48,256]{1,0:T(8,128)S(1)} %bitcast.45), custom_call_target="tpu_custom_call" | custom-call | tf_op jit(solution)/shard_map/pallas_call | solution.py:120
  34.6 4.7 %all-to-all-start.1 = ((f32[64,2,128]{2,1,0:T(2,128)}), f32[64,2,128]{2,1,0:T(2,128)S(1)}, u32[]{:S(2)}, u32[]{:S(2)}) async-start(f32[64,2,128]{2,1,0:T(2,128)} %bitcast.12), calls=%async_computation.1 | async-start | bytes 131072 | tf_op jit(solution)/shard_map/all_to_all | solution.py:213
  39.3 5.1 %collective-permute-start = (f32[32,32]{1,0:T(8,128)S(1)}, f32[32,32]{1,0:T(8,128)S(1)}, u32[]{:S(2)}, u32[]{:S(2)}) collective-permute-start(f32[32,32]{1,0:T(8,128)S(1)} %bitcast.102), channel_id=1, source_target_pairs={{0,1},{1,2},{2,3},{3,4},{4,5},{5,6},{6,7},{8,9},{9,10},{10,11},{11... | collective-permute-start | bytes 12296 | tf_op jit(solution)/shard_map/ppermute | solution.py:166
  44.5 1.9 %collective-permute-start.1 = (f32[32,32]{1,0:T(8,128)S(1)}, f32[32,32]{1,0:T(8,128)S(1)}, u32[]{:S(2)}, u32[]{:S(2)}) collective-permute-start(f32[32,32]{1,0:T(8,128)S(1)} %bitcast.101), channel_id=1, source_target_pairs={{1,0},{2,1},{3,2},{4,3},{5,4},{6,5},{7,6},{9,8},{10,9},{11,10},{12... | collective-permute-start | bytes 12296 | tf_op jit(solution)/shard_map/ppermute | solution.py:167
  46.4 0.0 copy-start.18
  46.5 0.6 copy-done.23
  47.1 2.7 %collective-permute-done.1.refs_17_ = f32[32,32]{1,0:T(8,128)S(1)} collective-permute-done((f32[32,32]{1,0:T(8,128)S(1)}, f32[32,32]{1,0:T(8,128)S(1)}, u32[]{:S(2)}, u32[]{:S(2)}) %collective-permute-start.1) | collective-permute-done | bytes 4128 | tf_op jit(solution)/shard_map/ppermute | solution.py:167
  49.9 0.6 copy-done.9
  50.5 0.0 copy-done.15
  50.5 0.0 copy-done.16
  50.5 0.0 copy-done.8
  50.5 2.9 %shard_map.274 = (f32[4,48,256]{2,1,0:T(8,128)S(1)}, f32[2,48,256]{2,1,0:T(8,128)S(1)}, f32[8,48,256]{2,1,0:T(8,128)S(1)}, f32[80,32]{1,0:T(8,128)S(1)}, f32[48,32]{1,0:T(8,128)S(1)}) custom-call(f32[48,256]{1,0:T(8,128)S(1)} %bitcast.39, f32[48,256]{1,0:T(8,128)S(1)} %bitcast.46, s32[1,256]{1,0:T(1,128)S(1)} %bitcast.59, s32[1,256]{1,0:T(1,128)S(1)} %bitcast.63, ...), custom_call_target="tpu_custom_call" | custom-call | tf_op jit(solution)/shard_map/pallas_call | solution.py:120
  53.4 1.7 %shard_map.275 = (f32[4,48,256]{2,1,0:T(8,128)S(1)}, f32[8,48,128]{2,1,0:T(8,128)S(1)}) custom-call(f32[128,128]{1,0:T(8,128)S(1)} %get-tuple-element.28.mirror_ref.refs_6_, f32[48,256]{1,0:T(8,128)S(1)} %bitcast.40, f32[48,256]{1,0:T(8,128)S(1)} %bitcast.47), custom_call_target="tpu_custom_call" | custom-call | tf_op jit(solution)/shard_map/pallas_call | solution.py:120
  55.2 2.8 %shard_map.276 = (f32[8,48,64]{2,1,0:T(8,128)S(1)}, f32[4,48,256]{2,1,0:T(8,128)S(1)}, f32[128,384]{1,0:T(8,128)S(1)}) custom-call(f32[48,256]{1,0:T(8,128)S(1)} %bitcast.41, f32[48,256]{1,0:T(8,128)S(1)} %bitcast.42, f32[48,256]{1,0:T(8,128)S(1)} %bitcast.48, f32[48,256]{1,0:T(8,128)S(1)} %bitcast.52, f32[48,256]{1,0:T(8,128)S(1)} %bitcast.54, ...), custom_call_target="tpu_custom_call" | custom-call | tf_op jit(solution)/shard_map/pallas_call | solution.py:120
  58.0 0.8 all_to_all.27
  58.7 12.3 %all-to-all-start.2 = ((f32[64,2,384]{2,1,0:T(2,128)}), f32[64,2,384]{2,1,0:T(2,128)S(1)}, u32[]{:S(2)}, u32[]{:S(2)}) async-start(f32[64,2,384]{2,1,0:T(2,128)} %all_to_all.27), calls=%async_computation.2 | async-start | bytes 393216 | tf_op jit(solution)/shard_map/all_to_all | solution.py:373
  71.1 3.3 %shard_map.277 = (f32[4,48,256]{2,1,0:T(8,128)S(1)}, f32[2,48,256]{2,1,0:T(8,128)S(1)}, f32[48,32]{1,0:T(8,128)}, f32[48,32]{1,0:T(8,128)}) custom-call(f32[4,48,256]{2,1,0:T(8,128)S(1)} %get-tuple-element.33.refs_0_, s32[1,256]{1,0:T(1,128)S(1)} %bitcast.61, s32[1,256]{1,0:T(1,128)S(1)} %bitcast.65, f32[1,256]{1,0:T(1,128)S(1)} %bitcast.86, ...), custom_call_target="tpu_custom_call" | custom-call | tf_op jit(solution)/shard_map/pallas_call | solution.py:120
  74.3 9.4 %all-to-all-done.2 = f32[64,2,384]{2,1,0:T(2,128)S(1)} async-done(((f32[64,2,384]{2,1,0:T(2,128)}), f32[64,2,384]{2,1,0:T(2,128)S(1)}, u32[]{:S(2)}, u32[]{:S(2)}) %all-to-all-start.2) | async-done | bytes 196640 | tf_op jit(solution)/shard_map/all_to_all | solution.py:373
  83.7 0.1 all_to_all.29.refs_5_
  83.8 4.0 %shard_map.278 = (f32[48,256]{1,0:T(8,128)}, f32[48,256]{1,0:T(8,128)}, f32[48,256]{1,0:T(8,128)}) custom-call(f32[4,48,256]{2,1,0:T(8,128)S(1)} %get-tuple-element.33.refs_0_, f32[48,256]{1,0:T(8,128)S(1)} %bitcast.43, f32[48,256]{1,0:T(8,128)S(1)} %bitcast.49, f32[48,256]{1,0:T(8,128)S(1)} %bitcast.53, f32[48,256]{1,0:T(8,128)S(1)} %bitcast.55, ...), custom_call_target="tpu_custom_call" | custom-call | tf_op jit(solution)/shard_map/pallas_call | solution.py:120
  (44 shorter events, 0.1 us)
Async XLA Ops:
  0.6 0.7 copy-start.25
  1.3 0.7 copy-start.24
  2.1 0.7 copy-start.14
  2.1 0.7 copy-start.11
  2.1 0.7 copy-start.12
  2.1 0.7 copy-start.13
  2.8 0.8 copy-start
  3.6 0.8 copy-start.2
  5.4 28.2 %copy-start.1 = (f32[3,16,256]{2,1,0:T(8,128)S(1)}, f32[3,16,256]{2,1,0:T(8,128)}, u32[]{:S(2)}) copy-start(f32[3,16,256]{2,1,0:T(8,128)} %param.25) | copy-start | bytes 147460
  5.4 28.2 %copy-start.3 = (f32[3,16,256]{2,1,0:T(8,128)S(1)}, f32[3,16,256]{2,1,0:T(8,128)}, u32[]{:S(2)}) copy-start(f32[3,16,256]{2,1,0:T(8,128)} %param.26) | copy-start | bytes 147460
  34.6 4.7 %copy-start.6 = (f32[3,16,32]{2,1,0:T(8,128)S(1)}, f32[3,16,32]{2,1,0:T(8,128)}, u32[]{:S(2)}) copy-start(f32[3,16,32]{2,1,0:T(8,128)} %param.29) | copy-start | bytes 18436
  34.6 20.5 %all-to-all-start.1 = ((f32[64,2,128]{2,1,0:T(2,128)}), f32[64,2,128]{2,1,0:T(2,128)S(1)}, u32[]{:S(2)}, u32[]{:S(2)}) async-start(f32[64,2,128]{2,1,0:T(2,128)} %bitcast.12), calls=%async_computation.1 | async-start | bytes 131072 | tf_op jit(solution)/shard_map/all_to_all | solution.py:213
  39.3 7.7 %collective-permute-start = (f32[32,32]{1,0:T(8,128)S(1)}, f32[32,32]{1,0:T(8,128)S(1)}, u32[]{:S(2)}, u32[]{:S(2)}) collective-permute-start(f32[32,32]{1,0:T(8,128)S(1)} %bitcast.102), channel_id=1, source_target_pairs={{0,1},{1,2},{2,3},{3,4},{4,5},{5,6},{6,7},{8,9},{9,10},{10,11},{11... | collective-permute-start | bytes 12296 | tf_op jit(solution)/shard_map/ppermute | solution.py:166
  44.5 5.4 %collective-permute-start.1 = (f32[32,32]{1,0:T(8,128)S(1)}, f32[32,32]{1,0:T(8,128)S(1)}, u32[]{:S(2)}, u32[]{:S(2)}) collective-permute-start(f32[32,32]{1,0:T(8,128)S(1)} %bitcast.101), channel_id=1, source_target_pairs={{1,0},{2,1},{3,2},{4,3},{5,4},{6,5},{7,6},{9,8},{10,9},{11,10},{12... | collective-permute-start | bytes 12296 | tf_op jit(solution)/shard_map/ppermute | solution.py:167
  46.4 0.7 copy-start.23
  46.4 3.4 %copy-start.17 = (f32[256]{0:T(256)S(1)}, f32[256]{0:T(256)}, u32[]{:S(2)}) copy-start(f32[256]{0:T(256)} %param.41) | copy-start | bytes 3076
  46.4 3.4 %copy-start.18 = (f32[32]{0:T(128)S(1)}, f32[32]{0:T(128)}, u32[]{:S(2)}) copy-start(f32[32]{0:T(128)} %param.32) | copy-start | bytes 388
  46.4 3.4 %copy-start.19 = (f32[32]{0:T(128)S(1)}, f32[32]{0:T(128)}, u32[]{:S(2)}) copy-start(f32[32]{0:T(128)} %param.33) | copy-start | bytes 388
  46.4 3.4 %copy-start.20 = (f32[32]{0:T(128)S(1)}, f32[32]{0:T(128)}, u32[]{:S(2)}) copy-start(f32[32]{0:T(128)} %param.34) | copy-start | bytes 388
  46.4 3.4 %copy-start.21 = (f32[32]{0:T(128)S(1)}, f32[32]{0:T(128)}, u32[]{:S(2)}) copy-start(f32[32]{0:T(128)} %param.35) | copy-start | bytes 388
  46.5 3.4 %copy-start.22 = (f32[32]{0:T(128)S(1)}, f32[32]{0:T(128)}, u32[]{:S(2)}) copy-start(f32[32]{0:T(128)} %param.36) | copy-start | bytes 388
  47.1 2.8 %copy-start.7 = (f32[3,16,32]{2,1,0:T(8,128)S(1)}, f32[3,16,32]{2,1,0:T(8,128)}, u32[]{:S(2)}) copy-start(f32[3,16,32]{2,1,0:T(8,128)} %param.30) | copy-start | bytes 18436
  49.8 0.7 copy-start.9
  49.8 0.7 copy-start.15
  49.8 0.7 copy-start.16
  49.8 0.7 copy-start.8
  49.8 0.7 copy-start.10
  53.4 1.7 %copy-start.4 = (f32[3,16,256]{2,1,0:T(8,128)S(1)}, f32[3,16,256]{2,1,0:T(8,128)}, u32[]{:S(2)}) copy-start(f32[3,16,256]{2,1,0:T(8,128)} %param.27) | copy-start | bytes 147460
  53.4 1.7 %copy-start.5 = (f32[3,16,256]{2,1,0:T(8,128)S(1)}, f32[3,16,256]{2,1,0:T(8,128)}, u32[]{:S(2)}) copy-start(f32[3,16,256]{2,1,0:T(8,128)} %param.28) | copy-start | bytes 147460
  58.7 24.9 %all-to-all-start.2 = ((f32[64,2,384]{2,1,0:T(2,128)}), f32[64,2,384]{2,1,0:T(2,128)S(1)}, u32[]{:S(2)}, u32[]{:S(2)}) async-start(f32[64,2,384]{2,1,0:T(2,128)} %all_to_all.27), calls=%async_computation.2 | async-start | bytes 393216 | tf_op jit(solution)/shard_map/all_to_all | solution.py:373

commit v3 on v2

--- a/solution.py
+++ b/solution.py
@@ -34,11 +34,14 @@
     return jnp.concatenate(parts, axis=0)
 
 
-def flows(x, g, b):
-    mf, af, mt, at = x
-    d = af - at
-    c = jnp.cos(d)
-    s = jnp.sin(d)
+def trig(x):
+    d = x[1] - x[3]
+    return (jnp.cos(d), jnp.sin(d))
+
+
+def flows(x, cs, g, b):
+    mf, _, mt, _ = x
+    c, s = cs
     p = mf * mt
     return (
         g * mf * mf - p * (g * c + b * s),
@@ -48,20 +51,17 @@
     )
 
 
-def energy_grad(x, t, ft, g, b, l2):
+def energy_grad(x, cs, f, t, ft, g, b, l2):
     mf, af, mt, at = x
-    d = af - at
-    c = jnp.cos(d)
-    s = jnp.sin(d)
+    c, s = cs
     p = mf * mt
     ka = g * c + b * s
     kb = g * s - b * c
     kc = g * c - b * s
     kd = g * s + b * c
-    f0 = g * mf * mf - p * ka
-    f1 = -b * mf * mf - p * kb
-    f2 = g * mt * mt - p * kc
-    f3 = -b * mt * mt + p * kd
+    if f is None:
+        f = (g * mf * mf - p * ka, -b * mf * mf - p * kb, g * mt * mt - p * kc, -b * mt * mt + p * kd)
+    f0, f1, f2, f3 = f
     ef = jnp.maximum(f0 * f0 + f1 * f1 - l2, 0.0)
     et = jnp.maximum(f2 * f2 + f3 * f3 - l2, 0.0)
     w0 = (f0 - ft[0]) + 2.0 * ef * f0
@@ -74,13 +74,16 @@
     return (g_mf, (af - t[1]) + g_d, g_mt, (at - t[3]) - g_d)
 
 
-def solve(x, t, ft, g, b, l2, steps):
+def solve(x, cs, f, t, ft, g, b, l2, steps):
     for attempt in range(INNER):
-        grad = energy_grad(x, t, ft, g, b, l2)
+        if cs is None:
+            cs = trig(x)
+        grad = energy_grad(x, cs, f, t, ft, g, b, l2)
         x = tuple(
             jnp.where(attempt < steps, xi - jnp.clip(STEP_SIZE * gi, -RADIUS, RADIUS), xi)
             for xi, gi in zip(x, grad)
         )
+        cs, f = None, None
     return x
 
 
@@ -90,26 +93,40 @@
     prices = (near[2], near[3], far[2], far[3])
     if carry is None:
         copies = ends
-        flow_prev = flows(copies, g, b)
+        cs = trig(copies)
+        flow_prev = flows(copies, cs, g, b)
         volt = tuple(jnp.zeros_like(e) for e in ends)
         target = ends
         flow_target = flow_prev
         dual_flow = volt
     else:
-        copies, flow_prev = carry
+        copies, flow_prev, cs = carry
         volt = tuple(c - e for c, e in zip(copies, ends))
         target = tuple(e - v for e, v in zip(ends, volt))
         flow_target = tuple(f + 2.0 * q for f, q in zip(flow_prev, prices))
         dual_flow = tuple(-q for q in prices)
-    copies = solve(copies, target, flow_target, g, b, lim * lim, steps)
-    flow_prev = flows(copies, g, b)
+    copies = solve(copies, cs, flow_prev, target, flow_target, g, b, lim * lim, steps)
+    cs = trig(copies)
+    flow_prev = flows(copies, cs, g, b)
     side_from = rows(
         copies[0] + volt[0], copies[1] + volt[1], flow_prev[0] + dual_flow[0], flow_prev[1] + dual_flow[1]
     )
     side_to = rows(
         copies[2] + volt[2], copies[3] + volt[3], flow_prev[2] + dual_flow[2], flow_prev[3] + dual_flow[3]
     )
-    return (copies, flow_prev), side_from, side_to
+    return (copies, flow_prev, cs), side_from, side_to
+
+
+def store_carry(ref, carry):
+    for i in range(4):
+        ref[i] = carry[0][i]
+        ref[4 + i] = carry[1][i]
+    ref[8] = carry[2][0]
+    ref[9] = carry[2][1]
+
+
+def load_carry(ref):
+    return (tuple(ref[i] for i in range(4)), tuple(ref[4 + i] for i in range(4)), (ref[8], ref[9]))
 
 
 def split4(a, n):
@@ -227,7 +244,7 @@
              ci_ref, g0_ref, gq0_ref,
              tot_out, sup_out, gr_out, gq_out) = refs
             state = tuple(st_ref[i] for i in range(4))
-            carry_in = (tuple(ci_ref[i] for i in range(4)), tuple(ci_ref[4 + i] for i in range(4)))
+            carry_in = load_carry(ci_ref)
         inc_from = onehot(bf_ref[...], buses)
         inc_to = onehot(bt_ref[...], buses)
         inc_gen = onehot(gb_ref[...], buses)
@@ -251,9 +268,7 @@
             gen_real = g0[scen:scen + nrow]
             gen_react = jnp.clip(sq_ref[...], -capq, capq)
             supply = mm_t(rows(gen_real, gen_react), inc_gen)
-            for i in range(4):
-                ci_out[i] = carry_i[0][i]
-                ci_out[4 + i] = carry_i[1][i]
+            store_carry(ci_out, carry_i)
             g0_out[...] = g0
             gq0_out[...] = gen_react
         else:
@@ -273,9 +288,12 @@
         sup_out[0] = supply[0:nrow]
         sup_out[1] = supply[nrow:]
 
-    def mirror0_kernel(mirror_ref, wm_ref, wa_ref, tot_out, cm_out):
+    def mirror0_kernel(mirror_ref, wm_ref, wa_ref, bf_ref, bt_ref, cn_ref, gb_ref, tot_out, cm_out, dg_out):
         mirror = mirror_ref[...]
         inc_recv = onehot(mirror[0:1].astype(jnp.int32) - 1, buses)
+        degree = (col_sum(onehot(bf_ref[...], buses)) + col_sum(onehot(bt_ref[...], buses))
+                  + col_sum(onehot(cn_ref[...], buses)) + col_sum(inc_recv))
+        dg_out[...] = rows(degree, col_sum(onehot(gb_ref[...], buses)), jnp.zeros((6, buses), F32))
         zm = jnp.zeros((nrow, slots), F32)
         zero_b = jnp.zeros((nrow, buses), F32)
         stack = rows(wm_ref[...], wa_ref[...], zero_b, zero_b)
@@ -286,22 +304,20 @@
         totals = mm_t(tmr, inc_recv)
         for i in range(4):
             tot_out[i] = totals[i * nrow:(i + 1) * nrow]
-            cm_out[i] = carry_m[0][i]
-            cm_out[4 + i] = carry_m[1][i]
+        store_carry(cm_out, carry_m)
 
     def cut_part(first, refs):
         (st_ref, wm_ref, wa_ref, lr_ref, lq_ref, recv_ref, mirror_ref, slot_ref,
-         bf_ref, bt_ref, cn_ref, cc_ref, cs_ref, cl_ref, cstep_ref, gb_ref,
-         tin_ref, sup_ref, tm_ref) = refs[:19]
-        rest = refs[19:]
+         dg_ref, cn_ref, cc_ref, cs_ref, cl_ref, cstep_ref,
+         tin_ref, sup_ref, tm_ref) = refs[:17]
+        rest = refs[17:]
         wmv, wav = wm_ref[...], wa_ref[...]
         slot_t = slot_ref[...]
         mirror = mirror_ref[...]
         inc_near = onehot(cn_ref[...], buses)
         inc_recv = onehot(mirror[0:1].astype(jnp.int32) - 1, buses)
-        degree = (col_sum(onehot(bf_ref[...], buses)) + col_sum(onehot(bt_ref[...], buses)) + col_sum(inc_near)
-                  + col_sum(inc_recv))
-        gen_count = col_sum(onehot(gb_ref[...], buses))
+        degree = dg_ref[0:1]
+        gen_count = dg_ref[1:2]
         prm_cut = (cc_ref[...], cs_ref[...], cl_ref[...], cstep_ref[...])
         if first:
             (cc_out, st_out, pay_out) = rest
@@ -324,8 +340,8 @@
             stack = rows(*state)
             pick_near = split4(mm(stack, inc_near), nrow)
             pick_recv = split4(mm(stack, inc_recv), nrow)
-            carry_c_in = (tuple(cc_in_ref[i] for i in range(4)), tuple(cc_in_ref[4 + i] for i in range(4)))
-            carry_m_in = (tuple(cm_ref[i] for i in range(4)), tuple(cm_ref[4 + i] for i in range(4)))
+            carry_c_in = load_carry(cc_in_ref)
+            carry_m_in = load_carry(cm_ref)
             _, fc, _ = advance(carry_c_in, pick_near, far_cross, prm_cut)
             prm_mir = (mirror[1:2], mirror[2:3], mirror[3:4], mirror[4:5])
             _, _, tmr = advance(carry_m_in, near_mirror, pick_recv, prm_mir)
@@ -336,9 +352,7 @@
         pr = BALANCE_WEIGHT * (sup_ref[0] - totals[2] - lr_ref[...]) / weight
         pq = BALANCE_WEIGHT * (sup_ref[1] - totals[3] - lq_ref[...]) / weight
         if first:
-            for i in range(4):
-                cc_out[i] = carry_c[0][i]
-                cc_out[4 + i] = carry_c[1][i]
+            store_carry(cc_out, carry_c)
             st_out[0] = mag
             st_out[1] = ang
             st_out[2] = pr
@@ -357,18 +371,19 @@
     gen_all = (*gen_rows, period_ext)
     tin0, sup0, ci1, g0, gq0 = vmem_call(
         lambda *refs: local_part(True, refs),
-        (tot_shape, sds((2, nrow, buses), F32), sds((8, nrow, buses), F32), sds((window, gens), F32),
+        (tot_shape, sds((2, nrow, buses), F32), sds((10, nrow, buses), F32), sds((window, gens), F32),
          sds((nrow, gens), F32)),
         wm, wa, *br_all, *gen_all, lo, sr, hi, sq,
     )
-    tm0, cm1 = vmem_call(
-        mirror0_kernel, (tot_shape, sds((8, nrow, slots), F32)), mirror_t, wm, wa,
-    )
-    cut_in = (*cut_rows, gen_rows[0])
+    tm0, cm1, dg = vmem_call(
+        mirror0_kernel, (tot_shape, sds((10, nrow, slots), F32), sds((8, buses), F32)), mirror_t, wm, wa,
+        br_rows[0], br_rows[1], cut_rows[0], gen_rows[0],
+    )
+    cut_in = cut_rows
     cc1, st1, pay_1 = vmem_call(
         lambda *refs: cut_part(True, refs),
-        (sds((8, nrow, cuts), F32), tot_shape, sds((slots, 8 * nrow), F32)),
-        wm, wm, wa, lr, lq, recv_0, mirror_t, slot_t, br_rows[0], br_rows[1], *cut_in, tin0, sup0, tm0,
+        (sds((10, nrow, cuts), F32), tot_shape, sds((slots, 8 * nrow), F32)),
+        wm, wm, wa, lr, lq, recv_0, mirror_t, slot_t, dg, *cut_in, tin0, sup0, tm0,
     )
     recv_1 = lax.all_to_all(pay_1, "net", 0, 0, tiled=True)
     tin1, sup1, gr, gq = vmem_call(
@@ -379,7 +394,7 @@
     mag, ang, pr = vmem_call(
         lambda *refs: cut_part(False, refs),
         (sds((nrow, buses), F32), sds((nrow, buses), F32), sds((nrow, buses), F32)),
-        st1, wm, wa, lr, lq, recv_1, mirror_t, slot_t, br_rows[0], br_rows[1], *cut_in, tin1, sup1, tin1,
+        st1, wm, wa, lr, lq, recv_1, mirror_t, slot_t, dg, *cut_in, tin1, sup1, tin1,
         cc1, cm1,
     )
     shape_b = (periods, scen, buses)

time: 88.4 us -> 87.6 us (level)
  Pallas kernels: 16.7 us -> 15.7 us
    pallas_call x7, Pallas kernels: 16.7 us -> 15.7 us  [vmem_call(): pl.pallas_call(kernel, out_shape=outs, in_specs=[pl.BlockSpec(memory_spac...]
where the time goes in v3:
time: 87.6 us; the launch traced here: 87 us
  blocking collectives  28.1 us (32%)
  starting transfers between devices  24 us (27%)
  Pallas kernels  15.7 us (18%)
  waiting for transfers between devices  12.2 us (14%)
  local copies, waits for them, and re-layouts  5.25 us (6%)
  between operations  0.95 us (1%)
    all_to_all x1, blocking collectives, on_device(): recv_setup = lax.all_to_all(pay_setup, 'net', 0, 0, tiled=True)  28.1 us
    pallas_call x7, Pallas kernels, vmem_call(): pl.pallas_call(kernel, out_shape=outs, in_specs=[pl.BlockSpec(memory_spac...  15.7 us
    all_to_all x1, starting transfers between devices, on_device(): recv_1 = lax.all_to_all(pay_1, 'net', 0, 0, tiled=True)  12.3 us
    all_to_all x1, waiting for transfers between devices, on_device(): recv_1 = lax.all_to_all(pay_1, 'net', 0, 0, tiled=True)  9.48 us
    ppermute x1, starting transfers between devices, on_device(): lax.ppermute(sr[nrow - halo:], 'tm', [(i, i + 1) for i in range(ntm - 1)])  5.11 us
    all_to_all x1, starting transfers between devices, on_device(): recv_0 = lax.all_to_all(pay_0, 'net', 0, 0, tiled=True)  4.68 us
    unnamed x53, local copies, waits for them, and re-layouts  4.32 us
    ppermute x1, waiting for transfers between devices, on_device(): hi = lax.ppermute(sr[:halo], 'tm', [(i + 1, i) for i in range(ntm - 1)])  2.73 us
  transfers between devices with their start and end apart: 4, of which 2 were waited for; matrix products, arithmetic and copies ran while one was open for 0% of the time, Pallas kernels for 9%

profile of v3, /device:TPU:1, one launch (start us, length us, event | category | flops | bytes accessed | tf_op | source)
XLA Modules:
  0.0 87.0 jit_solution(7959152708020818010)
XLA Ops:
  0.6 0.7 convert_bitcast_fusion.steps_ref.refs_13_
  1.3 0.6 copy-done.24
  2.0 0.1 copy.30.peer_ref
  2.1 0.0 copy-start.13
  2.1 0.6 copy-done.14
  2.7 0.0 copy-done.10
  2.7 0.0 copy-done.12
  2.7 0.0 copy-done.13
  2.8 0.8 copy-done
  3.6 0.8 copy-done.2
  4.4 1.1 %shard_map.272 = (f32[64,128]{1,0:T(8,128)S(1)}, f32[128,128]{1,0:T(8,128)S(1)}) custom-call(s32[64,1]{1,0:T(8,128)S(1)} %copy.30.peer_ref, s32[1,64]{1,0:T(1,128)S(1)} %bitcast.67, f32[1,64]{1,0:T(1,128)S(1)} %convert_bitcast_fusion.1.bus_ref, f32[1,64]{1,0:T(1,128)S(1)} %bitcast.74, f32[1,64]{1,0:T(1,128)S(1)} %bitcast.77, f32[1,64]{1,0:T(1,128)S(1)} %bitcast.80, ...), custom_call_target="tpu_custom_call" | custom-call | tf_op jit(solution)/shard_map/pallas_call | solution.py:137
  5.5 28.1 %all_to_all.33 = f32[64,2,128]{2,1,0:T(2,128)S(1)} all-to-all(f32[64,2,128]{2,1,0:T(2,128)S(1)} %bitcast.57), channel_id=1, replica_groups=mesh['net'=64,'tm'=8] {'net'}, dimensions={0} | all-to-all | bytes 131072 | tf_op jit(solution)/shard_map/all_to_all | solution.py:216
  33.6 1.0 %shard_map.273 = (f32[128,128]{1,0:T(8,128)S(1)}, f32[128,128]{1,0:T(8,128)}) custom-call(f32[128,128]{1,0:T(8,128)S(1)} %bitcast.51, f32[48,256]{1,0:T(8,128)S(1)} %bitcast.38, f32[48,256]{1,0:T(8,128)S(1)} %bitcast.45), custom_call_target="tpu_custom_call" | custom-call | tf_op jit(solution)/shard_map/pallas_call | solution.py:137
  34.6 4.7 %all-to-all-start.1 = ((f32[64,2,128]{2,1,0:T(2,128)}), f32[64,2,128]{2,1,0:T(2,128)S(1)}, u32[]{:S(2)}, u32[]{:S(2)}) async-start(f32[64,2,128]{2,1,0:T(2,128)} %bitcast.12), calls=%async_computation.1 | async-start | bytes 131072 | tf_op jit(solution)/shard_map/all_to_all | solution.py:230
  39.3 5.1 %collective-permute-start = (f32[32,32]{1,0:T(8,128)S(1)}, f32[32,32]{1,0:T(8,128)S(1)}, u32[]{:S(2)}, u32[]{:S(2)}) collective-permute-start(f32[32,32]{1,0:T(8,128)S(1)} %bitcast.100), channel_id=1, source_target_pairs={{0,1},{1,2},{2,3},{3,4},{4,5},{5,6},{6,7},{8,9},{9,10},{10,11},{11... | collective-permute-start | bytes 12296 | tf_op jit(solution)/shard_map/ppermute | solution.py:183
  44.5 1.9 %collective-permute-start.1 = (f32[32,32]{1,0:T(8,128)S(1)}, f32[32,32]{1,0:T(8,128)S(1)}, u32[]{:S(2)}, u32[]{:S(2)}) collective-permute-start(f32[32,32]{1,0:T(8,128)S(1)} %bitcast.99), channel_id=1, source_target_pairs={{1,0},{2,1},{3,2},{4,3},{5,4},{6,5},{7,6},{9,8},{10,9},{11,10},{12... | collective-permute-start | bytes 12296 | tf_op jit(solution)/shard_map/ppermute | solution.py:184
  46.4 0.0 copy-start.18
  46.5 0.6 copy-done.23
  47.1 2.7 %collective-permute-done.1.refs_17_ = f32[32,32]{1,0:T(8,128)S(1)} collective-permute-done((f32[32,32]{1,0:T(8,128)S(1)}, f32[32,32]{1,0:T(8,128)S(1)}, u32[]{:S(2)}, u32[]{:S(2)}) %collective-permute-start.1) | collective-permute-done | bytes 4128 | tf_op jit(solution)/shard_map/ppermute | solution.py:184
  49.9 0.6 copy-done.9
  50.5 0.0 copy-done.15
  50.5 0.0 copy-done.16
  50.5 0.0 copy-done.8
  50.5 2.9 %shard_map.275 = (f32[4,48,256]{2,1,0:T(8,128)S(1)}, f32[2,48,256]{2,1,0:T(8,128)S(1)}, f32[10,48,256]{2,1,0:T(8,128)S(1)}, f32[80,32]{1,0:T(8,128)S(1)}, f32[48,32]{1,0:T(8,128)S(1)}) custom-call(f32[48,256]{1,0:T(8,128)S(1)} %bitcast.39, f32[48,256]{1,0:T(8,128)S(1)} %bitcast.46, s32[1,256]{1,0:T(1,128)S(1)} %bitcast.59, s32[1,256]{1,0:T(1,128)S(1)} %bitcast.62, ...), custom_call_target="tpu_custom_call" | custom-call | tf_op jit(solution)/shard_map/pallas_call | solution.py:137
  53.5 2.1 %shard_map.274 = (f32[4,48,256]{2,1,0:T(8,128)S(1)}, f32[10,48,128]{2,1,0:T(8,128)S(1)}, f32[8,256]{1,0:T(8,128)S(1)}) custom-call(f32[128,128]{1,0:T(8,128)S(1)} %get-tuple-element.29.mirror_ref.refs_6_, f32[48,256]{1,0:T(8,128)S(1)} %bitcast.40, f32[48,256]{1,0:T(8,128)S(1)} %bitcast.47, s32[1,256]{1,0:T(1,128)S(1)} %bitcast.60, s32[1,256]{1,0:T(1,128)S(1)} %bitcast.63, ...), custom_call_target="tpu_custom_call" | custom-call | tf_op jit(solution)/shard_map/pallas_call | solution.py:137
  55.6 2.1 %shard_map.276 = (f32[10,48,64]{2,1,0:T(8,128)S(1)}, f32[4,48,256]{2,1,0:T(8,128)S(1)}, f32[128,384]{1,0:T(8,128)S(1)}) custom-call(f32[48,256]{1,0:T(8,128)S(1)} %bitcast.41, f32[48,256]{1,0:T(8,128)S(1)} %bitcast.42, f32[48,256]{1,0:T(8,128)S(1)} %bitcast.48, f32[48,256]{1,0:T(8,128)S(1)} %bitcast.52, f32[48,256]{1,0:T(8,128)S(1)} %bitcast.54, ...), custom_call_target="tpu_custom_call" | custom-call | tf_op jit(solution)/shard_map/pallas_call | solution.py:137
  57.7 0.8 all_to_all.27
  58.5 12.3 %all-to-all-start.2 = ((f32[64,2,384]{2,1,0:T(2,128)}), f32[64,2,384]{2,1,0:T(2,128)S(1)}, u32[]{:S(2)}, u32[]{:S(2)}) async-start(f32[64,2,384]{2,1,0:T(2,128)} %all_to_all.27), calls=%async_computation.2 | async-start | bytes 393216 | tf_op jit(solution)/shard_map/all_to_all | solution.py:388
  70.8 3.1 %shard_map.277 = (f32[4,48,256]{2,1,0:T(8,128)S(1)}, f32[2,48,256]{2,1,0:T(8,128)S(1)}, f32[48,32]{1,0:T(8,128)}, f32[48,32]{1,0:T(8,128)}) custom-call(f32[4,48,256]{2,1,0:T(8,128)S(1)} %get-tuple-element.35.refs_0_, s32[1,256]{1,0:T(1,128)S(1)} %bitcast.61, s32[1,256]{1,0:T(1,128)S(1)} %bitcast.64, f32[1,256]{1,0:T(1,128)S(1)} %bitcast.84, ...), custom_call_target="tpu_custom_call" | custom-call | tf_op jit(solution)/shard_map/pallas_call | solution.py:137
  73.9 9.5 %all-to-all-done.2 = f32[64,2,384]{2,1,0:T(2,128)S(1)} async-done(((f32[64,2,384]{2,1,0:T(2,128)}), f32[64,2,384]{2,1,0:T(2,128)S(1)}, u32[]{:S(2)}, u32[]{:S(2)}) %all-to-all-start.2) | async-done | bytes 196640 | tf_op jit(solution)/shard_map/all_to_all | solution.py:388
  83.4 0.1 all_to_all.29.refs_5_
  83.5 3.4 %shard_map.278 = (f32[48,256]{1,0:T(8,128)}, f32[48,256]{1,0:T(8,128)}, f32[48,256]{1,0:T(8,128)}) custom-call(f32[4,48,256]{2,1,0:T(8,128)S(1)} %get-tuple-element.35.refs_0_, f32[48,256]{1,0:T(8,128)S(1)} %bitcast.43, f32[48,256]{1,0:T(8,128)S(1)} %bitcast.49, f32[48,256]{1,0:T(8,128)S(1)} %bitcast.53, f32[48,256]{1,0:T(8,128)S(1)} %bitcast.55, ...), custom_call_target="tpu_custom_call" | custom-call | tf_op jit(solution)/shard_map/pallas_call | solution.py:137
  (44 shorter events, 0.1 us)
Async XLA Ops:
  0.6 0.7 copy-start.25
  1.3 0.7 copy-start.24
  2.1 0.7 copy-start.14
  2.1 0.7 copy-start.10
  2.1 0.7 copy-start.12
  2.1 0.7 copy-start.13
  2.8 0.8 copy-start
  3.6 0.8 copy-start.2
  5.4 28.2 %copy-start.1 = (f32[3,16,256]{2,1,0:T(8,128)S(1)}, f32[3,16,256]{2,1,0:T(8,128)}, u32[]{:S(2)}) copy-start(f32[3,16,256]{2,1,0:T(8,128)} %param.25) | copy-start | bytes 147460
  5.4 28.2 %copy-start.3 = (f32[3,16,256]{2,1,0:T(8,128)S(1)}, f32[3,16,256]{2,1,0:T(8,128)}, u32[]{:S(2)}) copy-start(f32[3,16,256]{2,1,0:T(8,128)} %param.26) | copy-start | bytes 147460
  34.6 4.7 %copy-start.6 = (f32[3,16,32]{2,1,0:T(8,128)S(1)}, f32[3,16,32]{2,1,0:T(8,128)}, u32[]{:S(2)}) copy-start(f32[3,16,32]{2,1,0:T(8,128)} %param.29) | copy-start | bytes 18436
  34.6 20.9 %all-to-all-start.1 = ((f32[64,2,128]{2,1,0:T(2,128)}), f32[64,2,128]{2,1,0:T(2,128)S(1)}, u32[]{:S(2)}, u32[]{:S(2)}) async-start(f32[64,2,128]{2,1,0:T(2,128)} %bitcast.12), calls=%async_computation.1 | async-start | bytes 131072 | tf_op jit(solution)/shard_map/all_to_all | solution.py:230
  39.3 7.7 %collective-permute-start = (f32[32,32]{1,0:T(8,128)S(1)}, f32[32,32]{1,0:T(8,128)S(1)}, u32[]{:S(2)}, u32[]{:S(2)}) collective-permute-start(f32[32,32]{1,0:T(8,128)S(1)} %bitcast.100), channel_id=1, source_target_pairs={{0,1},{1,2},{2,3},{3,4},{4,5},{5,6},{6,7},{8,9},{9,10},{10,11},{11... | collective-permute-start | bytes 12296 | tf_op jit(solution)/shard_map/ppermute | solution.py:183
  44.5 5.4 %collective-permute-start.1 = (f32[32,32]{1,0:T(8,128)S(1)}, f32[32,32]{1,0:T(8,128)S(1)}, u32[]{:S(2)}, u32[]{:S(2)}) collective-permute-start(f32[32,32]{1,0:T(8,128)S(1)} %bitcast.99), channel_id=1, source_target_pairs={{1,0},{2,1},{3,2},{4,3},{5,4},{6,5},{7,6},{9,8},{10,9},{11,10},{12... | collective-permute-start | bytes 12296 | tf_op jit(solution)/shard_map/ppermute | solution.py:184
  46.4 0.7 copy-start.23
  46.4 3.4 %copy-start.17 = (f32[256]{0:T(256)S(1)}, f32[256]{0:T(256)}, u32[]{:S(2)}) copy-start(f32[256]{0:T(256)} %param.41) | copy-start | bytes 3076
  46.4 3.4 %copy-start.18 = (f32[32]{0:T(128)S(1)}, f32[32]{0:T(128)}, u32[]{:S(2)}) copy-start(f32[32]{0:T(128)} %param.32) | copy-start | bytes 388
  46.4 3.4 %copy-start.19 = (f32[32]{0:T(128)S(1)}, f32[32]{0:T(128)}, u32[]{:S(2)}) copy-start(f32[32]{0:T(128)} %param.33) | copy-start | bytes 388
  46.4 3.4 %copy-start.20 = (f32[32]{0:T(128)S(1)}, f32[32]{0:T(128)}, u32[]{:S(2)}) copy-start(f32[32]{0:T(128)} %param.34) | copy-start | bytes 388
  46.4 3.4 %copy-start.21 = (f32[32]{0:T(128)S(1)}, f32[32]{0:T(128)}, u32[]{:S(2)}) copy-start(f32[32]{0:T(128)} %param.35) | copy-start | bytes 388
  46.5 3.4 %copy-start.22 = (f32[32]{0:T(128)S(1)}, f32[32]{0:T(128)}, u32[]{:S(2)}) copy-start(f32[32]{0:T(128)} %param.36) | copy-start | bytes 388
  47.1 2.8 %copy-start.7 = (f32[3,16,32]{2,1,0:T(8,128)S(1)}, f32[3,16,32]{2,1,0:T(8,128)}, u32[]{:S(2)}) copy-start(f32[3,16,32]{2,1,0:T(8,128)} %param.30) | copy-start | bytes 18436
  49.8 0.7 copy-start.9
  49.8 0.7 copy-start.15
  49.8 0.7 copy-start.16
  49.8 0.7 copy-start.8
  49.8 0.7 copy-start.11
  53.4 2.1 %copy-start.4 = (f32[3,16,256]{2,1,0:T(8,128)S(1)}, f32[3,16,256]{2,1,0:T(8,128)}, u32[]{:S(2)}) copy-start(f32[3,16,256]{2,1,0:T(8,128)} %param.27) | copy-start | bytes 147460
  53.4 2.1 %copy-start.5 = (f32[3,16,256]{2,1,0:T(8,128)S(1)}, f32[3,16,256]{2,1,0:T(8,128)}, u32[]{:S(2)}) copy-start(f32[3,16,256]{2,1,0:T(8,128)} %param.28) | copy-start | bytes 147460
  58.5 24.9 %all-to-all-start.2 = ((f32[64,2,384]{2,1,0:T(2,128)}), f32[64,2,384]{2,1,0:T(2,128)S(1)}, u32[]{:S(2)}, u32[]{:S(2)}) async-start(f32[64,2,384]{2,1,0:T(2,128)} %all_to_all.27), calls=%async_computation.2 | async-start | bytes 393216 | tf_op jit(solution)/shard_map/all_to_all | solution.py:388

commit v4 on v3

--- a/solution.py
+++ b/solution.py
@@ -193,14 +193,29 @@
     cut_bus_row = row(cut_bus.astype(F32))
     nvals0 = 128
 
-    def prep_kernel(peer_ref, near_ref, bus_ref, cond_ref, susc_ref, lim_ref, steps_ref, wm_ref, wa_ref,
-                    slot_out, pay_out):
-        slot_t = slot_table(peer_ref[...], cap, slots)
+    def prep_kernel(peer_hbm, near_hbm, bus_hbm, cond_hbm, susc_hbm, lim_hbm, steps_hbm, wm_hbm, wa_hbm,
+                    slot_out, pay_out,
+                    peer_ref, near_ref, bus_ref, cond_ref, susc_ref, lim_ref, steps_ref, wm_ref, wa_ref, sems):
+        pairs = ((peer_hbm, peer_ref), (near_hbm, near_ref), (bus_hbm, bus_ref), (cond_hbm, cond_ref),
+                 (susc_hbm, susc_ref), (lim_hbm, lim_ref), (steps_hbm, steps_ref), (wm_hbm, wm_ref),
+                 (wa_hbm, wa_ref))
+        copies = [pltpu.make_async_copy(src, dst, sems.at[i]) for i, (src, dst) in enumerate(pairs)]
+        for cp in copies:
+            cp.start()
+        for cp in copies:
+            cp.wait()
+        peer = peer_ref[...]
+        mine_t = (lax.broadcasted_iota(jnp.int32, (parts, cuts), 0) == peer).astype(F32)
+        same = mm(mine_t.T, mine_t)
+        earlier = lax.broadcasted_iota(jnp.int32, (cuts, cuts), 0) < lax.broadcasted_iota(jnp.int32, (cuts, cuts), 1)
+        rank = jnp.sum(jnp.where(earlier, same, 0.0), axis=0, keepdims=True)
+        position = peer.astype(F32) * cap + rank
+        slot_t = (lax.broadcasted_iota(jnp.int32, (slots, cuts), 0).astype(F32) == position).astype(F32).T
         slot_out[...] = slot_t
         inc_near = onehot(near_ref[...], buses)
         by_slot = mm(inc_near, slot_t)
-        prm = rows(bus_ref[...] + 1.0, cond_ref[...], susc_ref[...], lim_ref[...], steps_ref[...],
-                   jnp.zeros((3, cuts), F32))
+        prm = rows(bus_ref[...].astype(F32) + 1.0, cond_ref[...], susc_ref[...], lim_ref[...],
+                   steps_ref[...].astype(F32), jnp.zeros((3, cuts), F32))
         vals = rows(
             mm(prm, slot_t),
             mm(rows(wm_ref[...], wa_ref[...]), by_slot),
@@ -208,11 +223,15 @@
         )
         pay_out[...] = vals.T
 
-    slot_t, pay_setup = vmem_call(
+    prep_args = (row(cut_peer), cut_rows[0], row(cut_bus), cut_rows[1], cut_rows[2], cut_rows[3], row(cut_steps),
+                 wm, wa)
+    slot_t, pay_setup = pl.pallas_call(
         prep_kernel,
-        (jax.ShapeDtypeStruct((cuts, slots), F32), jax.ShapeDtypeStruct((slots, nvals0), F32)),
-        cut_peer, cut_rows[0], cut_bus_row, cut_rows[1], cut_rows[2], cut_rows[3], cut_rows[4], wm, wa,
-    )
+        out_shape=(jax.ShapeDtypeStruct((cuts, slots), F32), jax.ShapeDtypeStruct((slots, nvals0), F32)),
+        in_specs=[pl.BlockSpec(memory_space=pl.ANY)] * len(prep_args),
+        out_specs=(pl.BlockSpec(memory_space=pltpu.VMEM), pl.BlockSpec(memory_space=pltpu.VMEM)),
+        scratch_shapes=[pltpu.VMEM(a.shape, a.dtype) for a in prep_args] + [pltpu.SemaphoreType.DMA((len(prep_args),))],
+    )(*prep_args)
     recv_setup = lax.all_to_all(pay_setup, "net", 0, 0, tiled=True)
 
     def mid_kernel(recv_ref, wm_ref, wa_ref, mirror_out, pay_out):

time: 87.6 us -> 80.5 us (0.919)
  blocking collectives: 28.1 us -> 0 us
  starting transfers between devices: 24 us -> 38.5 us
  waiting for transfers between devices: 12.2 us -> 19.1 us
  local copies, waits for them, and re-layouts: 5.25 us -> 3.52 us
  Pallas kernels: 15.7 us -> 17.3 us
    all_to_all x1 -> x0, blocking collectives: 28.1 us -> none  [on_device(): recv_setup = lax.all_to_all(pay_setup, 'net', 0, 0, tiled=True)]
    all_to_all x0 -> x1, starting transfers between devices: none -> 17.3 us  [on_device(): recv_setup = lax.all_to_all(pay_setup, 'net', 0, 0, tiled=True)]
    all_to_all x0 -> x1, waiting for transfers between devices: none -> 5.15 us  [on_device(): recv_setup = lax.all_to_all(pay_setup, 'net', 0, 0, tiled=True)]
    all_to_all x1, waiting for transfers between devices: 0.01 us -> 4.43 us  [on_device(): recv_0 = lax.all_to_all(pay_0, 'net', 0, 0, tiled=True)]
    all_to_all x1, starting transfers between devices: 12.3 us -> 7.9 us  [on_device(): recv_1 = lax.all_to_all(pay_1, 'net', 0, 0, tiled=True)]
    all_to_all x1, starting transfers between devices: 4.68 us -> 7.43 us  [on_device(): recv_0 = lax.all_to_all(pay_0, 'net', 0, 0, tiled=True)]
    ppermute x1, waiting for transfers between devices: 2.73 us -> 0.01 us  [on_device(): hi = lax.ppermute(sr[:halo], 'tm', [(i + 1, i) for i in range(ntm - 1)])]
    pallas_call x0 -> x1, Pallas kernels: none -> 2.64 us  [on_device(): pl.pallas_call(prep_kernel, out_shape=(jax.ShapeDtypeStruct((cuts, slots)...]
  transfers between devices with their start and end apart: 4 -> 5, of which waited for: 2 -> 3; matrix products, arithmetic and copies ran while one was open for 0% -> 0% of each run, Pallas kernels for 9% -> 12%
where the time goes in v4:
time: 80.5 us; the launch traced here: 79.5 us
  starting transfers between devices  38.5 us (48%)
  waiting for transfers between devices  19.1 us (24%)
  Pallas kernels  17.3 us (21%)
  local copies, waits for them, and re-layouts  3.52 us (4%)
  between operations  0.97 us (1%)
    all_to_all x1, starting transfers between devices, on_device(): recv_setup = lax.all_to_all(pay_setup, 'net', 0, 0, tiled=True)  17.3 us
    pallas_call x6, Pallas kernels, vmem_call(): pl.pallas_call(kernel, out_shape=outs, in_specs=[pl.BlockSpec(memory_spac...  14.7 us
    all_to_all x1, waiting for transfers between devices, on_device(): recv_1 = lax.all_to_all(pay_1, 'net', 0, 0, tiled=True)  9.57 us
    all_to_all x1, starting transfers between devices, on_device(): recv_1 = lax.all_to_all(pay_1, 'net', 0, 0, tiled=True)  7.9 us
    all_to_all x1, starting transfers between devices, on_device(): recv_0 = lax.all_to_all(pay_0, 'net', 0, 0, tiled=True)  7.43 us
    all_to_all x1, waiting for transfers between devices, on_device(): recv_setup = lax.all_to_all(pay_setup, 'net', 0, 0, tiled=True)  5.15 us
    all_to_all x1, waiting for transfers between devices, on_device(): recv_0 = lax.all_to_all(pay_0, 'net', 0, 0, tiled=True)  4.43 us
    ppermute x1, starting transfers between devices, on_device(): lax.ppermute(sr[nrow - halo:], 'tm', [(i, i + 1) for i in range(ntm - 1)])  3.96 us
  transfers between devices with their start and end apart: 5, of which 3 were waited for; matrix products, arithmetic and copies ran while one was open for 0% of the time, Pallas kernels for 12%

profile of v4, /device:TPU:1, one launch (start us, length us, event | category | flops | bytes accessed | tf_op | source)
XLA Modules:
  0.0 79.5 jit_solution(17831002173397571009)
XLA Ops:
  0.6 2.6 %shard_map.272 = (f32[64,128]{1,0:T(8,128)}, f32[128,128]{1,0:T(8,128)}) custom-call(s32[1,64]{1,0:T(1,128)} %bitcast.102, s32[1,64]{1,0:T(1,128)} %bitcast.67, s32[1,64]{1,0:T(1,128)} %bitcast.103, f32[1,64]{1,0:T(1,128)} %bitcast.74, f32[1,64]{1,0:T(1,128)} %bitcast.77, f32[1,64]{1,0:T(1,128)} %bitcast.80, s32[1,64]{1,0:T(1,128)} %bitcast.104, ...), custom_call_target="tpu_custom_call" | custom-call | tf_op jit(solution)/shard_map/pallas_call | solution.py:228
  3.3 0.0 copy-start.4
  3.3 0.0 copy-start.1
  3.3 17.3 %all-to-all-start = ((f32[64,2,128]{2,1,0:T(2,128)}), f32[64,2,128]{2,1,0:T(2,128)S(1)}, u32[]{:S(2)}, u32[]{:S(2)}) async-start(f32[64,2,128]{2,1,0:T(2,128)} %bitcast.99), calls=%async_computation | async-start | bytes 131072 | tf_op jit(solution)/shard_map/all_to_all | solution.py:235
  20.6 0.0 copy-start
  20.6 4.0 %collective-permute-start = (f32[32,32]{1,0:T(8,128)S(1)}, f32[32,32]{1,0:T(8,128)S(1)}, u32[]{:S(2)}, u32[]{:S(2)}) collective-permute-start(f32[32,32]{1,0:T(8,128)S(1)} %bitcast.101), channel_id=1, source_target_pairs={{0,1},{1,2},{2,3},{3,4},{4,5},{5,6},{6,7},{8,9},{9,10},{10,11},{11... | collective-permute-start | bytes 12296 | tf_op jit(solution)/shard_map/ppermute | solution.py:183
  24.6 1.9 %collective-permute-start.1 = (f32[32,32]{1,0:T(8,128)S(1)}, f32[32,32]{1,0:T(8,128)S(1)}, u32[]{:S(2)}, u32[]{:S(2)}) collective-permute-start(f32[32,32]{1,0:T(8,128)S(1)} %bitcast.100), channel_id=1, source_target_pairs={{1,0},{2,1},{3,2},{4,3},{5,4},{6,5},{7,6},{9,8},{10,9},{11,10},{12... | collective-permute-start | bytes 12296 | tf_op jit(solution)/shard_map/ppermute | solution.py:184
  26.5 5.1 %all-to-all-done = f32[64,2,128]{2,1,0:T(2,128)S(1)} async-done(((f32[64,2,128]{2,1,0:T(2,128)}), f32[64,2,128]{2,1,0:T(2,128)S(1)}, u32[]{:S(2)}, u32[]{:S(2)}) %all-to-all-start) | async-done | bytes 65568 | tf_op jit(solution)/shard_map/all_to_all | solution.py:235
  31.7 1.0 %shard_map.273 = (f32[128,128]{1,0:T(8,128)S(1)}, f32[128,128]{1,0:T(8,128)}) custom-call(f32[128,128]{1,0:T(8,128)S(1)} %bitcast.52, f32[48,256]{1,0:T(8,128)S(1)} %bitcast.39, f32[48,256]{1,0:T(8,128)S(1)} %bitcast.46), custom_call_target="tpu_custom_call" | custom-call | tf_op jit(solution)/shard_map/pallas_call | solution.py:137
  32.7 7.4 %all-to-all-start.1 = ((f32[64,2,128]{2,1,0:T(2,128)}), f32[64,2,128]{2,1,0:T(2,128)S(1)}, u32[]{:S(2)}, u32[]{:S(2)}) async-start(f32[64,2,128]{2,1,0:T(2,128)} %bitcast.13), calls=%async_computation.1 | async-start | bytes 131072 | tf_op jit(solution)/shard_map/all_to_all | solution.py:249
  40.2 0.0 copy-start.16
  40.2 0.0 copy-start.17
  40.2 0.0 copy-start.20
  40.2 0.0 copy-start.21
  40.3 0.6 copy-done.22
  40.9 0.0 copy-start.15
  40.9 0.0 copy-start.7
  41.0 0.6 copy-done.6
  41.6 2.9 %shard_map.275 = (f32[4,48,256]{2,1,0:T(8,128)S(1)}, f32[2,48,256]{2,1,0:T(8,128)S(1)}, f32[10,48,256]{2,1,0:T(8,128)S(1)}, f32[80,32]{1,0:T(8,128)S(1)}, f32[48,32]{1,0:T(8,128)S(1)}) custom-call(f32[48,256]{1,0:T(8,128)S(1)} %bitcast.40, f32[48,256]{1,0:T(8,128)S(1)} %bitcast.47, s32[1,256]{1,0:T(1,128)S(1)} %bitcast.59, s32[1,256]{1,0:T(1,128)S(1)} %bitcast.62, ...), custom_call_target="tpu_custom_call" | custom-call | tf_op jit(solution)/shard_map/pallas_call | solution.py:137
  44.5 0.6 copy-done.9
  45.2 2.1 %shard_map.274 = (f32[4,48,256]{2,1,0:T(8,128)S(1)}, f32[10,48,128]{2,1,0:T(8,128)S(1)}, f32[8,256]{1,0:T(8,128)S(1)}) custom-call(f32[128,128]{1,0:T(8,128)S(1)} %get-tuple-element.29.mirror_ref.refs_6_, f32[48,256]{1,0:T(8,128)S(1)} %bitcast.41, f32[48,256]{1,0:T(8,128)S(1)} %bitcast.48, s32[1,256]{1,0:T(1,128)S(1)} %bitcast.60, s32[1,256]{1,0:T(1,128)S(1)} %bitcast.63, ...), custom_call_target="tpu_custom_call" | custom-call | tf_op jit(solution)/shard_map/pallas_call | solution.py:137
  47.3 4.4 %all-to-all-done.1 = f32[64,2,128]{2,1,0:T(2,128)S(1)} async-done(((f32[64,2,128]{2,1,0:T(2,128)}), f32[64,2,128]{2,1,0:T(2,128)S(1)}, u32[]{:S(2)}, u32[]{:S(2)}) %all-to-all-start.1) | async-done | bytes 65568 | tf_op jit(solution)/shard_map/all_to_all | solution.py:249
  51.7 0.6 copy-done.11
  52.3 0.0 copy-done.12
  52.4 0.0 copy-done.13
  52.4 2.1 %shard_map.276 = (f32[10,48,64]{2,1,0:T(8,128)S(1)}, f32[4,48,256]{2,1,0:T(8,128)S(1)}, f32[128,384]{1,0:T(8,128)S(1)}) custom-call(f32[48,256]{1,0:T(8,128)S(1)} %bitcast.42, f32[48,256]{1,0:T(8,128)S(1)} %bitcast.43, f32[48,256]{1,0:T(8,128)S(1)} %bitcast.49, f32[48,256]{1,0:T(8,128)S(1)} %bitcast.53, f32[48,256]{1,0:T(8,128)S(1)} %bitcast.55, ...), custom_call_target="tpu_custom_call" | custom-call | tf_op jit(solution)/shard_map/pallas_call | solution.py:137
  54.5 0.8 all_to_all.27
  55.3 7.9 %all-to-all-start.2 = ((f32[64,2,384]{2,1,0:T(2,128)}), f32[64,2,384]{2,1,0:T(2,128)S(1)}, u32[]{:S(2)}, u32[]{:S(2)}) async-start(f32[64,2,384]{2,1,0:T(2,128)} %all_to_all.27), calls=%async_computation.2 | async-start | bytes 393216 | tf_op jit(solution)/shard_map/all_to_all | solution.py:407
  63.2 3.2 %shard_map.277 = (f32[4,48,256]{2,1,0:T(8,128)S(1)}, f32[2,48,256]{2,1,0:T(8,128)S(1)}, f32[48,32]{1,0:T(8,128)}, f32[48,32]{1,0:T(8,128)}) custom-call(f32[4,48,256]{2,1,0:T(8,128)S(1)} %get-tuple-element.35.refs_0_, s32[1,256]{1,0:T(1,128)S(1)} %bitcast.61, s32[1,256]{1,0:T(1,128)S(1)} %bitcast.64, f32[1,256]{1,0:T(1,128)S(1)} %bitcast.84, ...), custom_call_target="tpu_custom_call" | custom-call | tf_op jit(solution)/shard_map/pallas_call | solution.py:137
  66.3 9.6 %all-to-all-done.2 = f32[64,2,384]{2,1,0:T(2,128)S(1)} async-done(((f32[64,2,384]{2,1,0:T(2,128)}), f32[64,2,384]{2,1,0:T(2,128)S(1)}, u32[]{:S(2)}, u32[]{:S(2)}) %all-to-all-start.2) | async-done | bytes 196640 | tf_op jit(solution)/shard_map/all_to_all | solution.py:407
  75.9 0.1 all_to_all.29.refs_5_
  76.0 3.5 %shard_map.278 = (f32[48,256]{1,0:T(8,128)}, f32[48,256]{1,0:T(8,128)}, f32[48,256]{1,0:T(8,128)}) custom-call(f32[4,48,256]{2,1,0:T(8,128)S(1)} %get-tuple-element.35.refs_0_, f32[48,256]{1,0:T(8,128)S(1)} %bitcast.44, f32[48,256]{1,0:T(8,128)S(1)} %bitcast.50, f32[48,256]{1,0:T(8,128)S(1)} %bitcast.54, f32[48,256]{1,0:T(8,128)S(1)} %bitcast.56, ...), custom_call_target="tpu_custom_call" | custom-call | tf_op jit(solution)/shard_map/pallas_call | solution.py:137
  (39 shorter events, 0.1 us)
Async XLA Ops:
  3.3 17.3 %copy-start.4 = (f32[3,16,32]{2,1,0:T(8,128)S(1)}, f32[3,16,32]{2,1,0:T(8,128)}, u32[]{:S(2)}) copy-start(f32[3,16,32]{2,1,0:T(8,128)} %param.29) | copy-start | bytes 18436
  3.3 28.4 %copy-start.1 = (f32[3,16,256]{2,1,0:T(8,128)S(1)}, f32[3,16,256]{2,1,0:T(8,128)}, u32[]{:S(2)}) copy-start(f32[3,16,256]{2,1,0:T(8,128)} %param.26) | copy-start | bytes 147460
  3.3 28.4 %all-to-all-start = ((f32[64,2,128]{2,1,0:T(2,128)}), f32[64,2,128]{2,1,0:T(2,128)S(1)}, u32[]{:S(2)}, u32[]{:S(2)}) async-start(f32[64,2,128]{2,1,0:T(2,128)} %bitcast.99), calls=%async_computation | async-start | bytes 131072 | tf_op jit(solution)/shard_map/all_to_all | solution.py:235
  20.6 11.1 %copy-start = (f32[3,16,256]{2,1,0:T(8,128)S(1)}, f32[3,16,256]{2,1,0:T(8,128)}, u32[]{:S(2)}) copy-start(f32[3,16,256]{2,1,0:T(8,128)} %param.25) | copy-start | bytes 147460
  20.6 20.2 %collective-permute-start = (f32[32,32]{1,0:T(8,128)S(1)}, f32[32,32]{1,0:T(8,128)S(1)}, u32[]{:S(2)}, u32[]{:S(2)}) collective-permute-start(f32[32,32]{1,0:T(8,128)S(1)} %bitcast.101), channel_id=1, source_target_pairs={{0,1},{1,2},{2,3},{3,4},{4,5},{5,6},{6,7},{8,9},{9,10},{10,11},{11... | collective-permute-start | bytes 12296 | tf_op jit(solution)/shard_map/ppermute | solution.py:183
  24.6 16.3 %collective-permute-start.1 = (f32[32,32]{1,0:T(8,128)S(1)}, f32[32,32]{1,0:T(8,128)S(1)}, u32[]{:S(2)}, u32[]{:S(2)}) collective-permute-start(f32[32,32]{1,0:T(8,128)S(1)} %bitcast.100), channel_id=1, source_target_pairs={{1,0},{2,1},{3,2},{4,3},{5,4},{6,5},{7,6},{9,8},{10,9},{11,10},{12... | collective-permute-start | bytes 12296 | tf_op jit(solution)/shard_map/ppermute | solution.py:184
  32.7 7.4 %copy-start.23 = (s32[64]{0:T(128)S(1)}, s32[64]{0:T(128)}, u32[]{:S(2)}) copy-start(s32[64]{0:T(128)} %param.49) | copy-start | bytes 772
  32.7 19.0 %all-to-all-start.1 = ((f32[64,2,128]{2,1,0:T(2,128)}), f32[64,2,128]{2,1,0:T(2,128)S(1)}, u32[]{:S(2)}, u32[]{:S(2)}) async-start(f32[64,2,128]{2,1,0:T(2,128)} %bitcast.13), calls=%async_computation.1 | async-start | bytes 131072 | tf_op jit(solution)/shard_map/all_to_all | solution.py:249
  40.1 0.7 copy-start.22
  40.2 0.7 copy-start.16
  40.2 0.7 copy-start.17
  40.2 0.7 copy-start.18
  40.2 0.7 copy-start.19
  40.2 0.7 copy-start.20
  40.2 0.7 copy-start.21
  40.8 0.7 copy-start.6
  40.8 0.7 copy-start.8
  40.9 0.7 copy-start.14
  40.9 0.7 copy-start.15
  40.9 0.7 copy-start.7
  40.9 0.7 copy-start.10
  44.5 0.7 copy-start.9
  45.2 6.5 %copy-start.2 = (f32[3,16,256]{2,1,0:T(8,128)S(1)}, f32[3,16,256]{2,1,0:T(8,128)}, u32[]{:S(2)}) copy-start(f32[3,16,256]{2,1,0:T(8,128)} %param.27) | copy-start | bytes 147460
  45.2 6.5 %copy-start.3 = (f32[3,16,256]{2,1,0:T(8,128)S(1)}, f32[3,16,256]{2,1,0:T(8,128)}, u32[]{:S(2)}) copy-start(f32[3,16,256]{2,1,0:T(8,128)} %param.28) | copy-start | bytes 147460
  45.2 6.5 %copy-start.5 = (f32[64,128]{1,0:T(8,128)S(1)}, f32[64,128]{1,0:T(8,128)}, u32[]{:S(2)}) copy-start(f32[64,128]{1,0:T(8,128)} %get-tuple-element.30.refs_7_) | copy-start | bytes 98308
  51.7 0.7 copy-start.11
  51.7 0.7 copy-start.12
  51.7 0.7 copy-start.13
  55.3 20.6 %all-to-all-start.2 = ((f32[64,2,384]{2,1,0:T(2,128)}), f32[64,2,384]{2,1,0:T(2,128)S(1)}, u32[]{:S(2)}, u32[]{:S(2)}) async-start(f32[64,2,384]{2,1,0:T(2,128)} %all_to_all.27), calls=%async_computation.2 | async-start | bytes 393216 | tf_op jit(solution)/shard_map/all_to_all | solution.py:407

commit v5 on v4

--- a/solution.py
+++ b/solution.py
@@ -247,6 +247,10 @@
         recv_setup, wm, wa,
     )
     recv_0 = lax.all_to_all(pay_0, "net", 0, 0, tiled=True)
+
+    def spread(p):
+        return (lax.broadcasted_iota(jnp.int32, (3 * slots, slots), 0)
+                == 3 * lax.broadcasted_iota(jnp.int32, (3 * slots, slots), 1) + p).astype(F32)
 
     def local_part(first, refs):
         if first:
@@ -327,17 +331,17 @@
 
     def cut_part(first, refs):
         (st_ref, wm_ref, wa_ref, lr_ref, lq_ref, recv_ref, mirror_ref, slot_ref,
-         dg_ref, cn_ref, cc_ref, cs_ref, cl_ref, cstep_ref,
-         tin_ref, sup_ref, tm_ref) = refs[:17]
-        rest = refs[17:]
+         dg_ref, cp_ref, tin_ref, sup_ref, tm_ref) = refs[:13]
+        rest = refs[13:]
+        cprm_v = cp_ref[...]
         wmv, wav = wm_ref[...], wa_ref[...]
         slot_t = slot_ref[...]
         mirror = mirror_ref[...]
-        inc_near = onehot(cn_ref[...], buses)
+        inc_near = onehot(cprm_v[0:1].astype(jnp.int32), buses)
         inc_recv = onehot(mirror[0:1].astype(jnp.int32) - 1, buses)
         degree = dg_ref[0:1]
         gen_count = dg_ref[1:2]
-        prm_cut = (cc_ref[...], cs_ref[...], cl_ref[...], cstep_ref[...])
+        prm_cut = (cprm_v[1:2], cprm_v[2:3], cprm_v[3:4], cprm_v[4:5])
         if first:
             (cc_out, st_out, pay_out) = rest
             zero_b = jnp.zeros((nrow, buses), F32)
@@ -353,7 +357,8 @@
         else:
             (cc_in_ref, cm_ref, mag_out, ang_out, pr_out) = rest
             state = tuple(st_ref[i] for i in range(4))
-            both = recv_ref[...].T
+            got = recv_ref[...]
+            both = rows(*(mm(spread(p).T, got).T for p in range(3)))
             near_mirror = split4(both[0:4 * nrow], nrow)
             far_cross = split4(mm_t(both[4 * nrow:], slot_t), nrow)
             stack = rows(*state)
@@ -378,7 +383,8 @@
             st_out[3] = pq
             new_stack = rows(mag, ang, pr, pq)
             near_slot = mm(inc_near, slot_t)
-            pay_out[...] = rows(mm(new_stack, near_slot), mm(new_stack, inc_recv)).T
+            vals = rows(mm(new_stack, near_slot), mm(new_stack, inc_recv))
+            pay_out[...] = sum(mm_t(spread(p), vals[p * 128:(p + 1) * 128]) for p in range(3))
         else:
             mag_out[...] = mag
             ang_out[...] = ang
@@ -398,13 +404,13 @@
         mirror0_kernel, (tot_shape, sds((10, nrow, slots), F32), sds((8, buses), F32)), mirror_t, wm, wa,
         br_rows[0], br_rows[1], cut_rows[0], gen_rows[0],
     )
-    cut_in = cut_rows
+    cprm = jnp.concatenate([cut_rows[0].astype(F32), *cut_rows[1:], jnp.zeros((3, cuts), F32)], axis=0)
     cc1, st1, pay_1 = vmem_call(
         lambda *refs: cut_part(True, refs),
-        (sds((10, nrow, cuts), F32), tot_shape, sds((slots, 8 * nrow), F32)),
-        wm, wm, wa, lr, lq, recv_0, mirror_t, slot_t, dg, *cut_in, tin0, sup0, tm0,
-    )
-    recv_1 = lax.all_to_all(pay_1, "net", 0, 0, tiled=True)
+        (sds((10, nrow, cuts), F32), tot_shape, sds((3 * slots, 128), F32)),
+        wm, wm, wa, lr, lq, recv_0, mirror_t, slot_t, dg, cprm, tin0, sup0, tm0,
+    )
+    recv_1 = lax.all_to_all(pay_1.reshape(3 * parts, 2, 128), "net", 0, 0, tiled=True).reshape(3 * slots, 128)
     tin1, sup1, gr, gq = vmem_call(
         lambda *refs: local_part(False, refs),
         (tot_shape, sds((2, nrow, buses), F32), sds((nrow, gens), F32), sds((nrow, gens), F32)),
@@ -413,7 +419,7 @@
     mag, ang, pr = vmem_call(
         lambda *refs: cut_part(False, refs),
         (sds((nrow, buses), F32), sds((nrow, buses), F32), sds((nrow, buses), F32)),
-        st1, wm, wa, lr, lq, recv_1, mirror_t, slot_t, dg, *cut_in, tin1, sup1, tin1,
+        st1, wm, wa, lr, lq, recv_1, mirror_t, slot_t, dg, cprm, tin1, sup1, tin1,
         cc1, cm1,
     )
     shape_b = (periods, scen, buses)

time: 80.5 us -> 81.2 us (level)
  Pallas kernels: 17.3 us -> 20.1 us
  local copies, waits for them, and re-layouts: 3.52 us -> 1.45 us
    pallas_call x6, Pallas kernels: 14.7 us -> 17.5 us  [vmem_call(): pl.pallas_call(kernel, out_shape=outs, in_specs=[pl.BlockSpec(memory_spac...]
    unnamed x48, local copies, waits for them, and re-layouts: 2.6 us -> 1.42 us
    all_to_all x2 -> x0, local copies, waits for them, and re-layouts: 0.92 us -> none  [on_device(): recv_1 = lax.all_to_all(pay_1, 'net', 0, 0, tiled=True)]
  transfers between devices with their start and end apart: 5 -> 5, of which waited for: 3 -> 3; matrix products, arithmetic and copies ran while one was open for 0% -> 0% of each run, Pallas kernels for 12% -> 11%
where the time goes in v5:
time: 81.2 us; the launch traced here: 80.1 us
  starting transfers between devices  38 us (47%)
  Pallas kernels  20.1 us (25%)
  waiting for transfers between devices  19.6 us (24%)
  local copies, waits for them, and re-layouts  1.45 us (2%)
  between operations  0.96 us (1%)
    pallas_call x6, Pallas kernels, vmem_call(): pl.pallas_call(kernel, out_shape=outs, in_specs=[pl.BlockSpec(memory_spac...  17.5 us
    all_to_all x1, starting transfers between devices, on_device(): recv_setup = lax.all_to_all(pay_setup, 'net', 0, 0, tiled=True)  17.3 us
    all_to_all x1, waiting for transfers between devices, on_device(): lax.all_to_all(pay_1.reshape(3 * parts, 2, 128), 'net', 0, 0, tiled=True)  9.49 us
    all_to_all x1, starting transfers between devices, on_device(): recv_0 = lax.all_to_all(pay_0, 'net', 0, 0, tiled=True)  7.43 us
    all_to_all x1, starting transfers between devices, on_device(): lax.all_to_all(pay_1.reshape(3 * parts, 2, 128), 'net', 0, 0, tiled=True)  7.41 us
    all_to_all x1, waiting for transfers between devices, on_device(): recv_setup = lax.all_to_all(pay_setup, 'net', 0, 0, tiled=True)  5.15 us
    all_to_all x1, waiting for transfers between devices, on_device(): recv_0 = lax.all_to_all(pay_0, 'net', 0, 0, tiled=True)  4.93 us
    ppermute x1, starting transfers between devices, on_device(): lax.ppermute(sr[nrow - halo:], 'tm', [(i, i + 1) for i in range(ntm - 1)])  3.96 us
  transfers between devices with their start and end apart: 5, of which 3 were waited for; matrix products, arithmetic and copies ran while one was open for 0% of the time, Pallas kernels for 11%

profile of v5, /device:TPU:1, one launch (start us, length us, event | category | flops | bytes accessed | tf_op | source)
XLA Modules:
  0.0 80.1 jit_solution(14530798149787620215)
XLA Ops:
  0.6 2.6 %shard_map.272 = (f32[64,128]{1,0:T(8,128)}, f32[128,128]{1,0:T(8,128)}) custom-call(s32[1,64]{1,0:T(1,128)} %bitcast.103, s32[1,64]{1,0:T(1,128)} %bitcast.75, s32[1,64]{1,0:T(1,128)} %bitcast.104, f32[1,64]{1,0:T(1,128)} %bitcast.96, f32[1,64]{1,0:T(1,128)} %bitcast.98, f32[1,64]{1,0:T(1,128)} %bitcast.100, s32[1,64]{1,0:T(1,128)} %bitcast.102, ...), custom_call_target="tpu_custom_call" | custom-call | tf_op jit(solution)/shard_map/pallas_call | solution.py:228
  3.3 17.3 %all-to-all-start = ((f32[64,2,128]{2,1,0:T(2,128)}), f32[64,2,128]{2,1,0:T(2,128)S(1)}, u32[]{:S(2)}, u32[]{:S(2)}) async-start(f32[64,2,128]{2,1,0:T(2,128)} %bitcast.93), calls=%async_computation | async-start | bytes 131072 | tf_op jit(solution)/shard_map/all_to_all | solution.py:235
  20.6 0.0 copy-start
  20.6 4.0 %collective-permute-start = (f32[32,32]{1,0:T(8,128)S(1)}, f32[32,32]{1,0:T(8,128)S(1)}, u32[]{:S(2)}, u32[]{:S(2)}) collective-permute-start(f32[32,32]{1,0:T(8,128)S(1)} %bitcast.95), channel_id=1, source_target_pairs={{0,1},{1,2},{2,3},{3,4},{4,5},{5,6},{6,7},{8,9},{9,10},{10,11},{11... | collective-permute-start | bytes 12296 | tf_op jit(solution)/shard_map/ppermute | solution.py:183
  24.6 1.9 %collective-permute-start.1 = (f32[32,32]{1,0:T(8,128)S(1)}, f32[32,32]{1,0:T(8,128)S(1)}, u32[]{:S(2)}, u32[]{:S(2)}) collective-permute-start(f32[32,32]{1,0:T(8,128)S(1)} %bitcast.94), channel_id=1, source_target_pairs={{1,0},{2,1},{3,2},{4,3},{5,4},{6,5},{7,6},{9,8},{10,9},{11,10},{12... | collective-permute-start | bytes 12296 | tf_op jit(solution)/shard_map/ppermute | solution.py:184
  26.5 5.1 %all-to-all-done = f32[64,2,128]{2,1,0:T(2,128)S(1)} async-done(((f32[64,2,128]{2,1,0:T(2,128)}), f32[64,2,128]{2,1,0:T(2,128)S(1)}, u32[]{:S(2)}, u32[]{:S(2)}) %all-to-all-start) | async-done | bytes 65568 | tf_op jit(solution)/shard_map/all_to_all | solution.py:235
  31.7 1.0 %shard_map.273 = (f32[128,128]{1,0:T(8,128)S(1)}, f32[128,128]{1,0:T(8,128)}) custom-call(f32[128,128]{1,0:T(8,128)S(1)} %bitcast.57, f32[48,256]{1,0:T(8,128)S(1)} %bitcast.43, f32[48,256]{1,0:T(8,128)S(1)} %bitcast.50), custom_call_target="tpu_custom_call" | custom-call | tf_op jit(solution)/shard_map/pallas_call | solution.py:137
  32.7 7.4 %all-to-all-start.1 = ((f32[64,2,128]{2,1,0:T(2,128)}), f32[64,2,128]{2,1,0:T(2,128)S(1)}, u32[]{:S(2)}, u32[]{:S(2)}) async-start(f32[64,2,128]{2,1,0:T(2,128)} %bitcast.13), calls=%async_computation.1 | async-start | bytes 131072 | tf_op jit(solution)/shard_map/all_to_all | solution.py:249
  40.2 0.0 copy-start.19
  40.2 0.0 copy-start.20
  40.2 0.6 copy-done.23
  40.9 0.0 copy-start.11
  40.9 0.0 copy-start.12
  41.0 0.0 copy-start.15
  41.1 0.5 copy-done.6
  41.6 0.0 copy-done.8
  41.6 0.0 copy-done.11
  41.6 0.0 copy-done.12
  41.6 0.0 copy-done.13
  41.7 0.0 copy-done.15
  41.7 0.0 copy-done.16
  41.7 0.0 copy-done.17
  41.7 0.0 copy-done.18
  41.7 0.0 copy-done.7
  41.7 2.9 %shard_map.275 = (f32[4,48,256]{2,1,0:T(8,128)S(1)}, f32[2,48,256]{2,1,0:T(8,128)S(1)}, f32[10,48,256]{2,1,0:T(8,128)S(1)}, f32[80,32]{1,0:T(8,128)S(1)}, f32[48,32]{1,0:T(8,128)S(1)}) custom-call(f32[48,256]{1,0:T(8,128)S(1)} %bitcast.44, f32[48,256]{1,0:T(8,128)S(1)} %bitcast.51, s32[1,256]{1,0:T(1,128)S(1)} %bitcast.64, s32[1,256]{1,0:T(1,128)S(1)} %bitcast.67, ...), custom_call_target="tpu_custom_call" | custom-call | tf_op jit(solution)/shard_map/pallas_call | solution.py:137
  44.7 2.1 %shard_map.274 = (f32[4,48,256]{2,1,0:T(8,128)S(1)}, f32[10,48,128]{2,1,0:T(8,128)S(1)}, f32[8,256]{1,0:T(8,128)S(1)}) custom-call(f32[128,128]{1,0:T(8,128)S(1)} %get-tuple-element.29.mirror_ref.refs_6_, f32[48,256]{1,0:T(8,128)S(1)} %bitcast.45, f32[48,256]{1,0:T(8,128)S(1)} %bitcast.52, s32[1,256]{1,0:T(1,128)S(1)} %bitcast.65, s32[1,256]{1,0:T(1,128)S(1)} %bitcast.68, ...), custom_call_target="tpu_custom_call" | custom-call | tf_op jit(solution)/shard_map/pallas_call | solution.py:137
  46.8 4.9 %all-to-all-done.1 = f32[64,2,128]{2,1,0:T(2,128)S(1)} async-done(((f32[64,2,128]{2,1,0:T(2,128)}), f32[64,2,128]{2,1,0:T(2,128)S(1)}, u32[]{:S(2)}, u32[]{:S(2)}) %all-to-all-start.1) | async-done | bytes 65568 | tf_op jit(solution)/shard_map/all_to_all | solution.py:249
  51.7 4.1 %shard_map.276 = (f32[10,48,64]{2,1,0:T(8,128)S(1)}, f32[4,48,256]{2,1,0:T(8,128)S(1)}, f32[384,128]{1,0:T(8,128)}) custom-call(f32[48,256]{1,0:T(8,128)S(1)} %bitcast.46, f32[48,256]{1,0:T(8,128)S(1)} %bitcast.47, f32[48,256]{1,0:T(8,128)S(1)} %bitcast.53, f32[48,256]{1,0:T(8,128)S(1)} %bitcast.58, f32[48,256]{1,0:T(8,128)S(1)} %bitcast.60, ...), custom_call_target="tpu_custom_call" | custom-call | tf_op jit(solution)/shard_map/pallas_call | solution.py:137
  55.9 7.4 %all-to-all-start.2 = ((f32[192,2,128]{2,1,0:T(2,128)}), f32[192,2,128]{2,1,0:T(2,128)S(1)}, u32[]{:S(2)}, u32[]{:S(2)}) async-start(f32[192,2,128]{2,1,0:T(2,128)} %bitcast.33), calls=%async_computation.2 | async-start | bytes 393216 | tf_op jit(solution)/shard_map/all_to_all | solution.py:413
  63.3 3.2 %shard_map.277 = (f32[4,48,256]{2,1,0:T(8,128)S(1)}, f32[2,48,256]{2,1,0:T(8,128)S(1)}, f32[48,32]{1,0:T(8,128)}, f32[48,32]{1,0:T(8,128)}) custom-call(f32[4,48,256]{2,1,0:T(8,128)S(1)} %get-tuple-element.35.refs_0_, s32[1,256]{1,0:T(1,128)S(1)} %bitcast.66, s32[1,256]{1,0:T(1,128)S(1)} %bitcast.69, f32[1,256]{1,0:T(1,128)S(1)} %bitcast.78, ...), custom_call_target="tpu_custom_call" | custom-call | tf_op jit(solution)/shard_map/pallas_call | solution.py:137
  66.4 9.5 %all-to-all-done.2 = f32[192,2,128]{2,1,0:T(2,128)S(1)} async-done(((f32[192,2,128]{2,1,0:T(2,128)}), f32[192,2,128]{2,1,0:T(2,128)S(1)}, u32[]{:S(2)}, u32[]{:S(2)}) %all-to-all-start.2) | async-done | bytes 196640 | tf_op jit(solution)/shard_map/all_to_all | solution.py:413
  75.9 4.2 %shard_map.278 = (f32[48,256]{1,0:T(8,128)}, f32[48,256]{1,0:T(8,128)}, f32[48,256]{1,0:T(8,128)}) custom-call(f32[4,48,256]{2,1,0:T(8,128)S(1)} %get-tuple-element.35.refs_0_, f32[48,256]{1,0:T(8,128)S(1)} %bitcast.48, f32[48,256]{1,0:T(8,128)S(1)} %bitcast.54, f32[48,256]{1,0:T(8,128)S(1)} %bitcast.59, f32[48,256]{1,0:T(8,128)S(1)} %bitcast.61, ...), custom_call_target="tpu_custom_call" | custom-call | tf_op jit(solution)/shard_map/pallas_call | solution.py:137
  (39 shorter events, 0.1 us)
Async XLA Ops:
  3.3 17.3 %copy-start.4 = (f32[3,16,32]{2,1,0:T(8,128)S(1)}, f32[3,16,32]{2,1,0:T(8,128)}, u32[]{:S(2)}) copy-start(f32[3,16,32]{2,1,0:T(8,128)} %param.29) | copy-start | bytes 18436
  3.3 28.4 %copy-start.1 = (f32[3,16,256]{2,1,0:T(8,128)S(1)}, f32[3,16,256]{2,1,0:T(8,128)}, u32[]{:S(2)}) copy-start(f32[3,16,256]{2,1,0:T(8,128)} %param.26) | copy-start | bytes 147460
  3.3 28.4 %all-to-all-start = ((f32[64,2,128]{2,1,0:T(2,128)}), f32[64,2,128]{2,1,0:T(2,128)S(1)}, u32[]{:S(2)}, u32[]{:S(2)}) async-start(f32[64,2,128]{2,1,0:T(2,128)} %bitcast.93), calls=%async_computation | async-start | bytes 131072 | tf_op jit(solution)/shard_map/all_to_all | solution.py:235
  20.6 11.1 %copy-start = (f32[3,16,256]{2,1,0:T(8,128)S(1)}, f32[3,16,256]{2,1,0:T(8,128)}, u32[]{:S(2)}) copy-start(f32[3,16,256]{2,1,0:T(8,128)} %param.25) | copy-start | bytes 147460
  20.6 20.3 %collective-permute-start = (f32[32,32]{1,0:T(8,128)S(1)}, f32[32,32]{1,0:T(8,128)S(1)}, u32[]{:S(2)}, u32[]{:S(2)}) collective-permute-start(f32[32,32]{1,0:T(8,128)S(1)} %bitcast.95), channel_id=1, source_target_pairs={{0,1},{1,2},{2,3},{3,4},{4,5},{5,6},{6,7},{8,9},{9,10},{10,11},{11... | collective-permute-start | bytes 12296 | tf_op jit(solution)/shard_map/ppermute | solution.py:183
  24.6 16.3 %collective-permute-start.1 = (f32[32,32]{1,0:T(8,128)S(1)}, f32[32,32]{1,0:T(8,128)S(1)}, u32[]{:S(2)}, u32[]{:S(2)}) collective-permute-start(f32[32,32]{1,0:T(8,128)S(1)} %bitcast.94), channel_id=1, source_target_pairs={{1,0},{2,1},{3,2},{4,3},{5,4},{6,5},{7,6},{9,8},{10,9},{11,10},{12... | collective-permute-start | bytes 12296 | tf_op jit(solution)/shard_map/ppermute | solution.py:184
  32.7 7.4 %copy-start.10 = (s32[64]{0:T(128)S(1)}, s32[64]{0:T(128)}, u32[]{:S(2)}) copy-start(s32[64]{0:T(128)} %param.43) | copy-start | bytes 772
  32.7 7.5 %copy-start.22 = (s32[64]{0:T(128)S(1)}, s32[64]{0:T(128)}, u32[]{:S(2)}) copy-start(s32[64]{0:T(128)} %param.49) | copy-start | bytes 772
  32.7 19.0 %all-to-all-start.1 = ((f32[64,2,128]{2,1,0:T(2,128)}), f32[64,2,128]{2,1,0:T(2,128)S(1)}, u32[]{:S(2)}, u32[]{:S(2)}) async-start(f32[64,2,128]{2,1,0:T(2,128)} %bitcast.13), calls=%async_computation.1 | async-start | bytes 131072 | tf_op jit(solution)/shard_map/all_to_all | solution.py:249
  40.2 0.7 copy-start.23
  40.2 0.7 copy-start.19
  40.2 0.7 copy-start.20
  40.2 0.7 copy-start.21
  40.8 0.7 copy-start.6
  40.9 0.7 copy-start.8
  40.9 0.7 copy-start.11
  40.9 0.7 copy-start.12
  41.0 0.7 copy-start.13
  41.0 0.7 copy-start.14
  41.0 0.7 copy-start.15
  41.0 0.7 copy-start.16
  41.0 0.7 copy-start.17
  41.0 0.7 copy-start.18
  41.0 0.7 copy-start.7
  41.0 0.7 copy-start.9
  44.6 7.1 %copy-start.2 = (f32[3,16,256]{2,1,0:T(8,128)S(1)}, f32[3,16,256]{2,1,0:T(8,128)}, u32[]{:S(2)}) copy-start(f32[3,16,256]{2,1,0:T(8,128)} %param.27) | copy-start | bytes 147460
  44.7 7.1 %copy-start.3 = (f32[3,16,256]{2,1,0:T(8,128)S(1)}, f32[3,16,256]{2,1,0:T(8,128)}, u32[]{:S(2)}) copy-start(f32[3,16,256]{2,1,0:T(8,128)} %param.28) | copy-start | bytes 147460
  44.7 7.0 %copy-start.5 = (f32[64,128]{1,0:T(8,128)S(1)}, f32[64,128]{1,0:T(8,128)}, u32[]{:S(2)}) copy-start(f32[64,128]{1,0:T(8,128)} %get-tuple-element.30.refs_7_) | copy-start | bytes 98308
  55.9 20.1 %all-to-all-start.2 = ((f32[192,2,128]{2,1,0:T(2,128)}), f32[192,2,128]{2,1,0:T(2,128)S(1)}, u32[]{:S(2)}, u32[]{:S(2)}) async-start(f32[192,2,128]{2,1,0:T(2,128)} %bitcast.33), calls=%async_computation.2 | async-start | bytes 393216 | tf_op jit(solution)/shard_map/all_to_all | solution.py:413

commit v6 on v5

--- a/solution.py
+++ b/solution.py
@@ -13,21 +13,50 @@
 F32 = jnp.float32
 
 
-def mm(a, b):
-    return lax.dot_general(a, b, (((1,), (0,)), ((), ())), precision=HI, preferred_element_type=F32)
-
-
-def mm_t(a, b):
-    return lax.dot_general(a, b, (((1,), (1,)), ((), ())), precision=HI, preferred_element_type=F32)
+NN = (((1,), (0,)), ((), ()))
+NT = (((1,), (1,)), ((), ()))
+BF = jnp.bfloat16
+
+
+def split3(x):
+    hi = x.astype(BF)
+    r = x - hi.astype(F32)
+    mid = r.astype(BF)
+    lo = (r - mid.astype(F32)).astype(BF)
+    return hi, mid, lo
+
+
+def dot(a, b, dims):
+    return lax.dot_general(a, b, dims, preferred_element_type=F32)
+
+
+def take(vals, oh):
+    hi, mid, lo = split3(vals)
+    return (dot(hi, oh, NN) + dot(mid, oh, NN)) + dot(lo, oh, NN)
+
+
+def give(vals, oh):
+    hi, mid, lo = split3(vals)
+    return (dot(hi, oh, NT) + dot(mid, oh, NT)) + dot(lo, oh, NT)
+
+
+def take_left(oh, vals):
+    hi, mid, lo = split3(vals)
+    return (dot(oh, hi, NN) + dot(oh, mid, NN)) + dot(oh, lo, NN)
+
+
+def give_left(oh, vals):
+    hi, mid, lo = split3(vals)
+    return (dot(oh, hi, NT) + dot(oh, mid, NT)) + dot(oh, lo, NT)
 
 
 def onehot(ids_row, count):
     n = ids_row.shape[1]
-    return (lax.broadcasted_iota(jnp.int32, (count, n), 0) == ids_row).astype(F32)
+    return (lax.broadcasted_iota(jnp.int32, (count, n), 0) == ids_row).astype(BF)
 
 
 def col_sum(inc):
-    return mm_t(jnp.ones((8, inc.shape[1]), F32), inc)[0:1]
+    return dot(jnp.ones((8, inc.shape[1]), BF), inc, NT)[0:1]
 
 
 def rows(*parts):
@@ -143,17 +172,6 @@
     )(*args)
 
 
-def slot_table(peer_col, cap, slots):
-    cuts = peer_col.shape[0]
-    parts = slots // cap
-    mine = (peer_col == lax.broadcasted_iota(jnp.int32, (cuts, parts), 1)).astype(F32)
-    same = mm_t(mine, mine)
-    earlier = lax.broadcasted_iota(jnp.int32, (cuts, cuts), 1) < lax.broadcasted_iota(jnp.int32, (cuts, cuts), 0)
-    rank = jnp.sum(jnp.where(earlier, same, 0.0), axis=1, keepdims=True)
-    position = peer_col.astype(F32) * cap + rank
-    return (position == lax.broadcasted_iota(jnp.int32, (cuts, slots), 1).astype(F32)).astype(F32)
-
-
 def on_device(
     warm_mag, warm_angle, load_real, load_react, start_real, start_react,
     gen_bus, gen_linear, gen_quad, gen_ramp, gen_cap_real, gen_cap_react,
@@ -206,19 +224,20 @@
             cp.wait()
         peer = peer_ref[...]
         mine_t = (lax.broadcasted_iota(jnp.int32, (parts, cuts), 0) == peer).astype(F32)
-        same = mm(mine_t.T, mine_t)
+        same = dot(mine_t.T.astype(BF), mine_t.astype(BF), NN)
         earlier = lax.broadcasted_iota(jnp.int32, (cuts, cuts), 0) < lax.broadcasted_iota(jnp.int32, (cuts, cuts), 1)
         rank = jnp.sum(jnp.where(earlier, same, 0.0), axis=0, keepdims=True)
         position = peer.astype(F32) * cap + rank
         slot_t = (lax.broadcasted_iota(jnp.int32, (slots, cuts), 0).astype(F32) == position).astype(F32).T
+        slot_b = slot_t.astype(BF)
         slot_out[...] = slot_t
         inc_near = onehot(near_ref[...], buses)
-        by_slot = mm(inc_near, slot_t)
+        by_slot = dot(inc_near, slot_b, NN).astype(BF)
         prm = rows(bus_ref[...].astype(F32) + 1.0, cond_ref[...], susc_ref[...], lim_ref[...],
                    steps_ref[...].astype(F32), jnp.zeros((3, cuts), F32))
         vals = rows(
-            mm(prm, slot_t),
-            mm(rows(wm_ref[...], wa_ref[...]), by_slot),
+            take(prm, slot_b),
+            take(rows(wm_ref[...], wa_ref[...]), by_slot),
             jnp.zeros((nvals0 - 8 - 2 * nrow, slots), F32),
         )
         pay_out[...] = vals.T
@@ -238,7 +257,7 @@
         mirror = recv_ref[...].T
         mirror_out[...] = mirror
         inc_recv = onehot(mirror[0:1].astype(jnp.int32) - 1, buses)
-        vals = rows(mm(rows(wm_ref[...], wa_ref[...]), inc_recv), jnp.zeros((nvals0 - 2 * nrow, slots), F32))
+        vals = rows(take(rows(wm_ref[...], wa_ref[...]), inc_recv), jnp.zeros((nvals0 - 2 * nrow, slots), F32))
         pay_out[...] = vals.T
 
     mirror_t, pay_0 = vmem_call(
@@ -250,7 +269,7 @@
 
     def spread(p):
         return (lax.broadcasted_iota(jnp.int32, (3 * slots, slots), 0)
-                == 3 * lax.broadcasted_iota(jnp.int32, (3 * slots, slots), 1) + p).astype(F32)
+                == 3 * lax.broadcasted_iota(jnp.int32, (3 * slots, slots), 1) + p).astype(BF)
 
     def local_part(first, refs):
         if first:
@@ -272,11 +291,11 @@
         inc_to = onehot(bt_ref[...], buses)
         inc_gen = onehot(gb_ref[...], buses)
         stack = rows(*state)
-        pick_from = split4(mm(stack, inc_from), nrow)
-        pick_to = split4(mm(stack, inc_to), nrow)
+        pick_from = split4(take(stack, inc_from), nrow)
+        pick_to = split4(take(stack, inc_to), nrow)
         prm_in = (bc_ref[...], bs_ref[...], bl_ref[...], bn_ref[...])
         carry_i, fi, ti = advance(carry_in, pick_from, pick_to, prm_in)
-        totals = mm_t(fi, inc_from) + mm_t(ti, inc_to)
+        totals = give(fi, inc_from) + give(ti, inc_to)
         for i in range(4):
             tot_out[i] = totals[i * nrow:(i + 1) * nrow]
         lin, quad, ramp, capr, capq = gl_ref[...], gq_ref[...], gr_ref[...], gcr_ref[...], gcq_ref[...]
@@ -290,13 +309,13 @@
             g0 = jnp.where((per >= 0) & (per < horizon), g0, 0.0)
             gen_real = g0[scen:scen + nrow]
             gen_react = jnp.clip(sq_ref[...], -capq, capq)
-            supply = mm_t(rows(gen_real, gen_react), inc_gen)
+            supply = give(rows(gen_real, gen_react), inc_gen)
             store_carry(ci_out, carry_i)
             g0_out[...] = g0
             gq0_out[...] = gen_react
         else:
             g0 = g0_ref[...]
-            gp = mm(rows(state[2], state[3]), inc_gen)
+            gp = take(rows(state[2], state[3]), inc_gen)
             gp_r, gp_q = gp[0:nrow], gp[nrow:]
             gen_real = jnp.clip(
                 (g0[scen:scen + nrow] - 2.0 * gp_r - lin + ramp * (g0[0:nrow] + g0[2 * scen:2 * scen + nrow]))
@@ -305,7 +324,7 @@
                 capr,
             )
             gen_react = jnp.clip(gq0_ref[...] - 2.0 * gp_q, -capq, capq)
-            supply = mm_t(rows(gen_real + gp_r, gen_react + gp_q), inc_gen)
+            supply = give(rows(gen_real + gp_r, gen_react + gp_q), inc_gen)
             gr_out[...] = gen_real
             gq_out[...] = gen_react
         sup_out[0] = supply[0:nrow]
@@ -320,11 +339,11 @@
         zm = jnp.zeros((nrow, slots), F32)
         zero_b = jnp.zeros((nrow, buses), F32)
         stack = rows(wm_ref[...], wa_ref[...], zero_b, zero_b)
-        pick_recv = split4(mm(stack, inc_recv), nrow)
+        pick_recv = split4(take(stack, inc_recv), nrow)
         near_mirror = (mirror[8:8 + nrow], mirror[8 + nrow:8 + 2 * nrow], zm, zm)
         prm_mir = (mirror[1:2], mirror[2:3], mirror[3:4], mirror[4:5])
         carry_m, _, tmr = advance(None, near_mirror, pick_recv, prm_mir)
-        totals = mm_t(tmr, inc_recv)
+        totals = give(tmr, inc_recv)
         for i in range(4):
             tot_out[i] = totals[i * nrow:(i + 1) * nrow]
         store_carry(cm_out, carry_m)
@@ -335,7 +354,7 @@
         rest = refs[13:]
         cprm_v = cp_ref[...]
         wmv, wav = wm_ref[...], wa_ref[...]
-        slot_t = slot_ref[...]
+        slot_t = slot_ref[...].astype(BF)
         mirror = mirror_ref[...]
         inc_near = onehot(cprm_v[0:1].astype(jnp.int32), buses)
         inc_recv = onehot(mirror[0:1].astype(jnp.int32) - 1, buses)
@@ -348,28 +367,28 @@
             state = (wmv, wav, zero_b, zero_b)
             far_slot = recv_ref[...].T
             zc = jnp.zeros((nrow, cuts), F32)
-            far_c = mm_t(rows(far_slot[0:nrow], far_slot[nrow:2 * nrow]), slot_t)
+            far_c = give(rows(far_slot[0:nrow], far_slot[nrow:2 * nrow]), slot_t)
             far_cross = (far_c[0:nrow], far_c[nrow:], zc, zc)
             stack = rows(*state)
-            pick_near = split4(mm(stack, inc_near), nrow)
+            pick_near = split4(take(stack, inc_near), nrow)
             carry_c, fc, _ = advance(None, pick_near, far_cross, prm_cut)
-            totals = tin_ref[...] + tm_ref[...] + mm_t(fc, inc_near).reshape(4, nrow, buses)
+            totals = tin_ref[...] + tm_ref[...] + give(fc, inc_near).reshape(4, nrow, buses)
         else:
             (cc_in_ref, cm_ref, mag_out, ang_out, pr_out) = rest
             state = tuple(st_ref[i] for i in range(4))
             got = recv_ref[...]
-            both = rows(*(mm(spread(p).T, got).T for p in range(3)))
+            both = rows(*(take_left(spread(p).T, got).T for p in range(3)))
             near_mirror = split4(both[0:4 * nrow], nrow)
-            far_cross = split4(mm_t(both[4 * nrow:], slot_t), nrow)
+            far_cross = split4(give(both[4 * nrow:], slot_t), nrow)
             stack = rows(*state)
-            pick_near = split4(mm(stack, inc_near), nrow)
-            pick_recv = split4(mm(stack, inc_recv), nrow)
+            pick_near = split4(take(stack, inc_near), nrow)
+            pick_recv = split4(take(stack, inc_recv), nrow)
             carry_c_in = load_carry(cc_in_ref)
             carry_m_in = load_carry(cm_ref)
             _, fc, _ = advance(carry_c_in, pick_near, far_cross, prm_cut)
             prm_mir = (mirror[1:2], mirror[2:3], mirror[3:4], mirror[4:5])
             _, _, tmr = advance(carry_m_in, near_mirror, pick_recv, prm_mir)
-            totals = tin_ref[...] + (mm_t(fc, inc_near) + mm_t(tmr, inc_recv)).reshape(4, nrow, buses)
+            totals = tin_ref[...] + (give(fc, inc_near) + give(tmr, inc_recv)).reshape(4, nrow, buses)
         mag = (totals[0] + wmv) / (degree + 1.0)
         ang = (totals[1] + wav) / (degree + 1.0)
         weight = 1.0 + BALANCE_WEIGHT * (gen_count + degree)
@@ -382,9 +401,9 @@
             st_out[2] = pr
             st_out[3] = pq
             new_stack = rows(mag, ang, pr, pq)
-            near_slot = mm(inc_near, slot_t)
-            vals = rows(mm(new_stack, near_slot), mm(new_stack, inc_recv))
-            pay_out[...] = sum(mm_t(spread(p), vals[p * 128:(p + 1) * 128]) for p in range(3))
+            near_slot = dot(inc_near, slot_t, NN).astype(BF)
+            vals = rows(take(new_stack, near_slot), take(new_stack, inc_recv))
+            pay_out[...] = sum(give_left(spread(p), vals[p * 128:(p + 1) * 128]) for p in range(3))
         else:
             mag_out[...] = mag
             ang_out[...] = ang

time: 81.2 us -> 77.5 us (0.954)
  Pallas kernels: 20.1 us -> 16.2 us
  waiting for transfers between devices: 19.6 us -> 20.9 us
  starting transfers between devices: 38 us -> 36.9 us
    pallas_call x6, Pallas kernels: 17.5 us -> 13.9 us  [vmem_call(): pl.pallas_call(kernel, out_shape=outs, in_specs=[pl.BlockSpec(memory_spac...]
    all_to_all x1, starting transfers between devices: 7.41 us -> 6.26 us  [on_device(): lax.all_to_all(pay_1.reshape(3 * parts, 2, 128), 'net', 0, 0, tiled=True)]
    all_to_all x1, waiting for transfers between devices: 4.93 us -> 6.08 us  [on_device(): recv_0 = lax.all_to_all(pay_0, 'net', 0, 0, tiled=True)]
  transfers between devices with their start and end apart: 5 -> 5, of which waited for: 3 -> 3; matrix products, arithmetic and copies ran while one was open for 0% -> 0% of each run, Pallas kernels for 11% -> 10%
where the time goes in v6:
time: 77.5 us; the launch traced here: 76.5 us
  starting transfers between devices  36.9 us (48%)
  waiting for transfers between devices  20.9 us (27%)
  Pallas kernels  16.2 us (21%)
  local copies, waits for them, and re-layouts  1.45 us (2%)
  between operations  0.96 us (1%)
    all_to_all x1, starting transfers between devices, on_device(): recv_setup = lax.all_to_all(pay_setup, 'net', 0, 0, tiled=True)  17.3 us
    pallas_call x6, Pallas kernels, vmem_call(): pl.pallas_call(kernel, out_shape=outs, in_specs=[pl.BlockSpec(memory_spac...  13.9 us
    all_to_all x1, waiting for transfers between devices, on_device(): lax.all_to_all(pay_1.reshape(3 * parts, 2, 128), 'net', 0, 0, tiled=True)  9.7 us
    all_to_all x1, starting transfers between devices, on_device(): recv_0 = lax.all_to_all(pay_0, 'net', 0, 0, tiled=True)  7.43 us
    all_to_all x1, starting transfers between devices, on_device(): lax.all_to_all(pay_1.reshape(3 * parts, 2, 128), 'net', 0, 0, tiled=True)  6.26 us
    all_to_all x1, waiting for transfers between devices, on_device(): recv_0 = lax.all_to_all(pay_0, 'net', 0, 0, tiled=True)  6.08 us
    all_to_all x1, waiting for transfers between devices, on_device(): recv_setup = lax.all_to_all(pay_setup, 'net', 0, 0, tiled=True)  5.14 us
    ppermute x1, starting transfers between devices, on_device(): lax.ppermute(sr[nrow - halo:], 'tm', [(i, i + 1) for i in range(ntm - 1)])  3.96 us
  transfers between devices with their start and end apart: 5, of which 3 were waited for; matrix products, arithmetic and copies ran while one was open for 0% of the time, Pallas kernels for 10%

profile of v6, /device:TPU:1, one launch (start us, length us, event | category | flops | bytes accessed | tf_op | source)
XLA Modules:
  0.0 76.5 jit_solution(15457303306469544800)
XLA Ops:
  0.6 2.3 %shard_map.272 = (f32[64,128]{1,0:T(8,128)}, f32[128,128]{1,0:T(8,128)}) custom-call(s32[1,64]{1,0:T(1,128)} %bitcast.103, s32[1,64]{1,0:T(1,128)} %bitcast.75, s32[1,64]{1,0:T(1,128)} %bitcast.104, f32[1,64]{1,0:T(1,128)} %bitcast.96, f32[1,64]{1,0:T(1,128)} %bitcast.98, f32[1,64]{1,0:T(1,128)} %bitcast.100, s32[1,64]{1,0:T(1,128)} %bitcast.102, ...), custom_call_target="tpu_custom_call" | custom-call | tf_op jit(solution)/shard_map/pallas_call | solution.py:247
  3.0 0.0 copy-start.1
  3.0 17.3 %all-to-all-start = ((f32[64,2,128]{2,1,0:T(2,128)}), f32[64,2,128]{2,1,0:T(2,128)S(1)}, u32[]{:S(2)}, u32[]{:S(2)}) async-start(f32[64,2,128]{2,1,0:T(2,128)} %bitcast.93), calls=%async_computation | async-start | bytes 131072 | tf_op jit(solution)/shard_map/all_to_all | solution.py:254
  20.3 4.0 %collective-permute-start = (f32[32,32]{1,0:T(8,128)S(1)}, f32[32,32]{1,0:T(8,128)S(1)}, u32[]{:S(2)}, u32[]{:S(2)}) collective-permute-start(f32[32,32]{1,0:T(8,128)S(1)} %bitcast.95), channel_id=1, source_target_pairs={{0,1},{1,2},{2,3},{3,4},{4,5},{5,6},{6,7},{8,9},{9,10},{10,11},{11... | collective-permute-start | bytes 12296 | tf_op jit(solution)/shard_map/ppermute | solution.py:201
  24.3 1.9 %collective-permute-start.1 = (f32[32,32]{1,0:T(8,128)S(1)}, f32[32,32]{1,0:T(8,128)S(1)}, u32[]{:S(2)}, u32[]{:S(2)}) collective-permute-start(f32[32,32]{1,0:T(8,128)S(1)} %bitcast.94), channel_id=1, source_target_pairs={{1,0},{2,1},{3,2},{4,3},{5,4},{6,5},{7,6},{9,8},{10,9},{11,10},{12... | collective-permute-start | bytes 12296 | tf_op jit(solution)/shard_map/ppermute | solution.py:202
  26.2 5.1 %all-to-all-done = f32[64,2,128]{2,1,0:T(2,128)S(1)} async-done(((f32[64,2,128]{2,1,0:T(2,128)}), f32[64,2,128]{2,1,0:T(2,128)S(1)}, u32[]{:S(2)}, u32[]{:S(2)}) %all-to-all-start) | async-done | bytes 65568 | tf_op jit(solution)/shard_map/all_to_all | solution.py:254
  31.4 1.0 %shard_map.273 = (f32[128,128]{1,0:T(8,128)S(1)}, f32[128,128]{1,0:T(8,128)}) custom-call(f32[128,128]{1,0:T(8,128)S(1)} %bitcast.57, f32[48,256]{1,0:T(8,128)S(1)} %bitcast.43, f32[48,256]{1,0:T(8,128)S(1)} %bitcast.50), custom_call_target="tpu_custom_call" | custom-call | tf_op jit(solution)/shard_map/pallas_call | solution.py:166
  32.3 7.4 %all-to-all-start.1 = ((f32[64,2,128]{2,1,0:T(2,128)}), f32[64,2,128]{2,1,0:T(2,128)S(1)}, u32[]{:S(2)}, u32[]{:S(2)}) async-start(f32[64,2,128]{2,1,0:T(2,128)} %bitcast.13), calls=%async_computation.1 | async-start | bytes 131072 | tf_op jit(solution)/shard_map/all_to_all | solution.py:268
  39.8 0.0 copy-start.20
  39.8 0.0 copy-start.21
  39.9 0.6 copy-done.23
  40.6 0.0 copy-start.12
  40.6 0.0 copy-start.13
  40.6 0.0 copy-start.15
  40.7 0.5 copy-done.6
  41.2 0.0 copy-done.8
  41.3 0.0 copy-done.11
  41.3 0.0 copy-done.12
  41.3 0.0 copy-done.13
  41.3 0.0 copy-done.15
  41.3 0.0 copy-done.16
  41.3 0.0 copy-done.17
  41.3 0.0 copy-done.18
  41.4 0.0 copy-done.7
  41.4 2.4 %shard_map.275 = (f32[4,48,256]{2,1,0:T(8,128)S(1)}, f32[2,48,256]{2,1,0:T(8,128)S(1)}, f32[10,48,256]{2,1,0:T(8,128)S(1)}, f32[80,32]{1,0:T(8,128)S(1)}, f32[48,32]{1,0:T(8,128)S(1)}) custom-call(f32[48,256]{1,0:T(8,128)S(1)} %bitcast.44, f32[48,256]{1,0:T(8,128)S(1)} %bitcast.51, s32[1,256]{1,0:T(1,128)S(1)} %bitcast.64, s32[1,256]{1,0:T(1,128)S(1)} %bitcast.67, ...), custom_call_target="tpu_custom_call" | custom-call | tf_op jit(solution)/shard_map/pallas_call | solution.py:166
  43.8 1.4 %shard_map.274 = (f32[4,48,256]{2,1,0:T(8,128)S(1)}, f32[10,48,128]{2,1,0:T(8,128)S(1)}, f32[8,256]{1,0:T(8,128)S(1)}) custom-call(f32[128,128]{1,0:T(8,128)S(1)} %get-tuple-element.29.mirror_ref.refs_6_, f32[48,256]{1,0:T(8,128)S(1)} %bitcast.45, f32[48,256]{1,0:T(8,128)S(1)} %bitcast.52, s32[1,256]{1,0:T(1,128)S(1)} %bitcast.65, s32[1,256]{1,0:T(1,128)S(1)} %bitcast.68, ...), custom_call_target="tpu_custom_call" | custom-call | tf_op jit(solution)/shard_map/pallas_call | solution.py:166
  45.3 6.1 %all-to-all-done.1 = f32[64,2,128]{2,1,0:T(2,128)S(1)} async-done(((f32[64,2,128]{2,1,0:T(2,128)}), f32[64,2,128]{2,1,0:T(2,128)S(1)}, u32[]{:S(2)}, u32[]{:S(2)}) %all-to-all-start.1) | async-done | bytes 65568 | tf_op jit(solution)/shard_map/all_to_all | solution.py:268
  51.4 2.9 %shard_map.276 = (f32[10,48,64]{2,1,0:T(8,128)S(1)}, f32[4,48,256]{2,1,0:T(8,128)S(1)}, f32[384,128]{1,0:T(8,128)}) custom-call(f32[48,256]{1,0:T(8,128)S(1)} %bitcast.46, f32[48,256]{1,0:T(8,128)S(1)} %bitcast.47, f32[48,256]{1,0:T(8,128)S(1)} %bitcast.53, f32[48,256]{1,0:T(8,128)S(1)} %bitcast.58, f32[48,256]{1,0:T(8,128)S(1)} %bitcast.60, ...), custom_call_target="tpu_custom_call" | custom-call | tf_op jit(solution)/shard_map/pallas_call | solution.py:166
  54.3 6.3 %all-to-all-start.2 = ((f32[192,2,128]{2,1,0:T(2,128)}), f32[192,2,128]{2,1,0:T(2,128)S(1)}, u32[]{:S(2)}, u32[]{:S(2)}) async-start(f32[192,2,128]{2,1,0:T(2,128)} %bitcast.33), calls=%async_computation.2 | async-start | bytes 393216 | tf_op jit(solution)/shard_map/all_to_all | solution.py:432
  60.5 2.9 %shard_map.277 = (f32[4,48,256]{2,1,0:T(8,128)S(1)}, f32[2,48,256]{2,1,0:T(8,128)S(1)}, f32[48,32]{1,0:T(8,128)}, f32[48,32]{1,0:T(8,128)}) custom-call(f32[4,48,256]{2,1,0:T(8,128)S(1)} %get-tuple-element.35.refs_0_, s32[1,256]{1,0:T(1,128)S(1)} %bitcast.66, s32[1,256]{1,0:T(1,128)S(1)} %bitcast.69, f32[1,256]{1,0:T(1,128)S(1)} %bitcast.78, ...), custom_call_target="tpu_custom_call" | custom-call | tf_op jit(solution)/shard_map/pallas_call | solution.py:166
  63.5 9.7 %all-to-all-done.2 = f32[192,2,128]{2,1,0:T(2,128)S(1)} async-done(((f32[192,2,128]{2,1,0:T(2,128)}), f32[192,2,128]{2,1,0:T(2,128)S(1)}, u32[]{:S(2)}, u32[]{:S(2)}) %all-to-all-start.2) | async-done | bytes 196640 | tf_op jit(solution)/shard_map/all_to_all | solution.py:432
  73.2 3.3 %shard_map.278 = (f32[48,256]{1,0:T(8,128)}, f32[48,256]{1,0:T(8,128)}, f32[48,256]{1,0:T(8,128)}) custom-call(f32[4,48,256]{2,1,0:T(8,128)S(1)} %get-tuple-element.35.refs_0_, f32[48,256]{1,0:T(8,128)S(1)} %bitcast.48, f32[48,256]{1,0:T(8,128)S(1)} %bitcast.54, f32[48,256]{1,0:T(8,128)S(1)} %bitcast.59, f32[48,256]{1,0:T(8,128)S(1)} %bitcast.61, ...), custom_call_target="tpu_custom_call" | custom-call | tf_op jit(solution)/shard_map/pallas_call | solution.py:166
  (39 shorter events, 0.1 us)
Async XLA Ops:
  3.0 17.3 %copy-start.4 = (f32[3,16,32]{2,1,0:T(8,128)S(1)}, f32[3,16,32]{2,1,0:T(8,128)}, u32[]{:S(2)}) copy-start(f32[3,16,32]{2,1,0:T(8,128)} %param.29) | copy-start | bytes 18436
  3.0 28.4 %copy-start.1 = (f32[3,16,256]{2,1,0:T(8,128)S(1)}, f32[3,16,256]{2,1,0:T(8,128)}, u32[]{:S(2)}) copy-start(f32[3,16,256]{2,1,0:T(8,128)} %param.26) | copy-start | bytes 147460
  3.0 28.4 %all-to-all-start = ((f32[64,2,128]{2,1,0:T(2,128)}), f32[64,2,128]{2,1,0:T(2,128)S(1)}, u32[]{:S(2)}, u32[]{:S(2)}) async-start(f32[64,2,128]{2,1,0:T(2,128)} %bitcast.93), calls=%async_computation | async-start | bytes 131072 | tf_op jit(solution)/shard_map/all_to_all | solution.py:254
  20.3 11.1 %copy-start = (f32[3,16,256]{2,1,0:T(8,128)S(1)}, f32[3,16,256]{2,1,0:T(8,128)}, u32[]{:S(2)}) copy-start(f32[3,16,256]{2,1,0:T(8,128)} %param.25) | copy-start | bytes 147460
  20.3 20.2 %collective-permute-start = (f32[32,32]{1,0:T(8,128)S(1)}, f32[32,32]{1,0:T(8,128)S(1)}, u32[]{:S(2)}, u32[]{:S(2)}) collective-permute-start(f32[32,32]{1,0:T(8,128)S(1)} %bitcast.95), channel_id=1, source_target_pairs={{0,1},{1,2},{2,3},{3,4},{4,5},{5,6},{6,7},{8,9},{9,10},{10,11},{11... | collective-permute-start | bytes 12296 | tf_op jit(solution)/shard_map/ppermute | solution.py:201
  24.3 16.3 %collective-permute-start.1 = (f32[32,32]{1,0:T(8,128)S(1)}, f32[32,32]{1,0:T(8,128)S(1)}, u32[]{:S(2)}, u32[]{:S(2)}) collective-permute-start(f32[32,32]{1,0:T(8,128)S(1)} %bitcast.94), channel_id=1, source_target_pairs={{1,0},{2,1},{3,2},{4,3},{5,4},{6,5},{7,6},{9,8},{10,9},{11,10},{12... | collective-permute-start | bytes 12296 | tf_op jit(solution)/shard_map/ppermute | solution.py:202
  32.3 7.4 %copy-start.10 = (s32[64]{0:T(128)S(1)}, s32[64]{0:T(128)}, u32[]{:S(2)}) copy-start(s32[64]{0:T(128)} %param.43) | copy-start | bytes 772
  32.3 7.5 %copy-start.22 = (s32[64]{0:T(128)S(1)}, s32[64]{0:T(128)}, u32[]{:S(2)}) copy-start(s32[64]{0:T(128)} %param.49) | copy-start | bytes 772
  32.3 19.0 %all-to-all-start.1 = ((f32[64,2,128]{2,1,0:T(2,128)}), f32[64,2,128]{2,1,0:T(2,128)S(1)}, u32[]{:S(2)}, u32[]{:S(2)}) async-start(f32[64,2,128]{2,1,0:T(2,128)} %bitcast.13), calls=%async_computation.1 | async-start | bytes 131072 | tf_op jit(solution)/shard_map/all_to_all | solution.py:268
  39.8 0.7 copy-start.23
  39.8 0.7 copy-start.19
  39.8 0.7 copy-start.20
  39.8 0.7 copy-start.21
  40.5 0.7 copy-start.6
  40.6 0.7 copy-start.8
  40.6 0.7 copy-start.11
  40.6 0.7 copy-start.12
  40.6 0.7 copy-start.13
  40.6 0.7 copy-start.14
  40.6 0.7 copy-start.15
  40.6 0.7 copy-start.16
  40.7 0.7 copy-start.17
  40.7 0.7 copy-start.18
  40.7 0.7 copy-start.7
  40.7 0.7 copy-start.9
  43.8 7.6 %copy-start.2 = (f32[3,16,256]{2,1,0:T(8,128)S(1)}, f32[3,16,256]{2,1,0:T(8,128)}, u32[]{:S(2)}) copy-start(f32[3,16,256]{2,1,0:T(8,128)} %param.27) | copy-start | bytes 147460
  43.8 7.6 %copy-start.3 = (f32[3,16,256]{2,1,0:T(8,128)S(1)}, f32[3,16,256]{2,1,0:T(8,128)}, u32[]{:S(2)}) copy-start(f32[3,16,256]{2,1,0:T(8,128)} %param.28) | copy-start | bytes 147460
  43.8 7.5 %copy-start.5 = (f32[64,128]{1,0:T(8,128)S(1)}, f32[64,128]{1,0:T(8,128)}, u32[]{:S(2)}) copy-start(f32[64,128]{1,0:T(8,128)} %get-tuple-element.30.refs_7_) | copy-start | bytes 98308
  54.3 18.9 %all-to-all-start.2 = ((f32[192,2,128]{2,1,0:T(2,128)}), f32[192,2,128]{2,1,0:T(2,128)S(1)}, u32[]{:S(2)}, u32[]{:S(2)}) async-start(f32[192,2,128]{2,1,0:T(2,128)} %bitcast.33), calls=%async_computation.2 | async-start | bytes 393216 | tf_op jit(solution)/shard_map/all_to_all | solution.py:432

commit v7 on v6

--- a/solution.py
+++ b/solution.py
@@ -162,12 +162,13 @@
     return tuple(a[i * n:(i + 1) * n] for i in range(4))
 
 
-def vmem_call(kernel, outs, *args):
+def vmem_call(kernel, outs, *args, scratch=()):
     return pl.pallas_call(
         kernel,
         out_shape=outs,
         in_specs=[pl.BlockSpec(memory_space=pltpu.VMEM)] * len(args),
         out_specs=tuple(pl.BlockSpec(memory_space=pltpu.VMEM) for _ in outs),
+        scratch_shapes=scratch,
         compiler_params=pltpu.CompilerParams(vmem_limit_bytes=48 * 1024 * 1024),
     )(*args)
 
@@ -362,7 +363,7 @@
         gen_count = dg_ref[1:2]
         prm_cut = (cprm_v[1:2], cprm_v[2:3], cprm_v[3:4], cprm_v[4:5])
         if first:
-            (cc_out, st_out, pay_out) = rest
+            (cc_out, st_out, pay_out, plane_ref) = rest
             zero_b = jnp.zeros((nrow, buses), F32)
             state = (wmv, wav, zero_b, zero_b)
             far_slot = recv_ref[...].T
@@ -374,10 +375,14 @@
             carry_c, fc, _ = advance(None, pick_near, far_cross, prm_cut)
             totals = tin_ref[...] + tm_ref[...] + give(fc, inc_near).reshape(4, nrow, buses)
         else:
-            (cc_in_ref, cm_ref, mag_out, ang_out, pr_out) = rest
+            (cc_in_ref, cm_ref, mag_out, ang_out, pr_out, plane_ref) = rest
             state = tuple(st_ref[i] for i in range(4))
-            got = recv_ref[...]
-            both = rows(*(take_left(spread(p).T, got).T for p in range(3)))
+            blocks = []
+            for p in range(3):
+                for k in range(cap):
+                    plane_ref[pl.ds(k, parts, stride=cap), :] = recv_ref[pl.ds(p * cap + k, parts, stride=3 * cap), :]
+                blocks.append(plane_ref[...].T)
+            both = rows(*blocks)
             near_mirror = split4(both[0:4 * nrow], nrow)
             far_cross = split4(give(both[4 * nrow:], slot_t), nrow)
             stack = rows(*state)
@@ -403,7 +408,10 @@
             new_stack = rows(mag, ang, pr, pq)
             near_slot = dot(inc_near, slot_t, NN).astype(BF)
             vals = rows(take(new_stack, near_slot), take(new_stack, inc_recv))
-            pay_out[...] = sum(give_left(spread(p), vals[p * 128:(p + 1) * 128]) for p in range(3))
+            for p in range(3):
+                plane_ref[...] = vals[p * 128:(p + 1) * 128].T
+                for k in range(cap):
+                    pay_out[pl.ds(p * cap + k, parts, stride=3 * cap), :] = plane_ref[pl.ds(k, parts, stride=cap), :]
         else:
             mag_out[...] = mag
             ang_out[...] = ang
@@ -428,6 +436,7 @@
         lambda *refs: cut_part(True, refs),
         (sds((10, nrow, cuts), F32), tot_shape, sds((3 * slots, 128), F32)),
         wm, wm, wa, lr, lq, recv_0, mirror_t, slot_t, dg, cprm, tin0, sup0, tm0,
+        scratch=[pltpu.VMEM((slots, 128), F32)],
     )
     recv_1 = lax.all_to_all(pay_1.reshape(3 * parts, 2, 128), "net", 0, 0, tiled=True).reshape(3 * slots, 128)
     tin1, sup1, gr, gq = vmem_call(
@@ -440,6 +449,7 @@
         (sds((nrow, buses), F32), sds((nrow, buses), F32), sds((nrow, buses), F32)),
         st1, wm, wa, lr, lq, recv_1, mirror_t, slot_t, dg, cprm, tin1, sup1, tin1,
         cc1, cm1,
+        scratch=[pltpu.VMEM((slots, 128), F32)],
     )
     shape_b = (periods, scen, buses)
     shape_g = (periods, scen, gens)

time: 77.5 us -> 76.5 us (0.987)
  Pallas kernels: 16.2 us -> 15.3 us
    pallas_call x6, Pallas kernels: 13.9 us -> 12.9 us  [vmem_call(): pl.pallas_call(kernel, out_shape=outs, in_specs=[pl.BlockSpec(memory_spac...]
where the time goes in v7:
time: 76.5 us; the launch traced here: 75.5 us
  starting transfers between devices  36.9 us (48%)
  waiting for transfers between devices  20.9 us (27%)
  Pallas kernels  15.3 us (20%)
  local copies, waits for them, and re-layouts  1.45 us (2%)
  between operations  0.96 us (1%)
    all_to_all x1, starting transfers between devices, on_device(): recv_setup = lax.all_to_all(pay_setup, 'net', 0, 0, tiled=True)  17.3 us
    pallas_call x6, Pallas kernels, vmem_call(): pl.pallas_call(kernel, out_shape=outs, in_specs=[pl.BlockSpec(memory_spac...  12.9 us
    all_to_all x1, waiting for transfers between devices, on_device(): lax.all_to_all(pay_1.reshape(3 * parts, 2, 128), 'net', 0, 0, tiled=True)  9.71 us
    all_to_all x1, starting transfers between devices, on_device(): recv_0 = lax.all_to_all(pay_0, 'net', 0, 0, tiled=True)  7.43 us
    all_to_all x1, starting transfers between devices, on_device(): lax.all_to_all(pay_1.reshape(3 * parts, 2, 128), 'net', 0, 0, tiled=True)  6.26 us
    all_to_all x1, waiting for transfers between devices, on_device(): recv_0 = lax.all_to_all(pay_0, 'net', 0, 0, tiled=True)  6.08 us
    all_to_all x1, waiting for transfers between devices, on_device(): recv_setup = lax.all_to_all(pay_setup, 'net', 0, 0, tiled=True)  5.14 us
    ppermute x1, starting transfers between devices, on_device(): lax.ppermute(sr[nrow - halo:], 'tm', [(i, i + 1) for i in range(ntm - 1)])  3.96 us
  transfers between devices with their start and end apart: 5, of which 3 were waited for; matrix products, arithmetic and copies ran while one was open for 0% of the time, Pallas kernels for 10%

profile of v7, /device:TPU:1, one launch (start us, length us, event | category | flops | bytes accessed | tf_op | source)
XLA Modules:
  0.0 75.5 jit_solution(2808004384870965788)
XLA Ops:
  0.6 2.3 %shard_map.272 = (f32[64,128]{1,0:T(8,128)}, f32[128,128]{1,0:T(8,128)}) custom-call(s32[1,64]{1,0:T(1,128)} %bitcast.103, s32[1,64]{1,0:T(1,128)} %bitcast.75, s32[1,64]{1,0:T(1,128)} %bitcast.104, f32[1,64]{1,0:T(1,128)} %bitcast.96, f32[1,64]{1,0:T(1,128)} %bitcast.98, f32[1,64]{1,0:T(1,128)} %bitcast.100, s32[1,64]{1,0:T(1,128)} %bitcast.102, ...), custom_call_target="tpu_custom_call" | custom-call | tf_op jit(solution)/shard_map/pallas_call | solution.py:248
  3.0 0.0 copy-start.1
  3.0 17.3 %all-to-all-start = ((f32[64,2,128]{2,1,0:T(2,128)}), f32[64,2,128]{2,1,0:T(2,128)S(1)}, u32[]{:S(2)}, u32[]{:S(2)}) async-start(f32[64,2,128]{2,1,0:T(2,128)} %bitcast.93), calls=%async_computation | async-start | bytes 131072 | tf_op jit(solution)/shard_map/all_to_all | solution.py:255
  20.3 4.0 %collective-permute-start = (f32[32,32]{1,0:T(8,128)S(1)}, f32[32,32]{1,0:T(8,128)S(1)}, u32[]{:S(2)}, u32[]{:S(2)}) collective-permute-start(f32[32,32]{1,0:T(8,128)S(1)} %bitcast.95), channel_id=1, source_target_pairs={{0,1},{1,2},{2,3},{3,4},{4,5},{5,6},{6,7},{8,9},{9,10},{10,11},{11... | collective-permute-start | bytes 12296 | tf_op jit(solution)/shard_map/ppermute | solution.py:202
  24.3 1.9 %collective-permute-start.1 = (f32[32,32]{1,0:T(8,128)S(1)}, f32[32,32]{1,0:T(8,128)S(1)}, u32[]{:S(2)}, u32[]{:S(2)}) collective-permute-start(f32[32,32]{1,0:T(8,128)S(1)} %bitcast.94), channel_id=1, source_target_pairs={{1,0},{2,1},{3,2},{4,3},{5,4},{6,5},{7,6},{9,8},{10,9},{11,10},{12... | collective-permute-start | bytes 12296 | tf_op jit(solution)/shard_map/ppermute | solution.py:203
  26.2 5.1 %all-to-all-done = f32[64,2,128]{2,1,0:T(2,128)S(1)} async-done(((f32[64,2,128]{2,1,0:T(2,128)}), f32[64,2,128]{2,1,0:T(2,128)S(1)}, u32[]{:S(2)}, u32[]{:S(2)}) %all-to-all-start) | async-done | bytes 65568 | tf_op jit(solution)/shard_map/all_to_all | solution.py:255
  31.4 1.0 %shard_map.273 = (f32[128,128]{1,0:T(8,128)S(1)}, f32[128,128]{1,0:T(8,128)}) custom-call(f32[128,128]{1,0:T(8,128)S(1)} %bitcast.57, f32[48,256]{1,0:T(8,128)S(1)} %bitcast.43, f32[48,256]{1,0:T(8,128)S(1)} %bitcast.50), custom_call_target="tpu_custom_call" | custom-call | tf_op jit(solution)/shard_map/pallas_call | solution.py:166
  32.3 7.4 %all-to-all-start.1 = ((f32[64,2,128]{2,1,0:T(2,128)}), f32[64,2,128]{2,1,0:T(2,128)S(1)}, u32[]{:S(2)}, u32[]{:S(2)}) async-start(f32[64,2,128]{2,1,0:T(2,128)} %bitcast.13), calls=%async_computation.1 | async-start | bytes 131072 | tf_op jit(solution)/shard_map/all_to_all | solution.py:269
  39.8 0.0 copy-start.20
  39.8 0.0 copy-start.21
  39.9 0.6 copy-done.23
  40.6 0.0 copy-start.12
  40.6 0.0 copy-start.13
  40.6 0.0 copy-start.15
  40.7 0.5 copy-done.6
  41.2 0.0 copy-done.8
  41.3 0.0 copy-done.11
  41.3 0.0 copy-done.12
  41.3 0.0 copy-done.13
  41.3 0.0 copy-done.15
  41.3 0.0 copy-done.16
  41.3 0.0 copy-done.17
  41.3 0.0 copy-done.18
  41.4 0.0 copy-done.7
  41.4 2.4 %shard_map.275 = (f32[4,48,256]{2,1,0:T(8,128)S(1)}, f32[2,48,256]{2,1,0:T(8,128)S(1)}, f32[10,48,256]{2,1,0:T(8,128)S(1)}, f32[80,32]{1,0:T(8,128)S(1)}, f32[48,32]{1,0:T(8,128)S(1)}) custom-call(f32[48,256]{1,0:T(8,128)S(1)} %bitcast.44, f32[48,256]{1,0:T(8,128)S(1)} %bitcast.51, s32[1,256]{1,0:T(1,128)S(1)} %bitcast.64, s32[1,256]{1,0:T(1,128)S(1)} %bitcast.67, ...), custom_call_target="tpu_custom_call" | custom-call | tf_op jit(solution)/shard_map/pallas_call | solution.py:166
  43.8 1.4 %shard_map.274 = (f32[4,48,256]{2,1,0:T(8,128)S(1)}, f32[10,48,128]{2,1,0:T(8,128)S(1)}, f32[8,256]{1,0:T(8,128)S(1)}) custom-call(f32[128,128]{1,0:T(8,128)S(1)} %get-tuple-element.29.mirror_ref.refs_6_, f32[48,256]{1,0:T(8,128)S(1)} %bitcast.45, f32[48,256]{1,0:T(8,128)S(1)} %bitcast.52, s32[1,256]{1,0:T(1,128)S(1)} %bitcast.65, s32[1,256]{1,0:T(1,128)S(1)} %bitcast.68, ...), custom_call_target="tpu_custom_call" | custom-call | tf_op jit(solution)/shard_map/pallas_call | solution.py:166
  45.3 6.1 %all-to-all-done.1 = f32[64,2,128]{2,1,0:T(2,128)S(1)} async-done(((f32[64,2,128]{2,1,0:T(2,128)}), f32[64,2,128]{2,1,0:T(2,128)S(1)}, u32[]{:S(2)}, u32[]{:S(2)}) %all-to-all-start.1) | async-done | bytes 65568 | tf_op jit(solution)/shard_map/all_to_all | solution.py:269
  51.4 2.5 %shard_map.276 = (f32[10,48,64]{2,1,0:T(8,128)S(1)}, f32[4,48,256]{2,1,0:T(8,128)S(1)}, f32[384,128]{1,0:T(8,128)}) custom-call(f32[48,256]{1,0:T(8,128)S(1)} %bitcast.46, f32[48,256]{1,0:T(8,128)S(1)} %bitcast.47, f32[48,256]{1,0:T(8,128)S(1)} %bitcast.53, f32[48,256]{1,0:T(8,128)S(1)} %bitcast.58, f32[48,256]{1,0:T(8,128)S(1)} %bitcast.60, ...), custom_call_target="tpu_custom_call" | custom-call | tf_op jit(solution)/shard_map/pallas_call | solution.py:166
  53.8 6.3 %all-to-all-start.2 = ((f32[192,2,128]{2,1,0:T(2,128)}), f32[192,2,128]{2,1,0:T(2,128)S(1)}, u32[]{:S(2)}, u32[]{:S(2)}) async-start(f32[192,2,128]{2,1,0:T(2,128)} %bitcast.33), calls=%async_computation.2 | async-start | bytes 393216 | tf_op jit(solution)/shard_map/all_to_all | solution.py:441
  60.1 2.9 %shard_map.277 = (f32[4,48,256]{2,1,0:T(8,128)S(1)}, f32[2,48,256]{2,1,0:T(8,128)S(1)}, f32[48,32]{1,0:T(8,128)}, f32[48,32]{1,0:T(8,128)}) custom-call(f32[4,48,256]{2,1,0:T(8,128)S(1)} %get-tuple-element.35.refs_0_, s32[1,256]{1,0:T(1,128)S(1)} %bitcast.66, s32[1,256]{1,0:T(1,128)S(1)} %bitcast.69, f32[1,256]{1,0:T(1,128)S(1)} %bitcast.78, ...), custom_call_target="tpu_custom_call" | custom-call | tf_op jit(solution)/shard_map/pallas_call | solution.py:166
  63.0 9.7 %all-to-all-done.2 = f32[192,2,128]{2,1,0:T(2,128)S(1)} async-done(((f32[192,2,128]{2,1,0:T(2,128)}), f32[192,2,128]{2,1,0:T(2,128)S(1)}, u32[]{:S(2)}, u32[]{:S(2)}) %all-to-all-start.2) | async-done | bytes 196640 | tf_op jit(solution)/shard_map/all_to_all | solution.py:441
  72.8 2.7 %shard_map.278 = (f32[48,256]{1,0:T(8,128)}, f32[48,256]{1,0:T(8,128)}, f32[48,256]{1,0:T(8,128)}) custom-call(f32[4,48,256]{2,1,0:T(8,128)S(1)} %get-tuple-element.35.refs_0_, f32[48,256]{1,0:T(8,128)S(1)} %bitcast.48, f32[48,256]{1,0:T(8,128)S(1)} %bitcast.54, f32[48,256]{1,0:T(8,128)S(1)} %bitcast.59, f32[48,256]{1,0:T(8,128)S(1)} %bitcast.61, ...), custom_call_target="tpu_custom_call" | custom-call | tf_op jit(solution)/shard_map/pallas_call | solution.py:166
  (39 shorter events, 0.1 us)
Async XLA Ops:
  3.0 17.3 %copy-start.4 = (f32[3,16,32]{2,1,0:T(8,128)S(1)}, f32[3,16,32]{2,1,0:T(8,128)}, u32[]{:S(2)}) copy-start(f32[3,16,32]{2,1,0:T(8,128)} %param.29) | copy-start | bytes 18436
  3.0 28.4 %copy-start.1 = (f32[3,16,256]{2,1,0:T(8,128)S(1)}, f32[3,16,256]{2,1,0:T(8,128)}, u32[]{:S(2)}) copy-start(f32[3,16,256]{2,1,0:T(8,128)} %param.26) | copy-start | bytes 147460
  3.0 28.4 %all-to-all-start = ((f32[64,2,128]{2,1,0:T(2,128)}), f32[64,2,128]{2,1,0:T(2,128)S(1)}, u32[]{:S(2)}, u32[]{:S(2)}) async-start(f32[64,2,128]{2,1,0:T(2,128)} %bitcast.93), calls=%async_computation | async-start | bytes 131072 | tf_op jit(solution)/shard_map/all_to_all | solution.py:255
  20.3 11.1 %copy-start = (f32[3,16,256]{2,1,0:T(8,128)S(1)}, f32[3,16,256]{2,1,0:T(8,128)}, u32[]{:S(2)}) copy-start(f32[3,16,256]{2,1,0:T(8,128)} %param.25) | copy-start | bytes 147460
  20.3 20.2 %collective-permute-start = (f32[32,32]{1,0:T(8,128)S(1)}, f32[32,32]{1,0:T(8,128)S(1)}, u32[]{:S(2)}, u32[]{:S(2)}) collective-permute-start(f32[32,32]{1,0:T(8,128)S(1)} %bitcast.95), channel_id=1, source_target_pairs={{0,1},{1,2},{2,3},{3,4},{4,5},{5,6},{6,7},{8,9},{9,10},{10,11},{11... | collective-permute-start | bytes 12296 | tf_op jit(solution)/shard_map/ppermute | solution.py:202
  24.3 16.3 %collective-permute-start.1 = (f32[32,32]{1,0:T(8,128)S(1)}, f32[32,32]{1,0:T(8,128)S(1)}, u32[]{:S(2)}, u32[]{:S(2)}) collective-permute-start(f32[32,32]{1,0:T(8,128)S(1)} %bitcast.94), channel_id=1, source_target_pairs={{1,0},{2,1},{3,2},{4,3},{5,4},{6,5},{7,6},{9,8},{10,9},{11,10},{12... | collective-permute-start | bytes 12296 | tf_op jit(solution)/shard_map/ppermute | solution.py:203
  32.3 7.4 %copy-start.10 = (s32[64]{0:T(128)S(1)}, s32[64]{0:T(128)}, u32[]{:S(2)}) copy-start(s32[64]{0:T(128)} %param.43) | copy-start | bytes 772
  32.3 7.5 %copy-start.22 = (s32[64]{0:T(128)S(1)}, s32[64]{0:T(128)}, u32[]{:S(2)}) copy-start(s32[64]{0:T(128)} %param.49) | copy-start | bytes 772
  32.3 19.0 %all-to-all-start.1 = ((f32[64,2,128]{2,1,0:T(2,128)}), f32[64,2,128]{2,1,0:T(2,128)S(1)}, u32[]{:S(2)}, u32[]{:S(2)}) async-start(f32[64,2,128]{2,1,0:T(2,128)} %bitcast.13), calls=%async_computation.1 | async-start | bytes 131072 | tf_op jit(solution)/shard_map/all_to_all | solution.py:269
  39.8 0.7 copy-start.23
  39.8 0.7 copy-start.19
  39.8 0.7 copy-start.20
  39.8 0.7 copy-start.21
  40.5 0.7 copy-start.6
  40.6 0.7 copy-start.8
  40.6 0.7 copy-start.11
  40.6 0.7 copy-start.12
  40.6 0.7 copy-start.13
  40.6 0.7 copy-start.14
  40.6 0.7 copy-start.15
  40.6 0.7 copy-start.16
  40.7 0.7 copy-start.17
  40.7 0.7 copy-start.18
  40.7 0.7 copy-start.7
  40.7 0.7 copy-start.9
  43.8 7.6 %copy-start.2 = (f32[3,16,256]{2,1,0:T(8,128)S(1)}, f32[3,16,256]{2,1,0:T(8,128)}, u32[]{:S(2)}) copy-start(f32[3,16,256]{2,1,0:T(8,128)} %param.27) | copy-start | bytes 147460
  43.8 7.6 %copy-start.3 = (f32[3,16,256]{2,1,0:T(8,128)S(1)}, f32[3,16,256]{2,1,0:T(8,128)}, u32[]{:S(2)}) copy-start(f32[3,16,256]{2,1,0:T(8,128)} %param.28) | copy-start | bytes 147460
  43.8 7.5 %copy-start.5 = (f32[64,128]{1,0:T(8,128)S(1)}, f32[64,128]{1,0:T(8,128)}, u32[]{:S(2)}) copy-start(f32[64,128]{1,0:T(8,128)} %get-tuple-element.30.refs_7_) | copy-start | bytes 98308
  53.8 18.9 %all-to-all-start.2 = ((f32[192,2,128]{2,1,0:T(2,128)}), f32[192,2,128]{2,1,0:T(2,128)S(1)}, u32[]{:S(2)}, u32[]{:S(2)}) async-start(f32[192,2,128]{2,1,0:T(2,128)} %bitcast.33), calls=%async_computation.2 | async-start | bytes 393216 | tf_op jit(solution)/shard_map/all_to_all | solution.py:441

commit v8 on v7

--- a/solution.py
+++ b/solution.py
@@ -28,6 +28,11 @@
 
 def dot(a, b, dims):
     return lax.dot_general(a, b, dims, preferred_element_type=F32)
+
+
+def take_split(parts, oh):
+    hi, mid, lo = parts
+    return (dot(hi, oh, NN) + dot(mid, oh, NN)) + dot(lo, oh, NN)
 
 
 def take(vals, oh):
@@ -221,8 +226,7 @@
         copies = [pltpu.make_async_copy(src, dst, sems.at[i]) for i, (src, dst) in enumerate(pairs)]
         for cp in copies:
             cp.start()
-        for cp in copies:
-            cp.wait()
+        copies[0].wait()
         peer = peer_ref[...]
         mine_t = (lax.broadcasted_iota(jnp.int32, (parts, cuts), 0) == peer).astype(F32)
         same = dot(mine_t.T.astype(BF), mine_t.astype(BF), NN)
@@ -232,8 +236,11 @@
         slot_t = (lax.broadcasted_iota(jnp.int32, (slots, cuts), 0).astype(F32) == position).astype(F32).T
         slot_b = slot_t.astype(BF)
         slot_out[...] = slot_t
+        copies[1].wait()
         inc_near = onehot(near_ref[...], buses)
         by_slot = dot(inc_near, slot_b, NN).astype(BF)
+        for cp in copies[2:]:
+            cp.wait()
         prm = rows(bus_ref[...].astype(F32) + 1.0, cond_ref[...], susc_ref[...], lim_ref[...],
                    steps_ref[...].astype(F32), jnp.zeros((3, cuts), F32))
         vals = rows(
@@ -284,16 +291,19 @@
         else:
             (st_ref, bf_ref, bt_ref, bc_ref, bs_ref, bl_ref, bn_ref,
              gb_ref, gl_ref, gq_ref, gr_ref, gcr_ref, gcq_ref, pe_ref,
-             ci_ref, g0_ref, gq0_ref,
-             tot_out, sup_out, gr_out, gq_out) = refs
+             ci_ref, g0_ref, gq0_ref, cp_ref, mir_ref,
+             tot_out, sup_out, gr_out, gq_out, pn_out, prc_out) = refs
             state = tuple(st_ref[i] for i in range(4))
             carry_in = load_carry(ci_ref)
         inc_from = onehot(bf_ref[...], buses)
         inc_to = onehot(bt_ref[...], buses)
         inc_gen = onehot(gb_ref[...], buses)
-        stack = rows(*state)
-        pick_from = split4(take(stack, inc_from), nrow)
-        pick_to = split4(take(stack, inc_to), nrow)
+        stack = split3(rows(*state))
+        pick_from = split4(take_split(stack, inc_from), nrow)
+        pick_to = split4(take_split(stack, inc_to), nrow)
+        if not first:
+            pn_out[...] = take_split(stack, onehot(cp_ref[0:1].astype(jnp.int32), buses))
+            prc_out[...] = take_split(stack, onehot(mir_ref[0:1].astype(jnp.int32) - 1, buses))
         prm_in = (bc_ref[...], bs_ref[...], bl_ref[...], bn_ref[...])
         carry_i, fi, ti = advance(carry_in, pick_from, pick_to, prm_in)
         totals = give(fi, inc_from) + give(ti, inc_to)
@@ -375,7 +385,7 @@
             carry_c, fc, _ = advance(None, pick_near, far_cross, prm_cut)
             totals = tin_ref[...] + tm_ref[...] + give(fc, inc_near).reshape(4, nrow, buses)
         else:
-            (cc_in_ref, cm_ref, mag_out, ang_out, pr_out, plane_ref) = rest
+            (cc_in_ref, cm_ref, pn_ref, prc_ref, mag_out, ang_out, pr_out, plane_ref) = rest
             state = tuple(st_ref[i] for i in range(4))
             blocks = []
             for p in range(3):
@@ -385,9 +395,8 @@
             both = rows(*blocks)
             near_mirror = split4(both[0:4 * nrow], nrow)
             far_cross = split4(give(both[4 * nrow:], slot_t), nrow)
-            stack = rows(*state)
-            pick_near = split4(take(stack, inc_near), nrow)
-            pick_recv = split4(take(stack, inc_recv), nrow)
+            pick_near = split4(pn_ref[...], nrow)
+            pick_recv = split4(prc_ref[...], nrow)
             carry_c_in = load_carry(cc_in_ref)
             carry_m_in = load_carry(cm_ref)
             _, fc, _ = advance(carry_c_in, pick_near, far_cross, prm_cut)
@@ -439,16 +448,17 @@
         scratch=[pltpu.VMEM((slots, 128), F32)],
     )
     recv_1 = lax.all_to_all(pay_1.reshape(3 * parts, 2, 128), "net", 0, 0, tiled=True).reshape(3 * slots, 128)
-    tin1, sup1, gr, gq = vmem_call(
+    tin1, sup1, gr, gq, pn1, prc1 = vmem_call(
         lambda *refs: local_part(False, refs),
-        (tot_shape, sds((2, nrow, buses), F32), sds((nrow, gens), F32), sds((nrow, gens), F32)),
-        st1, *br_all, *gen_all, ci1, g0, gq0,
+        (tot_shape, sds((2, nrow, buses), F32), sds((nrow, gens), F32), sds((nrow, gens), F32),
+         sds((4 * nrow, cuts), F32), sds((4 * nrow, slots), F32)),
+        st1, *br_all, *gen_all, ci1, g0, gq0, cprm, mirror_t,
     )
     mag, ang, pr = vmem_call(
         lambda *refs: cut_part(False, refs),
         (sds((nrow, buses), F32), sds((nrow, buses), F32), sds((nrow, buses), F32)),
         st1, wm, wa, lr, lq, recv_1, mirror_t, slot_t, dg, cprm, tin1, sup1, tin1,
-        cc1, cm1,
+        cc1, cm1, pn1, prc1,
         scratch=[pltpu.VMEM((slots, 128), F32)],
     )
     shape_b = (periods, scen, buses)

time: 76.5 us -> 76.1 us (level)
  no operation moved by 1% of the time
where the time goes in v8:
time: 76.1 us; the launch traced here: 75.1 us
  starting transfers between devices  36.9 us (48%)
  waiting for transfers between devices  20.9 us (27%)
  Pallas kernels  14.8 us (19%)
  local copies, waits for them, and re-layouts  1.45 us (2%)
  between operations  0.96 us (1%)
    all_to_all x1, starting transfers between devices, on_device(): recv_setup = lax.all_to_all(pay_setup, 'net', 0, 0, tiled=True)  17.3 us
    pallas_call x6, Pallas kernels, vmem_call(): pl.pallas_call(kernel, out_shape=outs, in_specs=[pl.BlockSpec(memory_spac...  12.7 us
    all_to_all x1, waiting for transfers between devices, on_device(): lax.all_to_all(pay_1.reshape(3 * parts, 2, 128), 'net', 0, 0, tiled=True)  9.72 us
    all_to_all x1, starting transfers between devices, on_device(): recv_0 = lax.all_to_all(pay_0, 'net', 0, 0, tiled=True)  7.44 us
    all_to_all x1, starting transfers between devices, on_device(): lax.all_to_all(pay_1.reshape(3 * parts, 2, 128), 'net', 0, 0, tiled=True)  6.27 us
    all_to_all x1, waiting for transfers between devices, on_device(): recv_0 = lax.all_to_all(pay_0, 'net', 0, 0, tiled=True)  6.08 us
    all_to_all x1, waiting for transfers between devices, on_device(): recv_setup = lax.all_to_all(pay_setup, 'net', 0, 0, tiled=True)  5.14 us
    ppermute x1, starting transfers between devices, on_device(): lax.ppermute(sr[nrow - halo:], 'tm', [(i, i + 1) for i in range(ntm - 1)])  3.96 us
  transfers between devices with their start and end apart: 5, of which 3 were waited for; matrix products, arithmetic and copies ran while one was open for 0% of the time, Pallas kernels for 10%

profile of v8, /device:TPU:1, one launch (start us, length us, event | category | flops | bytes accessed | tf_op | source)
XLA Modules:
  0.0 75.1 jit_solution(9471169376870494158)
XLA Ops:
  0.6 2.1 %shard_map.272 = (f32[64,128]{1,0:T(8,128)}, f32[128,128]{1,0:T(8,128)}) custom-call(s32[1,64]{1,0:T(1,128)} %bitcast.103, s32[1,64]{1,0:T(1,128)} %bitcast.72, s32[1,64]{1,0:T(1,128)} %bitcast.104, f32[1,64]{1,0:T(1,128)} %bitcast.96, f32[1,64]{1,0:T(1,128)} %bitcast.98, f32[1,64]{1,0:T(1,128)} %bitcast.100, s32[1,64]{1,0:T(1,128)} %bitcast.102, ...), custom_call_target="tpu_custom_call" | custom-call | tf_op jit(solution)/shard_map/pallas_call | solution.py:255
  2.7 0.0 copy-start.1
  2.8 17.3 %all-to-all-start = ((f32[64,2,128]{2,1,0:T(2,128)}), f32[64,2,128]{2,1,0:T(2,128)S(1)}, u32[]{:S(2)}, u32[]{:S(2)}) async-start(f32[64,2,128]{2,1,0:T(2,128)} %bitcast.93), calls=%async_computation | async-start | bytes 131072 | tf_op jit(solution)/shard_map/all_to_all | solution.py:262
  20.1 4.0 %collective-permute-start = (f32[32,32]{1,0:T(8,128)S(1)}, f32[32,32]{1,0:T(8,128)S(1)}, u32[]{:S(2)}, u32[]{:S(2)}) collective-permute-start(f32[32,32]{1,0:T(8,128)S(1)} %bitcast.95), channel_id=1, source_target_pairs={{0,1},{1,2},{2,3},{3,4},{4,5},{5,6},{6,7},{8,9},{9,10},{10,11},{11... | collective-permute-start | bytes 12296 | tf_op jit(solution)/shard_map/ppermute | solution.py:207
  24.0 1.9 %collective-permute-start.1 = (f32[32,32]{1,0:T(8,128)S(1)}, f32[32,32]{1,0:T(8,128)S(1)}, u32[]{:S(2)}, u32[]{:S(2)}) collective-permute-start(f32[32,32]{1,0:T(8,128)S(1)} %bitcast.94), channel_id=1, source_target_pairs={{1,0},{2,1},{3,2},{4,3},{5,4},{6,5},{7,6},{9,8},{10,9},{11,10},{12... | collective-permute-start | bytes 12296 | tf_op jit(solution)/shard_map/ppermute | solution.py:208
  26.0 5.1 %all-to-all-done = f32[64,2,128]{2,1,0:T(2,128)S(1)} async-done(((f32[64,2,128]{2,1,0:T(2,128)}), f32[64,2,128]{2,1,0:T(2,128)S(1)}, u32[]{:S(2)}, u32[]{:S(2)}) %all-to-all-start) | async-done | bytes 65568 | tf_op jit(solution)/shard_map/all_to_all | solution.py:262
  31.1 1.0 %shard_map.273 = (f32[128,128]{1,0:T(8,128)S(1)}, f32[128,128]{1,0:T(8,128)}) custom-call(f32[128,128]{1,0:T(8,128)S(1)} %bitcast.57, f32[48,256]{1,0:T(8,128)S(1)} %bitcast.43, f32[48,256]{1,0:T(8,128)S(1)} %bitcast.50), custom_call_target="tpu_custom_call" | custom-call | tf_op jit(solution)/shard_map/pallas_call | solution.py:171
  32.1 7.4 %all-to-all-start.1 = ((f32[64,2,128]{2,1,0:T(2,128)}), f32[64,2,128]{2,1,0:T(2,128)S(1)}, u32[]{:S(2)}, u32[]{:S(2)}) async-start(f32[64,2,128]{2,1,0:T(2,128)} %bitcast.13), calls=%async_computation.1 | async-start | bytes 131072 | tf_op jit(solution)/shard_map/all_to_all | solution.py:276
  39.6 0.0 copy-start.23
  39.6 0.0 copy-start.19
  39.6 0.0 copy-start.21
  39.6 0.6 copy-done.23
  40.3 0.0 copy-start.8
  40.3 0.0 copy-start.11
  40.5 0.5 copy-done.6
  41.0 0.0 copy-done.8
  41.0 0.0 copy-done.11
  41.0 0.0 copy-done.12
  41.1 0.0 copy-done.13
  41.1 0.0 copy-done.15
  41.1 0.0 copy-done.16
  41.1 0.0 copy-done.17
  41.1 0.0 copy-done.18
  41.1 0.0 copy-done.7
  41.2 2.4 %shard_map.275 = (f32[4,48,256]{2,1,0:T(8,128)S(1)}, f32[2,48,256]{2,1,0:T(8,128)S(1)}, f32[10,48,256]{2,1,0:T(8,128)S(1)}, f32[80,32]{1,0:T(8,128)S(1)}, f32[48,32]{1,0:T(8,128)S(1)}) custom-call(f32[48,256]{1,0:T(8,128)S(1)} %bitcast.44, f32[48,256]{1,0:T(8,128)S(1)} %bitcast.51, s32[1,256]{1,0:T(1,128)S(1)} %bitcast.64, s32[1,256]{1,0:T(1,128)S(1)} %bitcast.67, ...), custom_call_target="tpu_custom_call" | custom-call | tf_op jit(solution)/shard_map/pallas_call | solution.py:171
  43.6 1.4 %shard_map.274 = (f32[4,48,256]{2,1,0:T(8,128)S(1)}, f32[10,48,128]{2,1,0:T(8,128)S(1)}, f32[8,256]{1,0:T(8,128)S(1)}) custom-call(f32[128,128]{1,0:T(8,128)S(1)} %get-tuple-element.31.mirror_ref.refs_6_.refs_18_, f32[48,256]{1,0:T(8,128)S(1)} %bitcast.45, f32[48,256]{1,0:T(8,128)S(1)} %bitcast.52, s32[1,256]{1,0:T(1,128)S(1)} %bitcast.65, ...), custom_call_target="tpu_custom_call" | custom-call | tf_op jit(solution)/shard_map/pallas_call | solution.py:171
  45.0 6.1 %all-to-all-done.1 = f32[64,2,128]{2,1,0:T(2,128)S(1)} async-done(((f32[64,2,128]{2,1,0:T(2,128)}), f32[64,2,128]{2,1,0:T(2,128)S(1)}, u32[]{:S(2)}, u32[]{:S(2)}) %all-to-all-start.1) | async-done | bytes 65568 | tf_op jit(solution)/shard_map/all_to_all | solution.py:276
  51.1 2.5 %shard_map.276 = (f32[10,48,64]{2,1,0:T(8,128)S(1)}, f32[4,48,256]{2,1,0:T(8,128)S(1)}, f32[384,128]{1,0:T(8,128)}) custom-call(f32[48,256]{1,0:T(8,128)S(1)} %bitcast.46, f32[48,256]{1,0:T(8,128)S(1)} %bitcast.47, f32[48,256]{1,0:T(8,128)S(1)} %bitcast.53, f32[48,256]{1,0:T(8,128)S(1)} %bitcast.58, f32[48,256]{1,0:T(8,128)S(1)} %bitcast.60, ...), custom_call_target="tpu_custom_call" | custom-call | tf_op jit(solution)/shard_map/pallas_call | solution.py:171
  53.6 6.3 %all-to-all-start.2 = ((f32[192,2,128]{2,1,0:T(2,128)}), f32[192,2,128]{2,1,0:T(2,128)S(1)}, u32[]{:S(2)}, u32[]{:S(2)}) async-start(f32[192,2,128]{2,1,0:T(2,128)} %bitcast.33), calls=%async_computation.2 | async-start | bytes 393216 | tf_op jit(solution)/shard_map/all_to_all | solution.py:450
  59.9 2.9 %shard_map.277 = (f32[4,48,256]{2,1,0:T(8,128)S(1)}, f32[2,48,256]{2,1,0:T(8,128)S(1)}, f32[48,32]{1,0:T(8,128)}, f32[48,32]{1,0:T(8,128)}, f32[192,64]{1,0:T(8,128)S(1)}, /*index=5*/f32[192,128]{1,0:T(8,128)S(1)}) custom-call(f32[4,48,256]{2,1,0:T(8,128)S(1)} %get-tuple-element.37.refs_0_, s32[1,256]{1,0:T(1,128)S(1)} %bitcast.66, s32[1,256]{1,0:T(1,128)S(1)} %bitcast.69, ...), custom_call_target="tpu_custom_call" | custom-call | tf_op jit(solution)/shard_map/pallas_call | solution.py:171
  62.8 9.7 %all-to-all-done.2 = f32[192,2,128]{2,1,0:T(2,128)S(1)} async-done(((f32[192,2,128]{2,1,0:T(2,128)}), f32[192,2,128]{2,1,0:T(2,128)S(1)}, u32[]{:S(2)}, u32[]{:S(2)}) %all-to-all-start.2) | async-done | bytes 196640 | tf_op jit(solution)/shard_map/all_to_all | solution.py:450
  72.5 2.5 %shard_map.278 = (f32[48,256]{1,0:T(8,128)}, f32[48,256]{1,0:T(8,128)}, f32[48,256]{1,0:T(8,128)}) custom-call(f32[4,48,256]{2,1,0:T(8,128)S(1)} %get-tuple-element.37.refs_0_, f32[48,256]{1,0:T(8,128)S(1)} %bitcast.48, f32[48,256]{1,0:T(8,128)S(1)} %bitcast.54, f32[48,256]{1,0:T(8,128)S(1)} %bitcast.59, f32[48,256]{1,0:T(8,128)S(1)} %bitcast.61, ...), custom_call_target="tpu_custom_call" | custom-call | tf_op jit(solution)/shard_map/pallas_call | solution.py:171
  (39 shorter events, 0.1 us)
Async XLA Ops:
  2.7 17.3 %copy-start.4 = (f32[3,16,32]{2,1,0:T(8,128)S(1)}, f32[3,16,32]{2,1,0:T(8,128)}, u32[]{:S(2)}) copy-start(f32[3,16,32]{2,1,0:T(8,128)} %param.29) | copy-start | bytes 18436
  2.7 28.4 %copy-start.1 = (f32[3,16,256]{2,1,0:T(8,128)S(1)}, f32[3,16,256]{2,1,0:T(8,128)}, u32[]{:S(2)}) copy-start(f32[3,16,256]{2,1,0:T(8,128)} %param.26) | copy-start | bytes 147460
  2.8 28.4 %all-to-all-start = ((f32[64,2,128]{2,1,0:T(2,128)}), f32[64,2,128]{2,1,0:T(2,128)S(1)}, u32[]{:S(2)}, u32[]{:S(2)}) async-start(f32[64,2,128]{2,1,0:T(2,128)} %bitcast.93), calls=%async_computation | async-start | bytes 131072 | tf_op jit(solution)/shard_map/all_to_all | solution.py:262
  20.1 11.1 %copy-start = (f32[3,16,256]{2,1,0:T(8,128)S(1)}, f32[3,16,256]{2,1,0:T(8,128)}, u32[]{:S(2)}) copy-start(f32[3,16,256]{2,1,0:T(8,128)} %param.25) | copy-start | bytes 147460
  20.1 20.2 %collective-permute-start = (f32[32,32]{1,0:T(8,128)S(1)}, f32[32,32]{1,0:T(8,128)S(1)}, u32[]{:S(2)}, u32[]{:S(2)}) collective-permute-start(f32[32,32]{1,0:T(8,128)S(1)} %bitcast.95), channel_id=1, source_target_pairs={{0,1},{1,2},{2,3},{3,4},{4,5},{5,6},{6,7},{8,9},{9,10},{10,11},{11... | collective-permute-start | bytes 12296 | tf_op jit(solution)/shard_map/ppermute | solution.py:207
  24.0 16.3 %collective-permute-start.1 = (f32[32,32]{1,0:T(8,128)S(1)}, f32[32,32]{1,0:T(8,128)S(1)}, u32[]{:S(2)}, u32[]{:S(2)}) collective-permute-start(f32[32,32]{1,0:T(8,128)S(1)} %bitcast.94), channel_id=1, source_target_pairs={{1,0},{2,1},{3,2},{4,3},{5,4},{6,5},{7,6},{9,8},{10,9},{11,10},{12... | collective-permute-start | bytes 12296 | tf_op jit(solution)/shard_map/ppermute | solution.py:208
  32.1 7.5 %copy-start.9 = (s32[64]{0:T(128)S(1)}, s32[64]{0:T(128)}, u32[]{:S(2)}) copy-start(s32[64]{0:T(128)} %param.43) | copy-start | bytes 772
  32.1 7.5 %copy-start.22 = (s32[64]{0:T(128)S(1)}, s32[64]{0:T(128)}, u32[]{:S(2)}) copy-start(s32[64]{0:T(128)} %param.49) | copy-start | bytes 772
  32.1 19.0 %all-to-all-start.1 = ((f32[64,2,128]{2,1,0:T(2,128)}), f32[64,2,128]{2,1,0:T(2,128)S(1)}, u32[]{:S(2)}, u32[]{:S(2)}) async-start(f32[64,2,128]{2,1,0:T(2,128)} %bitcast.13), calls=%async_computation.1 | async-start | bytes 131072 | tf_op jit(solution)/shard_map/all_to_all | solution.py:276
  39.6 0.7 copy-start.23
  39.6 0.7 copy-start.19
  39.6 0.7 copy-start.20
  39.6 0.7 copy-start.21
  40.3 0.7 copy-start.6
  40.3 0.7 copy-start.8
  40.3 0.7 copy-start.11
  40.4 0.7 copy-start.12
  40.4 0.7 copy-start.13
  40.4 0.7 copy-start.14
  40.4 0.7 copy-start.15
  40.4 0.7 copy-start.16
  40.4 0.7 copy-start.17
  40.4 0.7 copy-start.18
  40.4 0.7 copy-start.7
  40.5 0.7 copy-start.10
  43.6 7.6 %copy-start.2 = (f32[3,16,256]{2,1,0:T(8,128)S(1)}, f32[3,16,256]{2,1,0:T(8,128)}, u32[]{:S(2)}) copy-start(f32[3,16,256]{2,1,0:T(8,128)} %param.27) | copy-start | bytes 147460
  43.6 7.5 %copy-start.3 = (f32[3,16,256]{2,1,0:T(8,128)S(1)}, f32[3,16,256]{2,1,0:T(8,128)}, u32[]{:S(2)}) copy-start(f32[3,16,256]{2,1,0:T(8,128)} %param.28) | copy-start | bytes 147460
  43.6 7.5 %copy-start.5 = (f32[64,128]{1,0:T(8,128)S(1)}, f32[64,128]{1,0:T(8,128)}, u32[]{:S(2)}) copy-start(f32[64,128]{1,0:T(8,128)} %get-tuple-element.32.refs_7_) | copy-start | bytes 98308
  53.6 18.9 %all-to-all-start.2 = ((f32[192,2,128]{2,1,0:T(2,128)}), f32[192,2,128]{2,1,0:T(2,128)S(1)}, u32[]{:S(2)}, u32[]{:S(2)}) async-start(f32[192,2,128]{2,1,0:T(2,128)} %bitcast.33), calls=%async_computation.2 | async-start | bytes 393216 | tf_op jit(solution)/shard_map/all_to_all | solution.py:450

commit v9 on v8

--- a/solution.py
+++ b/solution.py
@@ -380,8 +380,8 @@
             zc = jnp.zeros((nrow, cuts), F32)
             far_c = give(rows(far_slot[0:nrow], far_slot[nrow:2 * nrow]), slot_t)
             far_cross = (far_c[0:nrow], far_c[nrow:], zc, zc)
-            stack = rows(*state)
-            pick_near = split4(take(stack, inc_near), nrow)
+            warm_near = take(rows(wmv, wav), inc_near)
+            pick_near = (warm_near[0:nrow], warm_near[nrow:], zc, zc)
             carry_c, fc, _ = advance(None, pick_near, far_cross, prm_cut)
             totals = tin_ref[...] + tm_ref[...] + give(fc, inc_near).reshape(4, nrow, buses)
         else:
@@ -414,9 +414,9 @@
             st_out[1] = ang
             st_out[2] = pr
             st_out[3] = pq
-            new_stack = rows(mag, ang, pr, pq)
+            new_stack = split3(rows(mag, ang, pr, pq))
             near_slot = dot(inc_near, slot_t, NN).astype(BF)
-            vals = rows(take(new_stack, near_slot), take(new_stack, inc_recv))
+            vals = rows(take_split(new_stack, near_slot), take_split(new_stack, inc_recv))
             for p in range(3):
                 plane_ref[...] = vals[p * 128:(p + 1) * 128].T
                 for k in range(cap):

time: 76.1 us -> 76 us (level)
  no operation moved by 1% of the time
where the time goes in v9:
time: 76 us; the launch traced here: 75 us
  starting transfers between devices  36.9 us (49%)
  waiting for transfers between devices  20.9 us (28%)
  Pallas kernels  14.8 us (19%)
  local copies, waits for them, and re-layouts  1.45 us (2%)
  between operations  0.96 us (1%)
    all_to_all x1, starting transfers between devices, on_device(): recv_setup = lax.all_to_all(pay_setup, 'net', 0, 0, tiled=True)  17.3 us
    pallas_call x6, Pallas kernels, vmem_call(): pl.pallas_call(kernel, out_shape=outs, in_specs=[pl.BlockSpec(memory_spac...  12.7 us
    all_to_all x1, waiting for transfers between devices, on_device(): lax.all_to_all(pay_1.reshape(3 * parts, 2, 128), 'net', 0, 0, tiled=True)  9.72 us
    all_to_all x1, starting transfers between devices, on_device(): recv_0 = lax.all_to_all(pay_0, 'net', 0, 0, tiled=True)  7.44 us
    all_to_all x1, starting transfers between devices, on_device(): lax.all_to_all(pay_1.reshape(3 * parts, 2, 128), 'net', 0, 0, tiled=True)  6.27 us
    all_to_all x1, waiting for transfers between devices, on_device(): recv_0 = lax.all_to_all(pay_0, 'net', 0, 0, tiled=True)  6.08 us
    all_to_all x1, waiting for transfers between devices, on_device(): recv_setup = lax.all_to_all(pay_setup, 'net', 0, 0, tiled=True)  5.14 us
    ppermute x1, starting transfers between devices, on_device(): lax.ppermute(sr[nrow - halo:], 'tm', [(i, i + 1) for i in range(ntm - 1)])  3.96 us
  transfers between devices with their start and end apart: 5, of which 3 were waited for; matrix products, arithmetic and copies ran while one was open for 0% of the time, Pallas kernels for 10%

profile of v9, /device:TPU:1, one launch (start us, length us, event | category | flops | bytes accessed | tf_op | source)
XLA Modules:
  0.0 75.0 jit_solution(7539357858193680292)
XLA Ops:
  0.6 2.1 %shard_map.272 = (f32[64,128]{1,0:T(8,128)}, f32[128,128]{1,0:T(8,128)}) custom-call(s32[1,64]{1,0:T(1,128)} %bitcast.103, s32[1,64]{1,0:T(1,128)} %bitcast.72, s32[1,64]{1,0:T(1,128)} %bitcast.104, f32[1,64]{1,0:T(1,128)} %bitcast.96, f32[1,64]{1,0:T(1,128)} %bitcast.98, f32[1,64]{1,0:T(1,128)} %bitcast.100, s32[1,64]{1,0:T(1,128)} %bitcast.102, ...), custom_call_target="tpu_custom_call" | custom-call | tf_op jit(solution)/shard_map/pallas_call | solution.py:255
  2.7 0.0 copy-start.1
  2.8 17.3 %all-to-all-start = ((f32[64,2,128]{2,1,0:T(2,128)}), f32[64,2,128]{2,1,0:T(2,128)S(1)}, u32[]{:S(2)}, u32[]{:S(2)}) async-start(f32[64,2,128]{2,1,0:T(2,128)} %bitcast.93), calls=%async_computation | async-start | bytes 131072 | tf_op jit(solution)/shard_map/all_to_all | solution.py:262
  20.1 4.0 %collective-permute-start = (f32[32,32]{1,0:T(8,128)S(1)}, f32[32,32]{1,0:T(8,128)S(1)}, u32[]{:S(2)}, u32[]{:S(2)}) collective-permute-start(f32[32,32]{1,0:T(8,128)S(1)} %bitcast.95), channel_id=1, source_target_pairs={{0,1},{1,2},{2,3},{3,4},{4,5},{5,6},{6,7},{8,9},{9,10},{10,11},{11... | collective-permute-start | bytes 12296 | tf_op jit(solution)/shard_map/ppermute | solution.py:207
  24.0 1.9 %collective-permute-start.1 = (f32[32,32]{1,0:T(8,128)S(1)}, f32[32,32]{1,0:T(8,128)S(1)}, u32[]{:S(2)}, u32[]{:S(2)}) collective-permute-start(f32[32,32]{1,0:T(8,128)S(1)} %bitcast.94), channel_id=1, source_target_pairs={{1,0},{2,1},{3,2},{4,3},{5,4},{6,5},{7,6},{9,8},{10,9},{11,10},{12... | collective-permute-start | bytes 12296 | tf_op jit(solution)/shard_map/ppermute | solution.py:208
  26.0 5.1 %all-to-all-done = f32[64,2,128]{2,1,0:T(2,128)S(1)} async-done(((f32[64,2,128]{2,1,0:T(2,128)}), f32[64,2,128]{2,1,0:T(2,128)S(1)}, u32[]{:S(2)}, u32[]{:S(2)}) %all-to-all-start) | async-done | bytes 65568 | tf_op jit(solution)/shard_map/all_to_all | solution.py:262
  31.1 1.0 %shard_map.273 = (f32[128,128]{1,0:T(8,128)S(1)}, f32[128,128]{1,0:T(8,128)}) custom-call(f32[128,128]{1,0:T(8,128)S(1)} %bitcast.57, f32[48,256]{1,0:T(8,128)S(1)} %bitcast.43, f32[48,256]{1,0:T(8,128)S(1)} %bitcast.50), custom_call_target="tpu_custom_call" | custom-call | tf_op jit(solution)/shard_map/pallas_call | solution.py:171
  32.1 7.4 %all-to-all-start.1 = ((f32[64,2,128]{2,1,0:T(2,128)}), f32[64,2,128]{2,1,0:T(2,128)S(1)}, u32[]{:S(2)}, u32[]{:S(2)}) async-start(f32[64,2,128]{2,1,0:T(2,128)} %bitcast.13), calls=%async_computation.1 | async-start | bytes 131072 | tf_op jit(solution)/shard_map/all_to_all | solution.py:276
  39.6 0.0 copy-start.23
  39.6 0.0 copy-start.19
  39.6 0.0 copy-start.21
  39.6 0.6 copy-done.23
  40.3 0.0 copy-start.8
  40.3 0.0 copy-start.11
  40.5 0.5 copy-done.6
  41.0 0.0 copy-done.8
  41.0 0.0 copy-done.11
  41.0 0.0 copy-done.12
  41.1 0.0 copy-done.13
  41.1 0.0 copy-done.15
  41.1 0.0 copy-done.16
  41.1 0.0 copy-done.17
  41.1 0.0 copy-done.18
  41.1 0.0 copy-done.7
  41.2 2.4 %shard_map.275 = (f32[4,48,256]{2,1,0:T(8,128)S(1)}, f32[2,48,256]{2,1,0:T(8,128)S(1)}, f32[10,48,256]{2,1,0:T(8,128)S(1)}, f32[80,32]{1,0:T(8,128)S(1)}, f32[48,32]{1,0:T(8,128)S(1)}) custom-call(f32[48,256]{1,0:T(8,128)S(1)} %bitcast.44, f32[48,256]{1,0:T(8,128)S(1)} %bitcast.51, s32[1,256]{1,0:T(1,128)S(1)} %bitcast.64, s32[1,256]{1,0:T(1,128)S(1)} %bitcast.67, ...), custom_call_target="tpu_custom_call" | custom-call | tf_op jit(solution)/shard_map/pallas_call | solution.py:171
  43.6 1.4 %shard_map.274 = (f32[4,48,256]{2,1,0:T(8,128)S(1)}, f32[10,48,128]{2,1,0:T(8,128)S(1)}, f32[8,256]{1,0:T(8,128)S(1)}) custom-call(f32[128,128]{1,0:T(8,128)S(1)} %get-tuple-element.31.mirror_ref.refs_6_.refs_18_, f32[48,256]{1,0:T(8,128)S(1)} %bitcast.45, f32[48,256]{1,0:T(8,128)S(1)} %bitcast.52, s32[1,256]{1,0:T(1,128)S(1)} %bitcast.65, ...), custom_call_target="tpu_custom_call" | custom-call | tf_op jit(solution)/shard_map/pallas_call | solution.py:171
  45.0 6.1 %all-to-all-done.1 = f32[64,2,128]{2,1,0:T(2,128)S(1)} async-done(((f32[64,2,128]{2,1,0:T(2,128)}), f32[64,2,128]{2,1,0:T(2,128)S(1)}, u32[]{:S(2)}, u32[]{:S(2)}) %all-to-all-start.1) | async-done | bytes 65568 | tf_op jit(solution)/shard_map/all_to_all | solution.py:276
  51.1 2.5 %shard_map.276 = (f32[10,48,64]{2,1,0:T(8,128)S(1)}, f32[4,48,256]{2,1,0:T(8,128)S(1)}, f32[384,128]{1,0:T(8,128)}) custom-call(f32[48,256]{1,0:T(8,128)S(1)} %bitcast.46, f32[48,256]{1,0:T(8,128)S(1)} %bitcast.47, f32[48,256]{1,0:T(8,128)S(1)} %bitcast.53, f32[48,256]{1,0:T(8,128)S(1)} %bitcast.58, f32[48,256]{1,0:T(8,128)S(1)} %bitcast.60, ...), custom_call_target="tpu_custom_call" | custom-call | tf_op jit(solution)/shard_map/pallas_call | solution.py:171
  53.6 6.3 %all-to-all-start.2 = ((f32[192,2,128]{2,1,0:T(2,128)}), f32[192,2,128]{2,1,0:T(2,128)S(1)}, u32[]{:S(2)}, u32[]{:S(2)}) async-start(f32[192,2,128]{2,1,0:T(2,128)} %bitcast.33), calls=%async_computation.2 | async-start | bytes 393216 | tf_op jit(solution)/shard_map/all_to_all | solution.py:450
  59.9 2.9 %shard_map.277 = (f32[4,48,256]{2,1,0:T(8,128)S(1)}, f32[2,48,256]{2,1,0:T(8,128)S(1)}, f32[48,32]{1,0:T(8,128)}, f32[48,32]{1,0:T(8,128)}, f32[192,64]{1,0:T(8,128)S(1)}, /*index=5*/f32[192,128]{1,0:T(8,128)S(1)}) custom-call(f32[4,48,256]{2,1,0:T(8,128)S(1)} %get-tuple-element.37.refs_0_, s32[1,256]{1,0:T(1,128)S(1)} %bitcast.66, s32[1,256]{1,0:T(1,128)S(1)} %bitcast.69, ...), custom_call_target="tpu_custom_call" | custom-call | tf_op jit(solution)/shard_map/pallas_call | solution.py:171
  62.8 9.7 %all-to-all-done.2 = f32[192,2,128]{2,1,0:T(2,128)S(1)} async-done(((f32[192,2,128]{2,1,0:T(2,128)}), f32[192,2,128]{2,1,0:T(2,128)S(1)}, u32[]{:S(2)}, u32[]{:S(2)}) %all-to-all-start.2) | async-done | bytes 196640 | tf_op jit(solution)/shard_map/all_to_all | solution.py:450
  72.5 2.5 %shard_map.278 = (f32[48,256]{1,0:T(8,128)}, f32[48,256]{1,0:T(8,128)}, f32[48,256]{1,0:T(8,128)}) custom-call(f32[4,48,256]{2,1,0:T(8,128)S(1)} %get-tuple-element.37.refs_0_, f32[48,256]{1,0:T(8,128)S(1)} %bitcast.48, f32[48,256]{1,0:T(8,128)S(1)} %bitcast.54, f32[48,256]{1,0:T(8,128)S(1)} %bitcast.59, f32[48,256]{1,0:T(8,128)S(1)} %bitcast.61, ...), custom_call_target="tpu_custom_call" | custom-call | tf_op jit(solution)/shard_map/pallas_call | solution.py:171
  (39 shorter events, 0.1 us)
Async XLA Ops:
  2.7 17.3 %copy-start.4 = (f32[3,16,32]{2,1,0:T(8,128)S(1)}, f32[3,16,32]{2,1,0:T(8,128)}, u32[]{:S(2)}) copy-start(f32[3,16,32]{2,1,0:T(8,128)} %param.29) | copy-start | bytes 18436
  2.7 28.4 %copy-start.1 = (f32[3,16,256]{2,1,0:T(8,128)S(1)}, f32[3,16,256]{2,1,0:T(8,128)}, u32[]{:S(2)}) copy-start(f32[3,16,256]{2,1,0:T(8,128)} %param.26) | copy-start | bytes 147460
  2.8 28.4 %all-to-all-start = ((f32[64,2,128]{2,1,0:T(2,128)}), f32[64,2,128]{2,1,0:T(2,128)S(1)}, u32[]{:S(2)}, u32[]{:S(2)}) async-start(f32[64,2,128]{2,1,0:T(2,128)} %bitcast.93), calls=%async_computation | async-start | bytes 131072 | tf_op jit(solution)/shard_map/all_to_all | solution.py:262
  20.1 11.1 %copy-start = (f32[3,16,256]{2,1,0:T(8,128)S(1)}, f32[3,16,256]{2,1,0:T(8,128)}, u32[]{:S(2)}) copy-start(f32[3,16,256]{2,1,0:T(8,128)} %param.25) | copy-start | bytes 147460
  20.1 20.2 %collective-permute-start = (f32[32,32]{1,0:T(8,128)S(1)}, f32[32,32]{1,0:T(8,128)S(1)}, u32[]{:S(2)}, u32[]{:S(2)}) collective-permute-start(f32[32,32]{1,0:T(8,128)S(1)} %bitcast.95), channel_id=1, source_target_pairs={{0,1},{1,2},{2,3},{3,4},{4,5},{5,6},{6,7},{8,9},{9,10},{10,11},{11... | collective-permute-start | bytes 12296 | tf_op jit(solution)/shard_map/ppermute | solution.py:207
  24.0 16.3 %collective-permute-start.1 = (f32[32,32]{1,0:T(8,128)S(1)}, f32[32,32]{1,0:T(8,128)S(1)}, u32[]{:S(2)}, u32[]{:S(2)}) collective-permute-start(f32[32,32]{1,0:T(8,128)S(1)} %bitcast.94), channel_id=1, source_target_pairs={{1,0},{2,1},{3,2},{4,3},{5,4},{6,5},{7,6},{9,8},{10,9},{11,10},{12... | collective-permute-start | bytes 12296 | tf_op jit(solution)/shard_map/ppermute | solution.py:208
  32.1 7.5 %copy-start.9 = (s32[64]{0:T(128)S(1)}, s32[64]{0:T(128)}, u32[]{:S(2)}) copy-start(s32[64]{0:T(128)} %param.43) | copy-start | bytes 772
  32.1 7.5 %copy-start.22 = (s32[64]{0:T(128)S(1)}, s32[64]{0:T(128)}, u32[]{:S(2)}) copy-start(s32[64]{0:T(128)} %param.49) | copy-start | bytes 772
  32.1 19.0 %all-to-all-start.1 = ((f32[64,2,128]{2,1,0:T(2,128)}), f32[64,2,128]{2,1,0:T(2,128)S(1)}, u32[]{:S(2)}, u32[]{:S(2)}) async-start(f32[64,2,128]{2,1,0:T(2,128)} %bitcast.13), calls=%async_computation.1 | async-start | bytes 131072 | tf_op jit(solution)/shard_map/all_to_all | solution.py:276
  39.6 0.7 copy-start.23
  39.6 0.7 copy-start.19
  39.6 0.7 copy-start.20
  39.6 0.7 copy-start.21
  40.3 0.7 copy-start.6
  40.3 0.7 copy-start.8
  40.3 0.7 copy-start.11
  40.4 0.7 copy-start.12
  40.4 0.7 copy-start.13
  40.4 0.7 copy-start.14
  40.4 0.7 copy-start.15
  40.4 0.7 copy-start.16
  40.4 0.7 copy-start.17
  40.4 0.7 copy-start.18
  40.4 0.7 copy-start.7
  40.5 0.7 copy-start.10
  43.6 7.6 %copy-start.2 = (f32[3,16,256]{2,1,0:T(8,128)S(1)}, f32[3,16,256]{2,1,0:T(8,128)}, u32[]{:S(2)}) copy-start(f32[3,16,256]{2,1,0:T(8,128)} %param.27) | copy-start | bytes 147460
  43.6 7.5 %copy-start.3 = (f32[3,16,256]{2,1,0:T(8,128)S(1)}, f32[3,16,256]{2,1,0:T(8,128)}, u32[]{:S(2)}) copy-start(f32[3,16,256]{2,1,0:T(8,128)} %param.28) | copy-start | bytes 147460
  43.6 7.5 %copy-start.5 = (f32[64,128]{1,0:T(8,128)S(1)}, f32[64,128]{1,0:T(8,128)}, u32[]{:S(2)}) copy-start(f32[64,128]{1,0:T(8,128)} %get-tuple-element.32.refs_7_) | copy-start | bytes 98308
  53.6 18.9 %all-to-all-start.2 = ((f32[192,2,128]{2,1,0:T(2,128)}), f32[192,2,128]{2,1,0:T(2,128)S(1)}, u32[]{:S(2)}, u32[]{:S(2)}) async-start(f32[192,2,128]{2,1,0:T(2,128)} %bitcast.33), calls=%async_computation.2 | async-start | bytes 393216 | tf_op jit(solution)/shard_map/all_to_all | solution.py:450

commit v10 on v9

--- a/solution.py
+++ b/solution.py
@@ -261,18 +261,15 @@
     )(*prep_args)
     recv_setup = lax.all_to_all(pay_setup, "net", 0, 0, tiled=True)
 
-    def mid_kernel(recv_ref, wm_ref, wa_ref, mirror_out, pay_out):
-        mirror = recv_ref[...].T
-        mirror_out[...] = mirror
-        inc_recv = onehot(mirror[0:1].astype(jnp.int32) - 1, buses)
-        vals = rows(take(rows(wm_ref[...], wa_ref[...]), inc_recv), jnp.zeros((nvals0 - 2 * nrow, slots), F32))
-        pay_out[...] = vals.T
-
-    mirror_t, pay_0 = vmem_call(
-        mid_kernel,
-        (jax.ShapeDtypeStruct((nvals0, slots), F32), jax.ShapeDtypeStruct((slots, nvals0), F32)),
-        recv_setup, wm, wa,
-    )
+    def mid_kernel(recv_ref, wm_ref, wa_ref, pay_out):
+        ids = recv_ref[:, 0:1].astype(jnp.int32) - 1
+        inc_t = (ids == lax.broadcasted_iota(jnp.int32, (slots, buses), 1)).astype(BF)
+        warm = rows(wm_ref[...], wa_ref[...], jnp.zeros((nvals0 - 2 * nrow, buses), F32))
+        pay_out[...] = give_left(inc_t, warm)
+
+    pay_0 = vmem_call(
+        mid_kernel, (jax.ShapeDtypeStruct((slots, nvals0), F32),), recv_setup, wm, wa,
+    )[0]
     recv_0 = lax.all_to_all(pay_0, "net", 0, 0, tiled=True)
 
     def spread(p):
@@ -341,8 +338,9 @@
         sup_out[0] = supply[0:nrow]
         sup_out[1] = supply[nrow:]
 
-    def mirror0_kernel(mirror_ref, wm_ref, wa_ref, bf_ref, bt_ref, cn_ref, gb_ref, tot_out, cm_out, dg_out):
-        mirror = mirror_ref[...]
+    def mirror0_kernel(recv_ref, wm_ref, wa_ref, bf_ref, bt_ref, cn_ref, gb_ref, tot_out, cm_out, dg_out, mir_out):
+        mirror = recv_ref[...].T
+        mir_out[...] = mirror
         inc_recv = onehot(mirror[0:1].astype(jnp.int32) - 1, buses)
         degree = (col_sum(onehot(bf_ref[...], buses)) + col_sum(onehot(bt_ref[...], buses))
                   + col_sum(onehot(cn_ref[...], buses)) + col_sum(inc_recv))
@@ -436,8 +434,9 @@
          sds((nrow, gens), F32)),
         wm, wa, *br_all, *gen_all, lo, sr, hi, sq,
     )
-    tm0, cm1, dg = vmem_call(
-        mirror0_kernel, (tot_shape, sds((10, nrow, slots), F32), sds((8, buses), F32)), mirror_t, wm, wa,
+    tm0, cm1, dg, mirror_t = vmem_call(
+        mirror0_kernel,
+        (tot_shape, sds((10, nrow, slots), F32), sds((8, buses), F32), sds((nvals0, slots), F32)), recv_setup, wm, wa,
         br_rows[0], br_rows[1], cut_rows[0], gen_rows[0],
     )
     cprm = jnp.concatenate([cut_rows[0].astype(F32), *cut_rows[1:], jnp.zeros((3, cuts), F32)], axis=0)

time: 76 us -> 76 us (level)
  no operation moved by 1% of the time
where the time goes in v10:
time: 76 us; the launch traced here: 75 us
  starting transfers between devices  36.9 us (49%)
  waiting for transfers between devices  21 us (28%)
  Pallas kernels  14.7 us (19%)
  local copies, waits for them, and re-layouts  1.45 us (2%)
  between operations  0.96 us (1%)
    all_to_all x1, starting transfers between devices, on_device(): recv_setup = lax.all_to_all(pay_setup, 'net', 0, 0, tiled=True)  17.3 us
    pallas_call x6, Pallas kernels, vmem_call(): pl.pallas_call(kernel, out_shape=outs, in_specs=[pl.BlockSpec(memory_spac...  12.6 us
    all_to_all x1, waiting for transfers between devices, on_device(): lax.all_to_all(pay_1.reshape(3 * parts, 2, 128), 'net', 0, 0, tiled=True)  9.78 us
    all_to_all x1, starting transfers between devices, on_device(): recv_0 = lax.all_to_all(pay_0, 'net', 0, 0, tiled=True)  7.44 us
    all_to_all x1, starting transfers between devices, on_device(): lax.all_to_all(pay_1.reshape(3 * parts, 2, 128), 'net', 0, 0, tiled=True)  6.32 us
    all_to_all x1, waiting for transfers between devices, on_device(): recv_0 = lax.all_to_all(pay_0, 'net', 0, 0, tiled=True)  6.03 us
    all_to_all x1, waiting for transfers between devices, on_device(): recv_setup = lax.all_to_all(pay_setup, 'net', 0, 0, tiled=True)  5.14 us
    ppermute x1, starting transfers between devices, on_device(): lax.ppermute(sr[nrow - halo:], 'tm', [(i, i + 1) for i in range(ntm - 1)])  3.96 us
  transfers between devices with their start and end apart: 5, of which 3 were waited for; matrix products, arithmetic and copies ran while one was open for 0% of the time, Pallas kernels for 10%

profile of v10, /device:TPU:1, one launch (start us, length us, event | category | flops | bytes accessed | tf_op | source)
XLA Modules:
  0.0 75.0 jit_solution(12180988900825217389)
XLA Ops:
  0.6 2.1 %shard_map.272 = (f32[64,128]{1,0:T(8,128)}, f32[128,128]{1,0:T(8,128)}) custom-call(s32[1,64]{1,0:T(1,128)} %bitcast.104, s32[1,64]{1,0:T(1,128)} %bitcast.73, s32[1,64]{1,0:T(1,128)} %bitcast.105, f32[1,64]{1,0:T(1,128)} %bitcast.97, f32[1,64]{1,0:T(1,128)} %bitcast.99, f32[1,64]{1,0:T(1,128)} %bitcast.101, s32[1,64]{1,0:T(1,128)} %bitcast.103, ...), custom_call_target="tpu_custom_call" | custom-call | tf_op jit(solution)/shard_map/pallas_call | solution.py:255
  2.7 0.0 copy-start.4
  2.7 0.0 copy-start.1
  2.8 17.3 %all-to-all-start = ((f32[64,2,128]{2,1,0:T(2,128)}), f32[64,2,128]{2,1,0:T(2,128)S(1)}, u32[]{:S(2)}, u32[]{:S(2)}) async-start(f32[64,2,128]{2,1,0:T(2,128)} %bitcast.94), calls=%async_computation | async-start | bytes 131072 | tf_op jit(solution)/shard_map/all_to_all | solution.py:262
  20.1 4.0 %collective-permute-start = (f32[32,32]{1,0:T(8,128)S(1)}, f32[32,32]{1,0:T(8,128)S(1)}, u32[]{:S(2)}, u32[]{:S(2)}) collective-permute-start(f32[32,32]{1,0:T(8,128)S(1)} %bitcast.96), channel_id=1, source_target_pairs={{0,1},{1,2},{2,3},{3,4},{4,5},{5,6},{6,7},{8,9},{9,10},{10,11},{11... | collective-permute-start | bytes 12296 | tf_op jit(solution)/shard_map/ppermute | solution.py:207
  24.1 1.9 %collective-permute-start.1 = (f32[32,32]{1,0:T(8,128)S(1)}, f32[32,32]{1,0:T(8,128)S(1)}, u32[]{:S(2)}, u32[]{:S(2)}) collective-permute-start(f32[32,32]{1,0:T(8,128)S(1)} %bitcast.95), channel_id=1, source_target_pairs={{1,0},{2,1},{3,2},{4,3},{5,4},{6,5},{7,6},{9,8},{10,9},{11,10},{12... | collective-permute-start | bytes 12296 | tf_op jit(solution)/shard_map/ppermute | solution.py:208
  26.0 5.1 %all-to-all-done = f32[64,2,128]{2,1,0:T(2,128)S(1)} async-done(((f32[64,2,128]{2,1,0:T(2,128)}), f32[64,2,128]{2,1,0:T(2,128)S(1)}, u32[]{:S(2)}, u32[]{:S(2)}) %all-to-all-start) | async-done | bytes 65568 | tf_op jit(solution)/shard_map/all_to_all | solution.py:262
  31.1 0.9 %shard_map.273 = f32[128,128]{1,0:T(8,128)} custom-call(f32[128,128]{1,0:T(8,128)S(1)} %bitcast.56, f32[48,256]{1,0:T(8,128)S(1)} %bitcast.43, f32[48,256]{1,0:T(8,128)S(1)} %bitcast.50), custom_call_target="tpu_custom_call" | custom-call | tf_op jit(solution)/shard_map/pallas_call | solution.py:171
  32.0 7.4 %all-to-all-start.1 = ((f32[64,2,128]{2,1,0:T(2,128)}), f32[64,2,128]{2,1,0:T(2,128)S(1)}, u32[]{:S(2)}, u32[]{:S(2)}) async-start(f32[64,2,128]{2,1,0:T(2,128)} %bitcast.13), calls=%async_computation.1 | async-start | bytes 131072 | tf_op jit(solution)/shard_map/all_to_all | solution.py:273
  39.5 0.0 copy-start.20
  39.5 0.0 copy-start.21
  39.6 0.6 copy-done.23
  40.3 0.0 copy-start.12
  40.3 0.0 copy-start.13
  40.4 0.5 copy-done.6
  40.9 0.0 copy-done.8
  40.9 0.0 copy-done.11
  40.9 0.0 copy-done.12
  41.0 0.0 copy-done.13
  41.0 0.0 copy-done.15
  41.0 0.0 copy-done.16
  41.0 0.0 copy-done.17
  41.0 0.0 copy-done.18
  41.0 0.0 copy-done.7
  41.1 2.4 %shard_map.275 = (f32[4,48,256]{2,1,0:T(8,128)S(1)}, f32[2,48,256]{2,1,0:T(8,128)S(1)}, f32[10,48,256]{2,1,0:T(8,128)S(1)}, f32[80,32]{1,0:T(8,128)S(1)}, f32[48,32]{1,0:T(8,128)S(1)}) custom-call(f32[48,256]{1,0:T(8,128)S(1)} %bitcast.44, f32[48,256]{1,0:T(8,128)S(1)} %bitcast.51, s32[1,256]{1,0:T(1,128)S(1)} %bitcast.65, s32[1,256]{1,0:T(1,128)S(1)} %bitcast.68, ...), custom_call_target="tpu_custom_call" | custom-call | tf_op jit(solution)/shard_map/pallas_call | solution.py:171
  43.5 1.5 %shard_map.274 = (f32[4,48,256]{2,1,0:T(8,128)S(1)}, f32[10,48,128]{2,1,0:T(8,128)S(1)}, f32[8,256]{1,0:T(8,128)S(1)}, f32[128,128]{1,0:T(8,128)S(1)}) custom-call(f32[128,128]{1,0:T(8,128)S(1)} %bitcast.57, f32[48,256]{1,0:T(8,128)S(1)} %bitcast.45, f32[48,256]{1,0:T(8,128)S(1)} %bitcast.52, s32[1,256]{1,0:T(1,128)S(1)} %bitcast.66, s32[1,256]{1,0:T(1,128)S(1)} %bitcast.69, ...), custom_call_target="tpu_custom_call" | custom-call | tf_op jit(solution)/shard_map/pallas_call | solution.py:171
  45.0 6.0 %all-to-all-done.1 = f32[64,2,128]{2,1,0:T(2,128)S(1)} async-done(((f32[64,2,128]{2,1,0:T(2,128)}), f32[64,2,128]{2,1,0:T(2,128)S(1)}, u32[]{:S(2)}, u32[]{:S(2)}) %all-to-all-start.1) | async-done | bytes 65568 | tf_op jit(solution)/shard_map/all_to_all | solution.py:273
  51.0 2.4 %shard_map.276 = (f32[10,48,64]{2,1,0:T(8,128)S(1)}, f32[4,48,256]{2,1,0:T(8,128)S(1)}, f32[384,128]{1,0:T(8,128)}) custom-call(f32[48,256]{1,0:T(8,128)S(1)} %bitcast.46, f32[48,256]{1,0:T(8,128)S(1)} %bitcast.47, f32[48,256]{1,0:T(8,128)S(1)} %bitcast.53, f32[48,256]{1,0:T(8,128)S(1)} %bitcast.59, f32[48,256]{1,0:T(8,128)S(1)} %bitcast.61, ...), custom_call_target="tpu_custom_call" | custom-call | tf_op jit(solution)/shard_map/pallas_call | solution.py:171
  53.5 6.3 %all-to-all-start.2 = ((f32[192,2,128]{2,1,0:T(2,128)}), f32[192,2,128]{2,1,0:T(2,128)S(1)}, u32[]{:S(2)}, u32[]{:S(2)}) async-start(f32[192,2,128]{2,1,0:T(2,128)} %bitcast.33), calls=%async_computation.2 | async-start | bytes 393216 | tf_op jit(solution)/shard_map/all_to_all | solution.py:449
  59.8 2.9 %shard_map.277 = (f32[4,48,256]{2,1,0:T(8,128)S(1)}, f32[2,48,256]{2,1,0:T(8,128)S(1)}, f32[48,32]{1,0:T(8,128)}, f32[48,32]{1,0:T(8,128)}, f32[192,64]{1,0:T(8,128)S(1)}, /*index=5*/f32[192,128]{1,0:T(8,128)S(1)}) custom-call(f32[4,48,256]{2,1,0:T(8,128)S(1)} %get-tuple-element.35.refs_0_, s32[1,256]{1,0:T(1,128)S(1)} %bitcast.67, s32[1,256]{1,0:T(1,128)S(1)} %bitcast.70, ...), custom_call_target="tpu_custom_call" | custom-call | tf_op jit(solution)/shard_map/pallas_call | solution.py:171
  62.7 9.8 %all-to-all-done.2 = f32[192,2,128]{2,1,0:T(2,128)S(1)} async-done(((f32[192,2,128]{2,1,0:T(2,128)}), f32[192,2,128]{2,1,0:T(2,128)S(1)}, u32[]{:S(2)}, u32[]{:S(2)}) %all-to-all-start.2) | async-done | bytes 196640 | tf_op jit(solution)/shard_map/all_to_all | solution.py:449
  72.5 2.5 %shard_map.278 = (f32[48,256]{1,0:T(8,128)}, f32[48,256]{1,0:T(8,128)}, f32[48,256]{1,0:T(8,128)}) custom-call(f32[4,48,256]{2,1,0:T(8,128)S(1)} %get-tuple-element.35.refs_0_, f32[48,256]{1,0:T(8,128)S(1)} %bitcast.48, f32[48,256]{1,0:T(8,128)S(1)} %bitcast.54, f32[48,256]{1,0:T(8,128)S(1)} %bitcast.60, f32[48,256]{1,0:T(8,128)S(1)} %bitcast.62, ...), custom_call_target="tpu_custom_call" | custom-call | tf_op jit(solution)/shard_map/pallas_call | solution.py:171
  (39 shorter events, 0.1 us)
Async XLA Ops:
  2.7 17.3 %copy-start.4 = (f32[3,16,32]{2,1,0:T(8,128)S(1)}, f32[3,16,32]{2,1,0:T(8,128)}, u32[]{:S(2)}) copy-start(f32[3,16,32]{2,1,0:T(8,128)} %param.29) | copy-start | bytes 18436
  2.7 28.4 %copy-start.1 = (f32[3,16,256]{2,1,0:T(8,128)S(1)}, f32[3,16,256]{2,1,0:T(8,128)}, u32[]{:S(2)}) copy-start(f32[3,16,256]{2,1,0:T(8,128)} %param.26) | copy-start | bytes 147460
  2.8 28.4 %all-to-all-start = ((f32[64,2,128]{2,1,0:T(2,128)}), f32[64,2,128]{2,1,0:T(2,128)S(1)}, u32[]{:S(2)}, u32[]{:S(2)}) async-start(f32[64,2,128]{2,1,0:T(2,128)} %bitcast.94), calls=%async_computation | async-start | bytes 131072 | tf_op jit(solution)/shard_map/all_to_all | solution.py:262
  20.1 11.1 %copy-start = (f32[3,16,256]{2,1,0:T(8,128)S(1)}, f32[3,16,256]{2,1,0:T(8,128)}, u32[]{:S(2)}) copy-start(f32[3,16,256]{2,1,0:T(8,128)} %param.25) | copy-start | bytes 147460
  20.1 20.2 %collective-permute-start = (f32[32,32]{1,0:T(8,128)S(1)}, f32[32,32]{1,0:T(8,128)S(1)}, u32[]{:S(2)}, u32[]{:S(2)}) collective-permute-start(f32[32,32]{1,0:T(8,128)S(1)} %bitcast.96), channel_id=1, source_target_pairs={{0,1},{1,2},{2,3},{3,4},{4,5},{5,6},{6,7},{8,9},{9,10},{10,11},{11... | collective-permute-start | bytes 12296 | tf_op jit(solution)/shard_map/ppermute | solution.py:207
  24.1 16.2 %collective-permute-start.1 = (f32[32,32]{1,0:T(8,128)S(1)}, f32[32,32]{1,0:T(8,128)S(1)}, u32[]{:S(2)}, u32[]{:S(2)}) collective-permute-start(f32[32,32]{1,0:T(8,128)S(1)} %bitcast.95), channel_id=1, source_target_pairs={{1,0},{2,1},{3,2},{4,3},{5,4},{6,5},{7,6},{9,8},{10,9},{11,10},{12... | collective-permute-start | bytes 12296 | tf_op jit(solution)/shard_map/ppermute | solution.py:208
  32.0 7.5 %copy-start.9 = (s32[64]{0:T(128)S(1)}, s32[64]{0:T(128)}, u32[]{:S(2)}) copy-start(s32[64]{0:T(128)} %param.43) | copy-start | bytes 772
  32.0 7.5 %copy-start.22 = (s32[64]{0:T(128)S(1)}, s32[64]{0:T(128)}, u32[]{:S(2)}) copy-start(s32[64]{0:T(128)} %param.49) | copy-start | bytes 772
  32.0 19.0 %all-to-all-start.1 = ((f32[64,2,128]{2,1,0:T(2,128)}), f32[64,2,128]{2,1,0:T(2,128)S(1)}, u32[]{:S(2)}, u32[]{:S(2)}) async-start(f32[64,2,128]{2,1,0:T(2,128)} %bitcast.13), calls=%async_computation.1 | async-start | bytes 131072 | tf_op jit(solution)/shard_map/all_to_all | solution.py:273
  39.5 0.7 copy-start.23
  39.5 0.7 copy-start.19
  39.5 0.7 copy-start.20
  39.5 0.7 copy-start.21
  40.2 0.7 copy-start.6
  40.2 0.7 copy-start.8
  40.3 0.7 copy-start.11
  40.3 0.7 copy-start.12
  40.3 0.7 copy-start.13
  40.3 0.7 copy-start.14
  40.3 0.7 copy-start.15
  40.3 0.7 copy-start.16
  40.3 0.7 copy-start.17
  40.3 0.7 copy-start.18
  40.4 0.7 copy-start.7
  40.4 0.7 copy-start.10
  43.5 7.5 %copy-start.2 = (f32[3,16,256]{2,1,0:T(8,128)S(1)}, f32[3,16,256]{2,1,0:T(8,128)}, u32[]{:S(2)}) copy-start(f32[3,16,256]{2,1,0:T(8,128)} %param.27) | copy-start | bytes 147460
  43.5 7.5 %copy-start.3 = (f32[3,16,256]{2,1,0:T(8,128)S(1)}, f32[3,16,256]{2,1,0:T(8,128)}, u32[]{:S(2)}) copy-start(f32[3,16,256]{2,1,0:T(8,128)} %param.28) | copy-start | bytes 147460
  43.5 7.5 %copy-start.5 = (f32[64,128]{1,0:T(8,128)S(1)}, f32[64,128]{1,0:T(8,128)}, u32[]{:S(2)}) copy-start(f32[64,128]{1,0:T(8,128)} %get-tuple-element.30.refs_7_) | copy-start | bytes 98308
  53.5 19.0 %all-to-all-start.2 = ((f32[192,2,128]{2,1,0:T(2,128)}), f32[192,2,128]{2,1,0:T(2,128)S(1)}, u32[]{:S(2)}, u32[]{:S(2)}) async-start(f32[192,2,128]{2,1,0:T(2,128)} %bitcast.33), calls=%async_computation.2 | async-start | bytes 393216 | tf_op jit(solution)/shard_map/all_to_all | solution.py:449

commit v11 on v9

--- a/solution.py
+++ b/solution.py
@@ -378,12 +378,31 @@
             state = (wmv, wav, zero_b, zero_b)
             far_slot = recv_ref[...].T
             zc = jnp.zeros((nrow, cuts), F32)
-            far_c = give(rows(far_slot[0:nrow], far_slot[nrow:2 * nrow]), slot_t)
-            far_cross = (far_c[0:nrow], far_c[nrow:], zc, zc)
-            warm_near = take(rows(wmv, wav), inc_near)
-            pick_near = (warm_near[0:nrow], warm_near[nrow:], zc, zc)
-            carry_c, fc, _ = advance(None, pick_near, far_cross, prm_cut)
-            totals = tin_ref[...] + tm_ref[...] + give(fc, inc_near).reshape(4, nrow, buses)
+            hr = nrow // 2
+            low = lax.broadcasted_iota(jnp.int32, (hr, 2 * cuts), 1) < cuts
+            wide = lambda v: jnp.concatenate([v, v], axis=1)
+            inc2 = onehot(wide(cprm_v[0:1]).astype(jnp.int32), buses)
+
+            def pack(v):
+                return jnp.where(low, v[:hr], v[hr:])
+
+            far_c = give(rows(far_slot[0:nrow], far_slot[nrow:2 * nrow]), rows(slot_t, slot_t))
+            zp = jnp.zeros((hr, 2 * cuts), F32)
+            far_cross = (pack(far_c[0:nrow]), pack(far_c[nrow:]), zp, zp)
+            warm_near = take(rows(wmv, wav), inc2)
+            pick_near = (pack(warm_near[0:nrow]), pack(warm_near[nrow:]), zp, zp)
+            carry_p, fc, _ = advance(None, pick_near, far_cross, tuple(wide(v) for v in prm_cut))
+            t_low = give(jnp.where(rows(*(low,) * 4), fc, 0.0), inc2)
+            t_high = give(jnp.where(rows(*(low,) * 4), 0.0, fc), inc2)
+            cross_t = rows(*(x for i in range(4) for x in (t_low[i * hr:(i + 1) * hr], t_high[i * hr:(i + 1) * hr])))
+            totals = tin_ref[...] + tm_ref[...] + cross_t.reshape(4, nrow, buses)
+            flat = rows(*carry_p[0], *carry_p[1], *carry_p[2])
+            lanes = lax.broadcasted_iota(jnp.int32, (2 * cuts, cuts), 0)
+            cols = lax.broadcasted_iota(jnp.int32, (2 * cuts, cuts), 1)
+            u_low = take(flat, (lanes == cols).astype(BF))
+            u_high = take(flat, (lanes == cols + cuts).astype(BF))
+            unp = [rows(u_low[a * hr:(a + 1) * hr], u_high[a * hr:(a + 1) * hr]) for a in range(10)]
+            carry_c = (tuple(unp[0:4]), tuple(unp[4:8]), (unp[8], unp[9]))
         else:
             (cc_in_ref, cm_ref, pn_ref, prc_ref, mag_out, ang_out, pr_out, plane_ref) = rest
             state = tuple(st_ref[i] for i in range(4))

time: 76 us -> 75.9 us (level)
  no operation moved by 1% of the time
where the time goes in v11:
time: 75.9 us; the launch traced here: 74.9 us
  starting transfers between devices  36.9 us (49%)
  waiting for transfers between devices  20.9 us (28%)
  Pallas kernels  14.7 us (19%)
  local copies, waits for them, and re-layouts  1.45 us (2%)
  between operations  0.96 us (1%)
    all_to_all x1, starting transfers between devices, on_device(): recv_setup = lax.all_to_all(pay_setup, 'net', 0, 0, tiled=True)  17.3 us
    pallas_call x6, Pallas kernels, vmem_call(): pl.pallas_call(kernel, out_shape=outs, in_specs=[pl.BlockSpec(memory_spac...  12.6 us
    all_to_all x1, waiting for transfers between devices, on_device(): lax.all_to_all(pay_1.reshape(3 * parts, 2, 128), 'net', 0, 0, tiled=True)  9.7 us
    all_to_all x1, starting transfers between devices, on_device(): recv_0 = lax.all_to_all(pay_0, 'net', 0, 0, tiled=True)  7.44 us
    all_to_all x1, starting transfers between devices, on_device(): lax.all_to_all(pay_1.reshape(3 * parts, 2, 128), 'net', 0, 0, tiled=True)  6.27 us
    all_to_all x1, waiting for transfers between devices, on_device(): recv_0 = lax.all_to_all(pay_0, 'net', 0, 0, tiled=True)  6.08 us
    all_to_all x1, waiting for transfers between devices, on_device(): recv_setup = lax.all_to_all(pay_setup, 'net', 0, 0, tiled=True)  5.14 us
    ppermute x1, starting transfers between devices, on_device(): lax.ppermute(sr[nrow - halo:], 'tm', [(i, i + 1) for i in range(ntm - 1)])  3.96 us
  transfers between devices with their start and end apart: 5, of which 3 were waited for; matrix products, arithmetic and copies ran while one was open for 0% of the time, Pallas kernels for 10%

profile of v11, /device:TPU:1, one launch (start us, length us, event | category | flops | bytes accessed | tf_op | source)
XLA Modules:
  0.0 74.9 jit_solution(9867145495939501019)
XLA Ops:
  0.6 2.1 %shard_map.272 = (f32[64,128]{1,0:T(8,128)}, f32[128,128]{1,0:T(8,128)}) custom-call(s32[1,64]{1,0:T(1,128)} %bitcast.103, s32[1,64]{1,0:T(1,128)} %bitcast.72, s32[1,64]{1,0:T(1,128)} %bitcast.104, f32[1,64]{1,0:T(1,128)} %bitcast.96, f32[1,64]{1,0:T(1,128)} %bitcast.98, f32[1,64]{1,0:T(1,128)} %bitcast.100, s32[1,64]{1,0:T(1,128)} %bitcast.102, ...), custom_call_target="tpu_custom_call" | custom-call | tf_op jit(solution)/shard_map/pallas_call | solution.py:255
  2.7 0.0 copy-start.4
  2.7 0.0 copy-start.1
  2.8 17.3 %all-to-all-start = ((f32[64,2,128]{2,1,0:T(2,128)}), f32[64,2,128]{2,1,0:T(2,128)S(1)}, u32[]{:S(2)}, u32[]{:S(2)}) async-start(f32[64,2,128]{2,1,0:T(2,128)} %bitcast.93), calls=%async_computation | async-start | bytes 131072 | tf_op jit(solution)/shard_map/all_to_all | solution.py:262
  20.1 0.0 copy-start
  20.1 4.0 %collective-permute-start = (f32[32,32]{1,0:T(8,128)S(1)}, f32[32,32]{1,0:T(8,128)S(1)}, u32[]{:S(2)}, u32[]{:S(2)}) collective-permute-start(f32[32,32]{1,0:T(8,128)S(1)} %bitcast.95), channel_id=1, source_target_pairs={{0,1},{1,2},{2,3},{3,4},{4,5},{5,6},{6,7},{8,9},{9,10},{10,11},{11... | collective-permute-start | bytes 12296 | tf_op jit(solution)/shard_map/ppermute | solution.py:207
  24.0 1.9 %collective-permute-start.1 = (f32[32,32]{1,0:T(8,128)S(1)}, f32[32,32]{1,0:T(8,128)S(1)}, u32[]{:S(2)}, u32[]{:S(2)}) collective-permute-start(f32[32,32]{1,0:T(8,128)S(1)} %bitcast.94), channel_id=1, source_target_pairs={{1,0},{2,1},{3,2},{4,3},{5,4},{6,5},{7,6},{9,8},{10,9},{11,10},{12... | collective-permute-start | bytes 12296 | tf_op jit(solution)/shard_map/ppermute | solution.py:208
  26.0 5.1 %all-to-all-done = f32[64,2,128]{2,1,0:T(2,128)S(1)} async-done(((f32[64,2,128]{2,1,0:T(2,128)}), f32[64,2,128]{2,1,0:T(2,128)S(1)}, u32[]{:S(2)}, u32[]{:S(2)}) %all-to-all-start) | async-done | bytes 65568 | tf_op jit(solution)/shard_map/all_to_all | solution.py:262
  31.1 1.0 %shard_map.273 = (f32[128,128]{1,0:T(8,128)S(1)}, f32[128,128]{1,0:T(8,128)}) custom-call(f32[128,128]{1,0:T(8,128)S(1)} %bitcast.57, f32[48,256]{1,0:T(8,128)S(1)} %bitcast.43, f32[48,256]{1,0:T(8,128)S(1)} %bitcast.50), custom_call_target="tpu_custom_call" | custom-call | tf_op jit(solution)/shard_map/pallas_call | solution.py:171
  32.1 7.4 %all-to-all-start.1 = ((f32[64,2,128]{2,1,0:T(2,128)}), f32[64,2,128]{2,1,0:T(2,128)S(1)}, u32[]{:S(2)}, u32[]{:S(2)}) async-start(f32[64,2,128]{2,1,0:T(2,128)} %bitcast.13), calls=%async_computation.1 | async-start | bytes 131072 | tf_op jit(solution)/shard_map/all_to_all | solution.py:276
  39.6 0.0 copy-start.20
  39.6 0.0 copy-start.21
  39.6 0.6 copy-done.23
  40.4 0.0 copy-start.12
  40.5 0.5 copy-done.6
  41.0 0.0 copy-done.8
  41.0 0.0 copy-done.11
  41.0 0.0 copy-done.12
  41.1 0.0 copy-done.13
  41.1 0.0 copy-done.15
  41.1 0.0 copy-done.16
  41.1 0.0 copy-done.17
  41.1 0.0 copy-done.18
  41.1 0.0 copy-done.7
  41.2 2.4 %shard_map.275 = (f32[4,48,256]{2,1,0:T(8,128)S(1)}, f32[2,48,256]{2,1,0:T(8,128)S(1)}, f32[10,48,256]{2,1,0:T(8,128)S(1)}, f32[80,32]{1,0:T(8,128)S(1)}, f32[48,32]{1,0:T(8,128)S(1)}) custom-call(f32[48,256]{1,0:T(8,128)S(1)} %bitcast.44, f32[48,256]{1,0:T(8,128)S(1)} %bitcast.51, s32[1,256]{1,0:T(1,128)S(1)} %bitcast.64, s32[1,256]{1,0:T(1,128)S(1)} %bitcast.67, ...), custom_call_target="tpu_custom_call" | custom-call | tf_op jit(solution)/shard_map/pallas_call | solution.py:171
  43.6 1.4 %shard_map.274 = (f32[4,48,256]{2,1,0:T(8,128)S(1)}, f32[10,48,128]{2,1,0:T(8,128)S(1)}, f32[8,256]{1,0:T(8,128)S(1)}) custom-call(f32[128,128]{1,0:T(8,128)S(1)} %get-tuple-element.31.mirror_ref.refs_6_.refs_18_, f32[48,256]{1,0:T(8,128)S(1)} %bitcast.45, f32[48,256]{1,0:T(8,128)S(1)} %bitcast.52, s32[1,256]{1,0:T(1,128)S(1)} %bitcast.65, ...), custom_call_target="tpu_custom_call" | custom-call | tf_op jit(solution)/shard_map/pallas_call | solution.py:171
  45.0 6.1 %all-to-all-done.1 = f32[64,2,128]{2,1,0:T(2,128)S(1)} async-done(((f32[64,2,128]{2,1,0:T(2,128)}), f32[64,2,128]{2,1,0:T(2,128)S(1)}, u32[]{:S(2)}, u32[]{:S(2)}) %all-to-all-start.1) | async-done | bytes 65568 | tf_op jit(solution)/shard_map/all_to_all | solution.py:276
  51.1 2.3 %shard_map.276 = (f32[10,48,64]{2,1,0:T(8,128)S(1)}, f32[4,48,256]{2,1,0:T(8,128)S(1)}, f32[384,128]{1,0:T(8,128)}) custom-call(f32[48,256]{1,0:T(8,128)S(1)} %bitcast.46, f32[48,256]{1,0:T(8,128)S(1)} %bitcast.47, f32[48,256]{1,0:T(8,128)S(1)} %bitcast.53, f32[48,256]{1,0:T(8,128)S(1)} %bitcast.58, f32[48,256]{1,0:T(8,128)S(1)} %bitcast.60, ...), custom_call_target="tpu_custom_call" | custom-call | tf_op jit(solution)/shard_map/pallas_call | solution.py:171
  53.4 6.3 %all-to-all-start.2 = ((f32[192,2,128]{2,1,0:T(2,128)}), f32[192,2,128]{2,1,0:T(2,128)S(1)}, u32[]{:S(2)}, u32[]{:S(2)}) async-start(f32[192,2,128]{2,1,0:T(2,128)} %bitcast.33), calls=%async_computation.2 | async-start | bytes 393216 | tf_op jit(solution)/shard_map/all_to_all | solution.py:469
  59.7 2.9 %shard_map.277 = (f32[4,48,256]{2,1,0:T(8,128)S(1)}, f32[2,48,256]{2,1,0:T(8,128)S(1)}, f32[48,32]{1,0:T(8,128)}, f32[48,32]{1,0:T(8,128)}, f32[192,64]{1,0:T(8,128)S(1)}, /*index=5*/f32[192,128]{1,0:T(8,128)S(1)}) custom-call(f32[4,48,256]{2,1,0:T(8,128)S(1)} %get-tuple-element.37.refs_0_, s32[1,256]{1,0:T(1,128)S(1)} %bitcast.66, s32[1,256]{1,0:T(1,128)S(1)} %bitcast.69, ...), custom_call_target="tpu_custom_call" | custom-call | tf_op jit(solution)/shard_map/pallas_call | solution.py:171
  62.7 9.7 %all-to-all-done.2 = f32[192,2,128]{2,1,0:T(2,128)S(1)} async-done(((f32[192,2,128]{2,1,0:T(2,128)}), f32[192,2,128]{2,1,0:T(2,128)S(1)}, u32[]{:S(2)}, u32[]{:S(2)}) %all-to-all-start.2) | async-done | bytes 196640 | tf_op jit(solution)/shard_map/all_to_all | solution.py:469
  72.4 2.5 %shard_map.278 = (f32[48,256]{1,0:T(8,128)}, f32[48,256]{1,0:T(8,128)}, f32[48,256]{1,0:T(8,128)}) custom-call(f32[4,48,256]{2,1,0:T(8,128)S(1)} %get-tuple-element.37.refs_0_, f32[48,256]{1,0:T(8,128)S(1)} %bitcast.48, f32[48,256]{1,0:T(8,128)S(1)} %bitcast.54, f32[48,256]{1,0:T(8,128)S(1)} %bitcast.59, f32[48,256]{1,0:T(8,128)S(1)} %bitcast.61, ...), custom_call_target="tpu_custom_call" | custom-call | tf_op jit(solution)/shard_map/pallas_call | solution.py:171
  (39 shorter events, 0.1 us)
Async XLA Ops:
  2.7 17.3 %copy-start.4 = (f32[3,16,32]{2,1,0:T(8,128)S(1)}, f32[3,16,32]{2,1,0:T(8,128)}, u32[]{:S(2)}) copy-start(f32[3,16,32]{2,1,0:T(8,128)} %param.29) | copy-start | bytes 18436
  2.7 28.4 %copy-start.1 = (f32[3,16,256]{2,1,0:T(8,128)S(1)}, f32[3,16,256]{2,1,0:T(8,128)}, u32[]{:S(2)}) copy-start(f32[3,16,256]{2,1,0:T(8,128)} %param.26) | copy-start | bytes 147460
  2.8 28.4 %all-to-all-start = ((f32[64,2,128]{2,1,0:T(2,128)}), f32[64,2,128]{2,1,0:T(2,128)S(1)}, u32[]{:S(2)}, u32[]{:S(2)}) async-start(f32[64,2,128]{2,1,0:T(2,128)} %bitcast.93), calls=%async_computation | async-start | bytes 131072 | tf_op jit(solution)/shard_map/all_to_all | solution.py:262
  20.1 11.1 %copy-start = (f32[3,16,256]{2,1,0:T(8,128)S(1)}, f32[3,16,256]{2,1,0:T(8,128)}, u32[]{:S(2)}) copy-start(f32[3,16,256]{2,1,0:T(8,128)} %param.25) | copy-start | bytes 147460
  20.1 20.2 %collective-permute-start = (f32[32,32]{1,0:T(8,128)S(1)}, f32[32,32]{1,0:T(8,128)S(1)}, u32[]{:S(2)}, u32[]{:S(2)}) collective-permute-start(f32[32,32]{1,0:T(8,128)S(1)} %bitcast.95), channel_id=1, source_target_pairs={{0,1},{1,2},{2,3},{3,4},{4,5},{5,6},{6,7},{8,9},{9,10},{10,11},{11... | collective-permute-start | bytes 12296 | tf_op jit(solution)/shard_map/ppermute | solution.py:207
  24.0 16.3 %collective-permute-start.1 = (f32[32,32]{1,0:T(8,128)S(1)}, f32[32,32]{1,0:T(8,128)S(1)}, u32[]{:S(2)}, u32[]{:S(2)}) collective-permute-start(f32[32,32]{1,0:T(8,128)S(1)} %bitcast.94), channel_id=1, source_target_pairs={{1,0},{2,1},{3,2},{4,3},{5,4},{6,5},{7,6},{9,8},{10,9},{11,10},{12... | collective-permute-start | bytes 12296 | tf_op jit(solution)/shard_map/ppermute | solution.py:208
  32.1 7.5 %copy-start.9 = (s32[64]{0:T(128)S(1)}, s32[64]{0:T(128)}, u32[]{:S(2)}) copy-start(s32[64]{0:T(128)} %param.43) | copy-start | bytes 772
  32.1 7.5 %copy-start.22 = (s32[64]{0:T(128)S(1)}, s32[64]{0:T(128)}, u32[]{:S(2)}) copy-start(s32[64]{0:T(128)} %param.49) | copy-start | bytes 772
  32.1 19.0 %all-to-all-start.1 = ((f32[64,2,128]{2,1,0:T(2,128)}), f32[64,2,128]{2,1,0:T(2,128)S(1)}, u32[]{:S(2)}, u32[]{:S(2)}) async-start(f32[64,2,128]{2,1,0:T(2,128)} %bitcast.13), calls=%async_computation.1 | async-start | bytes 131072 | tf_op jit(solution)/shard_map/all_to_all | solution.py:276
  39.6 0.7 copy-start.23
  39.6 0.7 copy-start.19
  39.6 0.7 copy-start.20
  39.6 0.7 copy-start.21
  40.3 0.7 copy-start.6
  40.3 0.7 copy-start.8
  40.3 0.7 copy-start.11
  40.4 0.7 copy-start.12
  40.4 0.7 copy-start.13
  40.4 0.7 copy-start.14
  40.4 0.7 copy-start.15
  40.4 0.7 copy-start.16
  40.4 0.7 copy-start.17
  40.4 0.7 copy-start.18
  40.4 0.7 copy-start.7
  40.5 0.7 copy-start.10
  43.6 7.6 %copy-start.2 = (f32[3,16,256]{2,1,0:T(8,128)S(1)}, f32[3,16,256]{2,1,0:T(8,128)}, u32[]{:S(2)}) copy-start(f32[3,16,256]{2,1,0:T(8,128)} %param.27) | copy-start | bytes 147460
  43.6 7.5 %copy-start.3 = (f32[3,16,256]{2,1,0:T(8,128)S(1)}, f32[3,16,256]{2,1,0:T(8,128)}, u32[]{:S(2)}) copy-start(f32[3,16,256]{2,1,0:T(8,128)} %param.28) | copy-start | bytes 147460
  43.6 7.5 %copy-start.5 = (f32[64,128]{1,0:T(8,128)S(1)}, f32[64,128]{1,0:T(8,128)}, u32[]{:S(2)}) copy-start(f32[64,128]{1,0:T(8,128)} %get-tuple-element.32.refs_7_) | copy-start | bytes 98308
  53.4 18.9 %all-to-all-start.2 = ((f32[192,2,128]{2,1,0:T(2,128)}), f32[192,2,128]{2,1,0:T(2,128)S(1)}, u32[]{:S(2)}, u32[]{:S(2)}) async-start(f32[192,2,128]{2,1,0:T(2,128)} %bitcast.33), calls=%async_computation.2 | async-start | bytes 393216 | tf_op jit(solution)/shard_map/all_to_all | solution.py:469

commit v12 on v11

--- a/solution.py
+++ b/solution.py
@@ -413,15 +413,32 @@
                 blocks.append(plane_ref[...].T)
             both = rows(*blocks)
             near_mirror = split4(both[0:4 * nrow], nrow)
-            far_cross = split4(give(both[4 * nrow:], slot_t), nrow)
-            pick_near = split4(pn_ref[...], nrow)
+            hr = nrow // 2
+            low = lax.broadcasted_iota(jnp.int32, (hr, 2 * cuts), 1) < cuts
+            wide = lambda v: jnp.concatenate([v, v], axis=1)
+            inc2 = onehot(wide(cprm_v[0:1]).astype(jnp.int32), buses)
+
+            def pack(v):
+                return jnp.where(low, v[:hr], v[hr:])
+
+            def pack_narrow(v):
+                return jnp.where(low, wide(v[:hr]), wide(v[hr:]))
+
+            far_w = give(both[4 * nrow:], rows(slot_t, slot_t))
+            far_cross = tuple(pack(x) for x in split4(far_w, nrow))
+            pick_near = tuple(pack_narrow(x) for x in split4(pn_ref[...], nrow))
             pick_recv = split4(prc_ref[...], nrow)
-            carry_c_in = load_carry(cc_in_ref)
+            cc_in = load_carry(cc_in_ref)
+            carry_c_in = (tuple(pack_narrow(x) for x in cc_in[0]), tuple(pack_narrow(x) for x in cc_in[1]),
+                          tuple(pack_narrow(x) for x in cc_in[2]))
             carry_m_in = load_carry(cm_ref)
-            _, fc, _ = advance(carry_c_in, pick_near, far_cross, prm_cut)
+            _, fc, _ = advance(carry_c_in, pick_near, far_cross, tuple(wide(v) for v in prm_cut))
+            t_low = give(jnp.where(rows(*(low,) * 4), fc, 0.0), inc2)
+            t_high = give(jnp.where(rows(*(low,) * 4), 0.0, fc), inc2)
+            cross_t = rows(*(x for i in range(4) for x in (t_low[i * hr:(i + 1) * hr], t_high[i * hr:(i + 1) * hr])))
             prm_mir = (mirror[1:2], mirror[2:3], mirror[3:4], mirror[4:5])
             _, _, tmr = advance(carry_m_in, near_mirror, pick_recv, prm_mir)
-            totals = tin_ref[...] + (give(fc, inc_near) + give(tmr, inc_recv)).reshape(4, nrow, buses)
+            totals = tin_ref[...] + (cross_t + give(tmr, inc_recv)).reshape(4, nrow, buses)
         mag = (totals[0] + wmv) / (degree + 1.0)
         ang = (totals[1] + wav) / (degree + 1.0)
         weight = 1.0 + BALANCE_WEIGHT * (gen_count + degree)

time: 75.9 us -> 75.7 us (level)
  no operation moved by 1% of the time
where the time goes in v12:
time: 75.7 us; the launch traced here: 74.7 us
  starting transfers between devices  36.9 us (49%)
  waiting for transfers between devices  20.9 us (28%)
  Pallas kernels  14.4 us (19%)
  local copies, waits for them, and re-layouts  1.45 us (2%)
  between operations  0.96 us (1%)
    all_to_all x1, starting transfers between devices, on_device(): recv_setup = lax.all_to_all(pay_setup, 'net', 0, 0, tiled=True)  17.3 us
    pallas_call x6, Pallas kernels, vmem_call(): pl.pallas_call(kernel, out_shape=outs, in_specs=[pl.BlockSpec(memory_spac...  12.3 us
    all_to_all x1, waiting for transfers between devices, on_device(): lax.all_to_all(pay_1.reshape(3 * parts, 2, 128), 'net', 0, 0, tiled=True)  9.7 us
    all_to_all x1, starting transfers between devices, on_device(): recv_0 = lax.all_to_all(pay_0, 'net', 0, 0, tiled=True)  7.44 us
    all_to_all x1, starting transfers between devices, on_device(): lax.all_to_all(pay_1.reshape(3 * parts, 2, 128), 'net', 0, 0, tiled=True)  6.27 us
    all_to_all x1, waiting for transfers between devices, on_device(): recv_0 = lax.all_to_all(pay_0, 'net', 0, 0, tiled=True)  6.08 us
    all_to_all x1, waiting for transfers between devices, on_device(): recv_setup = lax.all_to_all(pay_setup, 'net', 0, 0, tiled=True)  5.14 us
    ppermute x1, starting transfers between devices, on_device(): lax.ppermute(sr[nrow - halo:], 'tm', [(i, i + 1) for i in range(ntm - 1)])  3.96 us
  transfers between devices with their start and end apart: 5, of which 3 were waited for; matrix products, arithmetic and copies ran while one was open for 0% of the time, Pallas kernels for 10%

profile of v12, /device:TPU:1, one launch (start us, length us, event | category | flops | bytes accessed | tf_op | source)
XLA Modules:
  0.0 74.7 jit_solution(9307420034920882029)
XLA Ops:
  0.6 2.1 %shard_map.272 = (f32[64,128]{1,0:T(8,128)}, f32[128,128]{1,0:T(8,128)}) custom-call(s32[1,64]{1,0:T(1,128)} %bitcast.103, s32[1,64]{1,0:T(1,128)} %bitcast.72, s32[1,64]{1,0:T(1,128)} %bitcast.104, f32[1,64]{1,0:T(1,128)} %bitcast.96, f32[1,64]{1,0:T(1,128)} %bitcast.98, f32[1,64]{1,0:T(1,128)} %bitcast.100, s32[1,64]{1,0:T(1,128)} %bitcast.102, ...), custom_call_target="tpu_custom_call" | custom-call | tf_op jit(solution)/shard_map/pallas_call | solution.py:255
  2.7 0.0 copy-start.1
  2.8 17.3 %all-to-all-start = ((f32[64,2,128]{2,1,0:T(2,128)}), f32[64,2,128]{2,1,0:T(2,128)S(1)}, u32[]{:S(2)}, u32[]{:S(2)}) async-start(f32[64,2,128]{2,1,0:T(2,128)} %bitcast.93), calls=%async_computation | async-start | bytes 131072 | tf_op jit(solution)/shard_map/all_to_all | solution.py:262
  20.1 4.0 %collective-permute-start = (f32[32,32]{1,0:T(8,128)S(1)}, f32[32,32]{1,0:T(8,128)S(1)}, u32[]{:S(2)}, u32[]{:S(2)}) collective-permute-start(f32[32,32]{1,0:T(8,128)S(1)} %bitcast.95), channel_id=1, source_target_pairs={{0,1},{1,2},{2,3},{3,4},{4,5},{5,6},{6,7},{8,9},{9,10},{10,11},{11... | collective-permute-start | bytes 12296 | tf_op jit(solution)/shard_map/ppermute | solution.py:207
  24.0 1.9 %collective-permute-start.1 = (f32[32,32]{1,0:T(8,128)S(1)}, f32[32,32]{1,0:T(8,128)S(1)}, u32[]{:S(2)}, u32[]{:S(2)}) collective-permute-start(f32[32,32]{1,0:T(8,128)S(1)} %bitcast.94), channel_id=1, source_target_pairs={{1,0},{2,1},{3,2},{4,3},{5,4},{6,5},{7,6},{9,8},{10,9},{11,10},{12... | collective-permute-start | bytes 12296 | tf_op jit(solution)/shard_map/ppermute | solution.py:208
  26.0 5.1 %all-to-all-done = f32[64,2,128]{2,1,0:T(2,128)S(1)} async-done(((f32[64,2,128]{2,1,0:T(2,128)}), f32[64,2,128]{2,1,0:T(2,128)S(1)}, u32[]{:S(2)}, u32[]{:S(2)}) %all-to-all-start) | async-done | bytes 65568 | tf_op jit(solution)/shard_map/all_to_all | solution.py:262
  31.1 1.0 %shard_map.273 = (f32[128,128]{1,0:T(8,128)S(1)}, f32[128,128]{1,0:T(8,128)}) custom-call(f32[128,128]{1,0:T(8,128)S(1)} %bitcast.57, f32[48,256]{1,0:T(8,128)S(1)} %bitcast.43, f32[48,256]{1,0:T(8,128)S(1)} %bitcast.50), custom_call_target="tpu_custom_call" | custom-call | tf_op jit(solution)/shard_map/pallas_call | solution.py:171
  32.1 7.4 %all-to-all-start.1 = ((f32[64,2,128]{2,1,0:T(2,128)}), f32[64,2,128]{2,1,0:T(2,128)S(1)}, u32[]{:S(2)}, u32[]{:S(2)}) async-start(f32[64,2,128]{2,1,0:T(2,128)} %bitcast.13), calls=%async_computation.1 | async-start | bytes 131072 | tf_op jit(solution)/shard_map/all_to_all | solution.py:276
  39.6 0.0 copy-start.23
  39.6 0.0 copy-start.21
  39.6 0.6 copy-done.23
  40.3 0.0 copy-start.8
  40.4 0.0 copy-start.13
  40.4 0.0 copy-start.14
  40.5 0.5 copy-done.6
  41.0 0.0 copy-done.8
  41.0 0.0 copy-done.11
  41.0 0.0 copy-done.12
  41.1 0.0 copy-done.13
  41.1 0.0 copy-done.15
  41.1 0.0 copy-done.16
  41.1 0.0 copy-done.17
  41.1 0.0 copy-done.18
  41.1 0.0 copy-done.7
  41.2 2.4 %shard_map.275 = (f32[4,48,256]{2,1,0:T(8,128)S(1)}, f32[2,48,256]{2,1,0:T(8,128)S(1)}, f32[10,48,256]{2,1,0:T(8,128)S(1)}, f32[80,32]{1,0:T(8,128)S(1)}, f32[48,32]{1,0:T(8,128)S(1)}) custom-call(f32[48,256]{1,0:T(8,128)S(1)} %bitcast.44, f32[48,256]{1,0:T(8,128)S(1)} %bitcast.51, s32[1,256]{1,0:T(1,128)S(1)} %bitcast.64, s32[1,256]{1,0:T(1,128)S(1)} %bitcast.67, ...), custom_call_target="tpu_custom_call" | custom-call | tf_op jit(solution)/shard_map/pallas_call | solution.py:171
  43.6 1.4 %shard_map.274 = (f32[4,48,256]{2,1,0:T(8,128)S(1)}, f32[10,48,128]{2,1,0:T(8,128)S(1)}, f32[8,256]{1,0:T(8,128)S(1)}) custom-call(f32[128,128]{1,0:T(8,128)S(1)} %get-tuple-element.31.mirror_ref.refs_6_.refs_18_, f32[48,256]{1,0:T(8,128)S(1)} %bitcast.45, f32[48,256]{1,0:T(8,128)S(1)} %bitcast.52, s32[1,256]{1,0:T(1,128)S(1)} %bitcast.65, ...), custom_call_target="tpu_custom_call" | custom-call | tf_op jit(solution)/shard_map/pallas_call | solution.py:171
  45.0 6.1 %all-to-all-done.1 = f32[64,2,128]{2,1,0:T(2,128)S(1)} async-done(((f32[64,2,128]{2,1,0:T(2,128)}), f32[64,2,128]{2,1,0:T(2,128)S(1)}, u32[]{:S(2)}, u32[]{:S(2)}) %all-to-all-start.1) | async-done | bytes 65568 | tf_op jit(solution)/shard_map/all_to_all | solution.py:276
  51.1 2.3 %shard_map.276 = (f32[10,48,64]{2,1,0:T(8,128)S(1)}, f32[4,48,256]{2,1,0:T(8,128)S(1)}, f32[384,128]{1,0:T(8,128)}) custom-call(f32[48,256]{1,0:T(8,128)S(1)} %bitcast.46, f32[48,256]{1,0:T(8,128)S(1)} %bitcast.47, f32[48,256]{1,0:T(8,128)S(1)} %bitcast.53, f32[48,256]{1,0:T(8,128)S(1)} %bitcast.58, f32[48,256]{1,0:T(8,128)S(1)} %bitcast.60, ...), custom_call_target="tpu_custom_call" | custom-call | tf_op jit(solution)/shard_map/pallas_call | solution.py:171
  53.4 6.3 %all-to-all-start.2 = ((f32[192,2,128]{2,1,0:T(2,128)}), f32[192,2,128]{2,1,0:T(2,128)S(1)}, u32[]{:S(2)}, u32[]{:S(2)}) async-start(f32[192,2,128]{2,1,0:T(2,128)} %bitcast.33), calls=%async_computation.2 | async-start | bytes 393216 | tf_op jit(solution)/shard_map/all_to_all | solution.py:486
  59.7 2.9 %shard_map.277 = (f32[4,48,256]{2,1,0:T(8,128)S(1)}, f32[2,48,256]{2,1,0:T(8,128)S(1)}, f32[48,32]{1,0:T(8,128)}, f32[48,32]{1,0:T(8,128)}, f32[192,64]{1,0:T(8,128)S(1)}, /*index=5*/f32[192,128]{1,0:T(8,128)S(1)}) custom-call(f32[4,48,256]{2,1,0:T(8,128)S(1)} %get-tuple-element.37.refs_0_, s32[1,256]{1,0:T(1,128)S(1)} %bitcast.66, s32[1,256]{1,0:T(1,128)S(1)} %bitcast.69, ...), custom_call_target="tpu_custom_call" | custom-call | tf_op jit(solution)/shard_map/pallas_call | solution.py:171
  62.7 9.7 %all-to-all-done.2 = f32[192,2,128]{2,1,0:T(2,128)S(1)} async-done(((f32[192,2,128]{2,1,0:T(2,128)}), f32[192,2,128]{2,1,0:T(2,128)S(1)}, u32[]{:S(2)}, u32[]{:S(2)}) %all-to-all-start.2) | async-done | bytes 196640 | tf_op jit(solution)/shard_map/all_to_all | solution.py:486
  72.4 2.3 %shard_map.278 = (f32[48,256]{1,0:T(8,128)}, f32[48,256]{1,0:T(8,128)}, f32[48,256]{1,0:T(8,128)}) custom-call(f32[4,48,256]{2,1,0:T(8,128)S(1)} %get-tuple-element.37.refs_0_, f32[48,256]{1,0:T(8,128)S(1)} %bitcast.48, f32[48,256]{1,0:T(8,128)S(1)} %bitcast.54, f32[48,256]{1,0:T(8,128)S(1)} %bitcast.59, f32[48,256]{1,0:T(8,128)S(1)} %bitcast.61, ...), custom_call_target="tpu_custom_call" | custom-call | tf_op jit(solution)/shard_map/pallas_call | solution.py:171
  (39 shorter events, 0.1 us)
Async XLA Ops:
  2.7 17.3 %copy-start.4 = (f32[3,16,32]{2,1,0:T(8,128)S(1)}, f32[3,16,32]{2,1,0:T(8,128)}, u32[]{:S(2)}) copy-start(f32[3,16,32]{2,1,0:T(8,128)} %param.29) | copy-start | bytes 18436
  2.7 28.4 %copy-start.1 = (f32[3,16,256]{2,1,0:T(8,128)S(1)}, f32[3,16,256]{2,1,0:T(8,128)}, u32[]{:S(2)}) copy-start(f32[3,16,256]{2,1,0:T(8,128)} %param.26) | copy-start | bytes 147460
  2.8 28.4 %all-to-all-start = ((f32[64,2,128]{2,1,0:T(2,128)}), f32[64,2,128]{2,1,0:T(2,128)S(1)}, u32[]{:S(2)}, u32[]{:S(2)}) async-start(f32[64,2,128]{2,1,0:T(2,128)} %bitcast.93), calls=%async_computation | async-start | bytes 131072 | tf_op jit(solution)/shard_map/all_to_all | solution.py:262
  20.1 11.1 %copy-start = (f32[3,16,256]{2,1,0:T(8,128)S(1)}, f32[3,16,256]{2,1,0:T(8,128)}, u32[]{:S(2)}) copy-start(f32[3,16,256]{2,1,0:T(8,128)} %param.25) | copy-start | bytes 147460
  20.1 20.2 %collective-permute-start = (f32[32,32]{1,0:T(8,128)S(1)}, f32[32,32]{1,0:T(8,128)S(1)}, u32[]{:S(2)}, u32[]{:S(2)}) collective-permute-start(f32[32,32]{1,0:T(8,128)S(1)} %bitcast.95), channel_id=1, source_target_pairs={{0,1},{1,2},{2,3},{3,4},{4,5},{5,6},{6,7},{8,9},{9,10},{10,11},{11... | collective-permute-start | bytes 12296 | tf_op jit(solution)/shard_map/ppermute | solution.py:207
  24.0 16.3 %collective-permute-start.1 = (f32[32,32]{1,0:T(8,128)S(1)}, f32[32,32]{1,0:T(8,128)S(1)}, u32[]{:S(2)}, u32[]{:S(2)}) collective-permute-start(f32[32,32]{1,0:T(8,128)S(1)} %bitcast.94), channel_id=1, source_target_pairs={{1,0},{2,1},{3,2},{4,3},{5,4},{6,5},{7,6},{9,8},{10,9},{11,10},{12... | collective-permute-start | bytes 12296 | tf_op jit(solution)/shard_map/ppermute | solution.py:208
  32.1 7.5 %copy-start.9 = (s32[64]{0:T(128)S(1)}, s32[64]{0:T(128)}, u32[]{:S(2)}) copy-start(s32[64]{0:T(128)} %param.43) | copy-start | bytes 772
  32.1 7.5 %copy-start.22 = (s32[64]{0:T(128)S(1)}, s32[64]{0:T(128)}, u32[]{:S(2)}) copy-start(s32[64]{0:T(128)} %param.49) | copy-start | bytes 772
  32.1 19.0 %all-to-all-start.1 = ((f32[64,2,128]{2,1,0:T(2,128)}), f32[64,2,128]{2,1,0:T(2,128)S(1)}, u32[]{:S(2)}, u32[]{:S(2)}) async-start(f32[64,2,128]{2,1,0:T(2,128)} %bitcast.13), calls=%async_computation.1 | async-start | bytes 131072 | tf_op jit(solution)/shard_map/all_to_all | solution.py:276
  39.6 0.7 copy-start.23
  39.6 0.7 copy-start.19
  39.6 0.7 copy-start.20
  39.6 0.7 copy-start.21
  40.3 0.7 copy-start.6
  40.3 0.7 copy-start.8
  40.3 0.7 copy-start.11
  40.4 0.7 copy-start.12
  40.4 0.7 copy-start.13
  40.4 0.7 copy-start.14
  40.4 0.7 copy-start.15
  40.4 0.7 copy-start.16
  40.4 0.7 copy-start.17
  40.4 0.7 copy-start.18
  40.4 0.7 copy-start.7
  40.5 0.7 copy-start.10
  43.6 7.6 %copy-start.2 = (f32[3,16,256]{2,1,0:T(8,128)S(1)}, f32[3,16,256]{2,1,0:T(8,128)}, u32[]{:S(2)}) copy-start(f32[3,16,256]{2,1,0:T(8,128)} %param.27) | copy-start | bytes 147460
  43.6 7.5 %copy-start.3 = (f32[3,16,256]{2,1,0:T(8,128)S(1)}, f32[3,16,256]{2,1,0:T(8,128)}, u32[]{:S(2)}) copy-start(f32[3,16,256]{2,1,0:T(8,128)} %param.28) | copy-start | bytes 147460
  43.6 7.5 %copy-start.5 = (f32[64,128]{1,0:T(8,128)S(1)}, f32[64,128]{1,0:T(8,128)}, u32[]{:S(2)}) copy-start(f32[64,128]{1,0:T(8,128)} %get-tuple-element.32.refs_7_) | copy-start | bytes 98308
  53.4 18.9 %all-to-all-start.2 = ((f32[192,2,128]{2,1,0:T(2,128)}), f32[192,2,128]{2,1,0:T(2,128)S(1)}, u32[]{:S(2)}, u32[]{:S(2)}) async-start(f32[192,2,128]{2,1,0:T(2,128)} %bitcast.33), calls=%async_computation.2 | async-start | bytes 393216 | tf_op jit(solution)/shard_map/all_to_all | solution.py:486

commit v13 on v11

--- a/solution.py
+++ b/solution.py
@@ -261,18 +261,15 @@
     )(*prep_args)
     recv_setup = lax.all_to_all(pay_setup, "net", 0, 0, tiled=True)
 
-    def mid_kernel(recv_ref, wm_ref, wa_ref, mirror_out, pay_out):
-        mirror = recv_ref[...].T
-        mirror_out[...] = mirror
-        inc_recv = onehot(mirror[0:1].astype(jnp.int32) - 1, buses)
-        vals = rows(take(rows(wm_ref[...], wa_ref[...]), inc_recv), jnp.zeros((nvals0 - 2 * nrow, slots), F32))
-        pay_out[...] = vals.T
-
-    mirror_t, pay_0 = vmem_call(
-        mid_kernel,
-        (jax.ShapeDtypeStruct((nvals0, slots), F32), jax.ShapeDtypeStruct((slots, nvals0), F32)),
-        recv_setup, wm, wa,
-    )
+    def mid_kernel(recv_ref, wm_ref, wa_ref, pay_out):
+        ids = recv_ref[:, 0:1].astype(jnp.int32) - 1
+        inc_t = (ids == lax.broadcasted_iota(jnp.int32, (slots, buses), 1)).astype(BF)
+        warm = rows(wm_ref[...], wa_ref[...], jnp.zeros((nvals0 - 2 * nrow, buses), F32))
+        pay_out[...] = give_left(inc_t, warm)
+
+    pay_0 = vmem_call(
+        mid_kernel, (jax.ShapeDtypeStruct((slots, nvals0), F32),), recv_setup, wm, wa,
+    )[0]
     recv_0 = lax.all_to_all(pay_0, "net", 0, 0, tiled=True)
 
     def spread(p):
@@ -341,8 +338,9 @@
         sup_out[0] = supply[0:nrow]
         sup_out[1] = supply[nrow:]
 
-    def mirror0_kernel(mirror_ref, wm_ref, wa_ref, bf_ref, bt_ref, cn_ref, gb_ref, tot_out, cm_out, dg_out):
-        mirror = mirror_ref[...]
+    def mirror0_kernel(recv_ref, wm_ref, wa_ref, bf_ref, bt_ref, cn_ref, gb_ref, tot_out, cm_out, dg_out, mir_out):
+        mirror = recv_ref[...].T
+        mir_out[...] = mirror
         inc_recv = onehot(mirror[0:1].astype(jnp.int32) - 1, buses)
         degree = (col_sum(onehot(bf_ref[...], buses)) + col_sum(onehot(bt_ref[...], buses))
                   + col_sum(onehot(cn_ref[...], buses)) + col_sum(inc_recv))
@@ -455,8 +453,9 @@
          sds((nrow, gens), F32)),
         wm, wa, *br_all, *gen_all, lo, sr, hi, sq,
     )
-    tm0, cm1, dg = vmem_call(
-        mirror0_kernel, (tot_shape, sds((10, nrow, slots), F32), sds((8, buses), F32)), mirror_t, wm, wa,
+    tm0, cm1, dg, mirror_t = vmem_call(
+        mirror0_kernel,
+        (tot_shape, sds((10, nrow, slots), F32), sds((8, buses), F32), sds((nvals0, slots), F32)), recv_setup, wm, wa,
         br_rows[0], br_rows[1], cut_rows[0], gen_rows[0],
     )
     cprm = jnp.concatenate([cut_rows[0].astype(F32), *cut_rows[1:], jnp.zeros((3, cuts), F32)], axis=0)

time: 75.9 us -> 75.8 us (level)
  no operation moved by 1% of the time
where the time goes in v13:
time: 75.8 us; the launch traced here: 74.9 us
  starting transfers between devices  36.9 us (49%)
  waiting for transfers between devices  21 us (28%)
  Pallas kernels  14.6 us (19%)
  local copies, waits for them, and re-layouts  1.45 us (2%)
  between operations  0.96 us (1%)
    all_to_all x1, starting transfers between devices, on_device(): recv_setup = lax.all_to_all(pay_setup, 'net', 0, 0, tiled=True)  17.3 us
    pallas_call x6, Pallas kernels, vmem_call(): pl.pallas_call(kernel, out_shape=outs, in_specs=[pl.BlockSpec(memory_spac...  12.5 us
    all_to_all x1, waiting for transfers between devices, on_device(): lax.all_to_all(pay_1.reshape(3 * parts, 2, 128), 'net', 0, 0, tiled=True)  9.81 us
    all_to_all x1, starting transfers between devices, on_device(): recv_0 = lax.all_to_all(pay_0, 'net', 0, 0, tiled=True)  7.44 us
    all_to_all x1, starting transfers between devices, on_device(): lax.all_to_all(pay_1.reshape(3 * parts, 2, 128), 'net', 0, 0, tiled=True)  6.33 us
    all_to_all x1, waiting for transfers between devices, on_device(): recv_0 = lax.all_to_all(pay_0, 'net', 0, 0, tiled=True)  6.03 us
    all_to_all x1, waiting for transfers between devices, on_device(): recv_setup = lax.all_to_all(pay_setup, 'net', 0, 0, tiled=True)  5.14 us
    ppermute x1, starting transfers between devices, on_device(): lax.ppermute(sr[nrow - halo:], 'tm', [(i, i + 1) for i in range(ntm - 1)])  3.96 us
  transfers between devices with their start and end apart: 5, of which 3 were waited for; matrix products, arithmetic and copies ran while one was open for 0% of the time, Pallas kernels for 10%

profile of v13, /device:TPU:1, one launch (start us, length us, event | category | flops | bytes accessed | tf_op | source)
XLA Modules:
  0.0 74.9 jit_solution(10075971007416266246)
XLA Ops:
  0.6 2.1 %shard_map.272 = (f32[64,128]{1,0:T(8,128)}, f32[128,128]{1,0:T(8,128)}) custom-call(s32[1,64]{1,0:T(1,128)} %bitcast.104, s32[1,64]{1,0:T(1,128)} %bitcast.73, s32[1,64]{1,0:T(1,128)} %bitcast.105, f32[1,64]{1,0:T(1,128)} %bitcast.97, f32[1,64]{1,0:T(1,128)} %bitcast.99, f32[1,64]{1,0:T(1,128)} %bitcast.101, s32[1,64]{1,0:T(1,128)} %bitcast.103, ...), custom_call_target="tpu_custom_call" | custom-call | tf_op jit(solution)/shard_map/pallas_call | solution.py:255
  2.7 0.0 copy-start.4
  2.8 17.3 %all-to-all-start = ((f32[64,2,128]{2,1,0:T(2,128)}), f32[64,2,128]{2,1,0:T(2,128)S(1)}, u32[]{:S(2)}, u32[]{:S(2)}) async-start(f32[64,2,128]{2,1,0:T(2,128)} %bitcast.94), calls=%async_computation | async-start | bytes 131072 | tf_op jit(solution)/shard_map/all_to_all | solution.py:262
  20.1 0.0 copy-start
  20.1 4.0 %collective-permute-start = (f32[32,32]{1,0:T(8,128)S(1)}, f32[32,32]{1,0:T(8,128)S(1)}, u32[]{:S(2)}, u32[]{:S(2)}) collective-permute-start(f32[32,32]{1,0:T(8,128)S(1)} %bitcast.96), channel_id=1, source_target_pairs={{0,1},{1,2},{2,3},{3,4},{4,5},{5,6},{6,7},{8,9},{9,10},{10,11},{11... | collective-permute-start | bytes 12296 | tf_op jit(solution)/shard_map/ppermute | solution.py:207
  24.1 1.9 %collective-permute-start.1 = (f32[32,32]{1,0:T(8,128)S(1)}, f32[32,32]{1,0:T(8,128)S(1)}, u32[]{:S(2)}, u32[]{:S(2)}) collective-permute-start(f32[32,32]{1,0:T(8,128)S(1)} %bitcast.95), channel_id=1, source_target_pairs={{1,0},{2,1},{3,2},{4,3},{5,4},{6,5},{7,6},{9,8},{10,9},{11,10},{12... | collective-permute-start | bytes 12296 | tf_op jit(solution)/shard_map/ppermute | solution.py:208
  26.0 5.1 %all-to-all-done = f32[64,2,128]{2,1,0:T(2,128)S(1)} async-done(((f32[64,2,128]{2,1,0:T(2,128)}), f32[64,2,128]{2,1,0:T(2,128)S(1)}, u32[]{:S(2)}, u32[]{:S(2)}) %all-to-all-start) | async-done | bytes 65568 | tf_op jit(solution)/shard_map/all_to_all | solution.py:262
  31.1 0.9 %shard_map.273 = f32[128,128]{1,0:T(8,128)} custom-call(f32[128,128]{1,0:T(8,128)S(1)} %bitcast.56, f32[48,256]{1,0:T(8,128)S(1)} %bitcast.43, f32[48,256]{1,0:T(8,128)S(1)} %bitcast.50), custom_call_target="tpu_custom_call" | custom-call | tf_op jit(solution)/shard_map/pallas_call | solution.py:171
  32.0 7.4 %all-to-all-start.1 = ((f32[64,2,128]{2,1,0:T(2,128)}), f32[64,2,128]{2,1,0:T(2,128)S(1)}, u32[]{:S(2)}, u32[]{:S(2)}) async-start(f32[64,2,128]{2,1,0:T(2,128)} %bitcast.13), calls=%async_computation.1 | async-start | bytes 131072 | tf_op jit(solution)/shard_map/all_to_all | solution.py:273
  39.5 0.0 copy-start.19
  39.5 0.0 copy-start.20
  39.6 0.6 copy-done.23
  40.3 0.0 copy-start.11
  40.3 0.0 copy-start.12
  40.4 0.5 copy-done.6
  40.9 0.0 copy-done.8
  40.9 0.0 copy-done.11
  40.9 0.0 copy-done.12
  41.0 0.0 copy-done.13
  41.0 0.0 copy-done.15
  41.0 0.0 copy-done.16
  41.0 0.0 copy-done.17
  41.0 0.0 copy-done.18
  41.0 0.0 copy-done.7
  41.1 2.4 %shard_map.275 = (f32[4,48,256]{2,1,0:T(8,128)S(1)}, f32[2,48,256]{2,1,0:T(8,128)S(1)}, f32[10,48,256]{2,1,0:T(8,128)S(1)}, f32[80,32]{1,0:T(8,128)S(1)}, f32[48,32]{1,0:T(8,128)S(1)}) custom-call(f32[48,256]{1,0:T(8,128)S(1)} %bitcast.44, f32[48,256]{1,0:T(8,128)S(1)} %bitcast.51, s32[1,256]{1,0:T(1,128)S(1)} %bitcast.65, s32[1,256]{1,0:T(1,128)S(1)} %bitcast.68, ...), custom_call_target="tpu_custom_call" | custom-call | tf_op jit(solution)/shard_map/pallas_call | solution.py:171
  43.5 1.5 %shard_map.274 = (f32[4,48,256]{2,1,0:T(8,128)S(1)}, f32[10,48,128]{2,1,0:T(8,128)S(1)}, f32[8,256]{1,0:T(8,128)S(1)}, f32[128,128]{1,0:T(8,128)S(1)}) custom-call(f32[128,128]{1,0:T(8,128)S(1)} %bitcast.57, f32[48,256]{1,0:T(8,128)S(1)} %bitcast.45, f32[48,256]{1,0:T(8,128)S(1)} %bitcast.52, s32[1,256]{1,0:T(1,128)S(1)} %bitcast.66, s32[1,256]{1,0:T(1,128)S(1)} %bitcast.69, ...), custom_call_target="tpu_custom_call" | custom-call | tf_op jit(solution)/shard_map/pallas_call | solution.py:171
  45.0 6.0 %all-to-all-done.1 = f32[64,2,128]{2,1,0:T(2,128)S(1)} async-done(((f32[64,2,128]{2,1,0:T(2,128)}), f32[64,2,128]{2,1,0:T(2,128)S(1)}, u32[]{:S(2)}, u32[]{:S(2)}) %all-to-all-start.1) | async-done | bytes 65568 | tf_op jit(solution)/shard_map/all_to_all | solution.py:273
  51.0 2.3 %shard_map.276 = (f32[10,48,64]{2,1,0:T(8,128)S(1)}, f32[4,48,256]{2,1,0:T(8,128)S(1)}, f32[384,128]{1,0:T(8,128)}) custom-call(f32[48,256]{1,0:T(8,128)S(1)} %bitcast.46, f32[48,256]{1,0:T(8,128)S(1)} %bitcast.47, f32[48,256]{1,0:T(8,128)S(1)} %bitcast.53, f32[48,256]{1,0:T(8,128)S(1)} %bitcast.59, f32[48,256]{1,0:T(8,128)S(1)} %bitcast.61, ...), custom_call_target="tpu_custom_call" | custom-call | tf_op jit(solution)/shard_map/pallas_call | solution.py:171
  53.3 6.3 %all-to-all-start.2 = ((f32[192,2,128]{2,1,0:T(2,128)}), f32[192,2,128]{2,1,0:T(2,128)S(1)}, u32[]{:S(2)}, u32[]{:S(2)}) async-start(f32[192,2,128]{2,1,0:T(2,128)} %bitcast.33), calls=%async_computation.2 | async-start | bytes 393216 | tf_op jit(solution)/shard_map/all_to_all | solution.py:468
  59.7 2.9 %shard_map.277 = (f32[4,48,256]{2,1,0:T(8,128)S(1)}, f32[2,48,256]{2,1,0:T(8,128)S(1)}, f32[48,32]{1,0:T(8,128)}, f32[48,32]{1,0:T(8,128)}, f32[192,64]{1,0:T(8,128)S(1)}, /*index=5*/f32[192,128]{1,0:T(8,128)S(1)}) custom-call(f32[4,48,256]{2,1,0:T(8,128)S(1)} %get-tuple-element.35.refs_0_, s32[1,256]{1,0:T(1,128)S(1)} %bitcast.67, s32[1,256]{1,0:T(1,128)S(1)} %bitcast.70, ...), custom_call_target="tpu_custom_call" | custom-call | tf_op jit(solution)/shard_map/pallas_call | solution.py:171
  62.6 9.8 %all-to-all-done.2 = f32[192,2,128]{2,1,0:T(2,128)S(1)} async-done(((f32[192,2,128]{2,1,0:T(2,128)}), f32[192,2,128]{2,1,0:T(2,128)S(1)}, u32[]{:S(2)}, u32[]{:S(2)}) %all-to-all-start.2) | async-done | bytes 196640 | tf_op jit(solution)/shard_map/all_to_all | solution.py:468
  72.4 2.5 %shard_map.278 = (f32[48,256]{1,0:T(8,128)}, f32[48,256]{1,0:T(8,128)}, f32[48,256]{1,0:T(8,128)}) custom-call(f32[4,48,256]{2,1,0:T(8,128)S(1)} %get-tuple-element.35.refs_0_, f32[48,256]{1,0:T(8,128)S(1)} %bitcast.48, f32[48,256]{1,0:T(8,128)S(1)} %bitcast.54, f32[48,256]{1,0:T(8,128)S(1)} %bitcast.60, f32[48,256]{1,0:T(8,128)S(1)} %bitcast.62, ...), custom_call_target="tpu_custom_call" | custom-call | tf_op jit(solution)/shard_map/pallas_call | solution.py:171
  (39 shorter events, 0.1 us)
Async XLA Ops:
  2.7 17.3 %copy-start.4 = (f32[3,16,32]{2,1,0:T(8,128)S(1)}, f32[3,16,32]{2,1,0:T(8,128)}, u32[]{:S(2)}) copy-start(f32[3,16,32]{2,1,0:T(8,128)} %param.29) | copy-start | bytes 18436
  2.7 28.4 %copy-start.1 = (f32[3,16,256]{2,1,0:T(8,128)S(1)}, f32[3,16,256]{2,1,0:T(8,128)}, u32[]{:S(2)}) copy-start(f32[3,16,256]{2,1,0:T(8,128)} %param.26) | copy-start | bytes 147460
  2.8 28.4 %all-to-all-start = ((f32[64,2,128]{2,1,0:T(2,128)}), f32[64,2,128]{2,1,0:T(2,128)S(1)}, u32[]{:S(2)}, u32[]{:S(2)}) async-start(f32[64,2,128]{2,1,0:T(2,128)} %bitcast.94), calls=%async_computation | async-start | bytes 131072 | tf_op jit(solution)/shard_map/all_to_all | solution.py:262
  20.1 11.1 %copy-start = (f32[3,16,256]{2,1,0:T(8,128)S(1)}, f32[3,16,256]{2,1,0:T(8,128)}, u32[]{:S(2)}) copy-start(f32[3,16,256]{2,1,0:T(8,128)} %param.25) | copy-start | bytes 147460
  20.1 20.2 %collective-permute-start = (f32[32,32]{1,0:T(8,128)S(1)}, f32[32,32]{1,0:T(8,128)S(1)}, u32[]{:S(2)}, u32[]{:S(2)}) collective-permute-start(f32[32,32]{1,0:T(8,128)S(1)} %bitcast.96), channel_id=1, source_target_pairs={{0,1},{1,2},{2,3},{3,4},{4,5},{5,6},{6,7},{8,9},{9,10},{10,11},{11... | collective-permute-start | bytes 12296 | tf_op jit(solution)/shard_map/ppermute | solution.py:207
  24.1 16.2 %collective-permute-start.1 = (f32[32,32]{1,0:T(8,128)S(1)}, f32[32,32]{1,0:T(8,128)S(1)}, u32[]{:S(2)}, u32[]{:S(2)}) collective-permute-start(f32[32,32]{1,0:T(8,128)S(1)} %bitcast.95), channel_id=1, source_target_pairs={{1,0},{2,1},{3,2},{4,3},{5,4},{6,5},{7,6},{9,8},{10,9},{11,10},{12... | collective-permute-start | bytes 12296 | tf_op jit(solution)/shard_map/ppermute | solution.py:208
  32.0 7.5 %copy-start.9 = (s32[64]{0:T(128)S(1)}, s32[64]{0:T(128)}, u32[]{:S(2)}) copy-start(s32[64]{0:T(128)} %param.43) | copy-start | bytes 772
  32.0 7.5 %copy-start.22 = (s32[64]{0:T(128)S(1)}, s32[64]{0:T(128)}, u32[]{:S(2)}) copy-start(s32[64]{0:T(128)} %param.49) | copy-start | bytes 772
  32.0 19.0 %all-to-all-start.1 = ((f32[64,2,128]{2,1,0:T(2,128)}), f32[64,2,128]{2,1,0:T(2,128)S(1)}, u32[]{:S(2)}, u32[]{:S(2)}) async-start(f32[64,2,128]{2,1,0:T(2,128)} %bitcast.13), calls=%async_computation.1 | async-start | bytes 131072 | tf_op jit(solution)/shard_map/all_to_all | solution.py:273
  39.5 0.7 copy-start.23
  39.5 0.7 copy-start.19
  39.5 0.7 copy-start.20
  39.5 0.7 copy-start.21
  40.2 0.7 copy-start.6
  40.2 0.7 copy-start.8
  40.3 0.7 copy-start.11
  40.3 0.7 copy-start.12
  40.3 0.7 copy-start.13
  40.3 0.7 copy-start.14
  40.3 0.7 copy-start.15
  40.3 0.7 copy-start.16
  40.3 0.7 copy-start.17
  40.3 0.7 copy-start.18
  40.4 0.7 copy-start.7
  40.4 0.7 copy-start.10
  43.5 7.5 %copy-start.2 = (f32[3,16,256]{2,1,0:T(8,128)S(1)}, f32[3,16,256]{2,1,0:T(8,128)}, u32[]{:S(2)}) copy-start(f32[3,16,256]{2,1,0:T(8,128)} %param.27) | copy-start | bytes 147460
  43.5 7.5 %copy-start.3 = (f32[3,16,256]{2,1,0:T(8,128)S(1)}, f32[3,16,256]{2,1,0:T(8,128)}, u32[]{:S(2)}) copy-start(f32[3,16,256]{2,1,0:T(8,128)} %param.28) | copy-start | bytes 147460
  43.5 7.5 %copy-start.5 = (f32[64,128]{1,0:T(8,128)S(1)}, f32[64,128]{1,0:T(8,128)}, u32[]{:S(2)}) copy-start(f32[64,128]{1,0:T(8,128)} %get-tuple-element.30.refs_7_) | copy-start | bytes 98308
  53.3 19.1 %all-to-all-start.2 = ((f32[192,2,128]{2,1,0:T(2,128)}), f32[192,2,128]{2,1,0:T(2,128)S(1)}, u32[]{:S(2)}, u32[]{:S(2)}) async-start(f32[192,2,128]{2,1,0:T(2,128)} %bitcast.33), calls=%async_computation.2 | async-start | bytes 393216 | tf_op jit(solution)/shard_map/all_to_all | solution.py:468
